TPU v7x, 32 devices: a whole 2x2x4 slice. The times are simulated.
32 devices in a mesh: group: 2 (over y), site: 4 (over z), inner: 4 (over x, core).
Axes of the slice: x: 2, y: 2, z: 4, core: 2. Of those that a mesh axis runs over, the one named last changes fastest.
Arguments:
- activations: bfloat16 [8, 384, 2560], P(('group', 'site'), None, 'inner'), parts along dimension 0, may hold values from -6 to 6
- out_grads: bfloat16 [8, 384, 1024], P(('group', 'site')), parts along dimension 0, may hold values from -6 to 6
- site_weights: bfloat16 [8, 1024, 2560], P(('group', 'site'), None, 'inner'), parts along dimension 0, may hold values from -6 to 6
Outputs:
- merged: float32 [2048, 2560], P(('group', 'site'), 'inner'), parts along dimension 0
There are 2 independent parts, one for each index of `group`. A program takes and returns all parts, laid end to end along the dimension named above; each array names one. Nothing has to cross between parts.
All inputs are finite; a program needn't handle non-finite values.
Results may differ from a plain program's by a relative error of at most 0.0003.
Values sent between devices are 32-bit elements; how exact they have to be, the bound alone decides.
No kernel may reach another device: no remote copies, remote signals or barrier semaphores. Data moves between devices by JAX's collectives and lax.ppermute only.
A program may use at most 64 MiB of HBM per device.

v0:
```python
import jax
import jax.numpy as jnp
from jax import lax
from jax.sharding import PartitionSpec as P

ITERS = 4


damping = 1.0
highest = lax.Precision.HIGHEST


def local_term(columns, inputs, grads):
    count = inputs.shape[0]
    in_float = inputs.astype(jnp.float32)
    grad_float = grads.astype(jnp.float32)
    left_prod = jnp.dot(grad_float, columns, precision=highest)
    partial_value = jnp.dot(left_prod, in_float.T, precision=highest)
    token_pair = lax.psum(partial_value, "inner")
    mixed = (
        jnp.dot(token_pair, in_float, precision=highest) / (count * count)
        + damping * left_prod / count
    )
    return jnp.dot(grad_float.T, mixed, precision=highest)


def combine(term):
    return lax.psum_scatter(term, "site", scatter_dimension=0, tiled=True)


def spread(vector):
    return lax.all_gather(vector, "site", axis=0, tiled=True)


def apply_operator(vector, inputs, grads):
    return combine(local_term(spread(vector), inputs, grads))


def square_sum(residual):
    return lax.psum(jnp.sum(residual * residual), ("site", "inner"))


def per_device(activations, out_grads, site_weights):
    inputs = activations[0]
    grads = out_grads[0]
    rhs = combine(local_term(site_weights[0].astype(jnp.float32), inputs, grads))
    merged = jnp.zeros_like(rhs)
    residual = rhs
    direction = rhs
    norm_now = square_sum(residual)
    for count_step in range(ITERS):
        image = apply_operator(direction, inputs, grads)
        inner_prod = lax.psum(jnp.sum(direction * image), ("site", "inner"))
        alpha = norm_now / inner_prod
        merged = merged + alpha * direction
        residual = residual - alpha * image
        norm_next = square_sum(residual)
        direction = residual + norm_next / norm_now * direction
        norm_now = norm_next
    return merged


def solution(mesh):
    return jax.shard_map(
        per_device,
        mesh=mesh,
        in_specs=(
            P(("group", "site"), None, "inner"),
            P(("group", "site"), None, None),
            P(("group", "site"), None, "inner"),
        ),
        out_specs=P(("group", "site"), "inner"),
        check_vma=False,
    )
```

profile of v0, /device:TPU:0, one launch (start us, length us, event | category | flops | bytes accessed | tf_op | source)
XLA Modules:
  0.0 976.1 jit_solution(10916573341953800317)
XLA Ops:
  12.6 36.3 %all-reduce.7.cloned.1.call-done = f32[384,384]{1,0:T(8,128)} async-done(((f32[384,384]{1,0:T(8,128)}), f32[384,384]{1,0:T(8,128)}) %all-reduce.7.cloned.1.call-update) | async-done | bytes 589840 | tf_op jit(solution)/shard_map/psum | solution.py:19
  55.1 52.2 %reduce-scatter.6.cloned.1.call-done = f32[256,640]{0,1:T(8,128)} async-done(((f32[1024,640]{0,1:T(8,128)}), f32[256,640]{0,1:T(8,128)}) %reduce-scatter.6.cloned.1.call-update) | async-done | bytes 655376 | tf_op jit(solution)/shard_map/reduce_scatter | solution.py:28
  107.4 56.0 %all-gather.5.cloned.1.call-done = f32[1024,640]{0,1:T(8,128)} async-done(((f32[256,640]{0,1:T(8,128)}), f32[1024,640]{0,1:T(8,128)}) %all-gather.5.cloned.1.call-update) | async-done | bytes 2621456 | tf_op jit(solution)/shard_map/all_gather | solution.py:32
  173.6 29.7 %all-reduce.9.cloned.1.call-done = f32[384,384]{1,0:T(8,128)} async-done(((f32[384,384]{1,0:T(8,128)}), f32[384,384]{1,0:T(8,128)}) %all-reduce.9.cloned.1.call-update) | async-done | bytes 589840 | tf_op jit(solution)/shard_map/psum | solution.py:19
  209.6 52.2 %reduce-scatter.8.cloned.1.call-done = f32[256,640]{0,1:T(8,128)} async-done(((f32[1024,640]{0,1:T(8,128)}), f32[256,640]{0,1:T(8,128)}) %reduce-scatter.8.cloned.1.call-update) | async-done | bytes 655376 | tf_op jit(solution)/shard_map/reduce_scatter | solution.py:28
  263.7 32.5 %all-reduce = (f32[]{:T(128)}, f32[]{:T(128)}) all-reduce(f32[]{:T(128)} %get-tuple-element.6, f32[]{:T(128)} %get-tuple-element.5), channel_id=1, replica_groups=mesh['group'=2,'site'=4,'inner'=4] {'site','inner'}, use_global_device_ids=true, to_apply=%region_3.0 | all-reduce | flops 2 | bytes 16 | tf_op jit(solution)/shard_map/psum | solution.py:40
  299.3 30.1 %psum.95 = f32[]{:T(128)} all-reduce(f32[]{:T(128)} %multiply_reduce_fusion.5), channel_id=1, replica_groups=mesh['group'=2,'site'=4,'inner'=4] {'site','inner'}, use_global_device_ids=true, to_apply=%region_9.0 | all-reduce | flops 1 | bytes 8 | tf_op jit(solution)/shard_map/psum | solution.py:40
  332.7 52.1 %all-gather.7.cloned.1.call-done = f32[1024,640]{0,1:T(8,128)} async-done(((f32[256,640]{0,1:T(8,128)}), f32[1024,640]{0,1:T(8,128)}) %all-gather.7.cloned.1.call-update) | async-done | bytes 2621456 | tf_op jit(solution)/shard_map/all_gather | solution.py:32
  384.8 3.9 fusion.14
  394.9 29.9 %all-reduce.11.cloned.1.call-done = f32[384,384]{1,0:T(8,128)} async-done(((f32[384,384]{1,0:T(8,128)}), f32[384,384]{1,0:T(8,128)}) %all-reduce.11.cloned.1.call-update) | async-done | bytes 589840 | tf_op jit(solution)/shard_map/psum | solution.py:19
  431.0 52.2 %reduce-scatter.10.cloned.1.call-done = f32[256,640]{0,1:T(8,128)} async-done(((f32[1024,640]{0,1:T(8,128)}), f32[256,640]{0,1:T(8,128)}) %reduce-scatter.10.cloned.1.call-update) | async-done | bytes 655376 | tf_op jit(solution)/shard_map/reduce_scatter | solution.py:28
  485.3 32.6 %psum.97 = f32[]{:T(128)} all-reduce(f32[]{:T(128)} %multiply_reduce_fusion.4), channel_id=1, replica_groups=mesh['group'=2,'site'=4,'inner'=4] {'site','inner'}, use_global_device_ids=true, to_apply=%region_13.0 | all-reduce | flops 1 | bytes 8 | tf_op jit(solution)/shard_map/psum | solution.py:53
  521.9 30.1 %psum.98 = f32[]{:T(128)} all-reduce(f32[]{:T(128)} %get-tuple-element.9), channel_id=1, replica_groups=mesh['group'=2,'site'=4,'inner'=4] {'site','inner'}, use_global_device_ids=true, to_apply=%region_15.0 | all-reduce | flops 1 | bytes 8 | tf_op jit(solution)/shard_map/psum | solution.py:40
  555.6 52.1 %all-gather.9.cloned.1.call-done = f32[1024,640]{0,1:T(8,128)} async-done(((f32[256,640]{0,1:T(8,128)}), f32[1024,640]{0,1:T(8,128)}) %all-gather.9.cloned.1.call-update) | async-done | bytes 2621456 | tf_op jit(solution)/shard_map/all_gather | solution.py:32
  607.7 3.9 fusion.11
  617.8 29.9 %all-reduce.13.cloned.1.call-done = f32[384,384]{1,0:T(8,128)} async-done(((f32[384,384]{1,0:T(8,128)}), f32[384,384]{1,0:T(8,128)}) %all-reduce.13.cloned.1.call-update) | async-done | bytes 589840 | tf_op jit(solution)/shard_map/psum | solution.py:19
  653.9 52.2 %reduce-scatter.12.cloned.1.call-done = f32[256,640]{0,1:T(8,128)} async-done(((f32[1024,640]{0,1:T(8,128)}), f32[256,640]{0,1:T(8,128)}) %reduce-scatter.12.cloned.1.call-update) | async-done | bytes 655376 | tf_op jit(solution)/shard_map/reduce_scatter | solution.py:28
  708.2 32.5 %psum.100 = f32[]{:T(128)} all-reduce(f32[]{:T(128)} %multiply_reduce_fusion.2), channel_id=1, replica_groups=mesh['group'=2,'site'=4,'inner'=4] {'site','inner'}, use_global_device_ids=true, to_apply=%region_19.0 | all-reduce | flops 1 | bytes 8 | tf_op jit(solution)/shard_map/psum | solution.py:53
  744.1 30.1 %psum.101 = f32[]{:T(128)} all-reduce(f32[]{:T(128)} %multiply_reduce_fusion.1), channel_id=1, replica_groups=mesh['group'=2,'site'=4,'inner'=4] {'site','inner'}, use_global_device_ids=true, to_apply=%region_21.0 | all-reduce | flops 1 | bytes 8 | tf_op jit(solution)/shard_map/psum | solution.py:40
  778.4 51.9 %all-gather.11.cloned.1.call-done = f32[1024,640]{0,1:T(8,128)} async-done(((f32[256,640]{0,1:T(8,128)}), f32[1024,640]{0,1:T(8,128)}) %all-gather.11.cloned.1.call-update) | async-done | bytes 2621456 | tf_op jit(solution)/shard_map/all_gather | solution.py:32
  830.2 3.9 fusion.8
  840.3 29.9 %all-reduce.15.cloned.1.call-done = f32[384,384]{1,0:T(8,128)} async-done(((f32[384,384]{1,0:T(8,128)}), f32[384,384]{1,0:T(8,128)}) %all-reduce.15.cloned.1.call-update) | async-done | bytes 589840 | tf_op jit(solution)/shard_map/psum | solution.py:19
  876.4 52.3 %reduce-scatter.14.cloned.1.call-done = f32[256,640]{0,1:T(8,128)} async-done(((f32[1024,640]{0,1:T(8,128)}), f32[256,640]{0,1:T(8,128)}) %reduce-scatter.14.cloned.1.call-update) | async-done | bytes 655376 | tf_op jit(solution)/shard_map/reduce_scatter | solution.py:28
  930.8 32.6 %psum.103 = f32[]{:T(128)} all-reduce(f32[]{:T(128)} %multiply_reduce_fusion), channel_id=1, replica_groups=mesh['group'=2,'site'=4,'inner'=4] {'site','inner'}, use_global_device_ids=true, to_apply=%region_25.0 | all-reduce | flops 1 | bytes 8 | tf_op jit(solution)/shard_map/psum | solution.py:53
  (81 shorter events, 92.3 us)
Async XLA Ops:
  6.5 1.3 copy-start
  6.5 4.2 copy-start.2
  6.5 42.3 %all-reduce.7.cloned.1.call-start = ((), (), s32[]{:S(2)}) async-start(), calls=%async_computation.5 | async-start | bytes 1179648 | tf_op jit(solution)/shard_map/psum | solution.py:19
  9.8 1.0 copy-start.9
  10.7 40.6 %copy-start.1 = (bf16[1,384,1024]{2,1,0:T(8,128)(2,1)S(1)}, bf16[1,384,1024]{2,1,0:T(8,128)(2,1)}, u32[]{:S(2)}) copy-start(bf16[1,384,1024]{2,1,0:T(8,128)(2,1)} %param.4) | copy-start | bytes 2359300
  12.6 94.7 %reduce-scatter.6.cloned.1.call-start = ((), (), s32[]{:S(2)}) async-start(), calls=%async_computation.6 | async-start | bytes 3276800 | tf_op jit(solution)/shard_map/reduce_scatter | solution.py:28
  55.1 108.3 %all-gather.5.cloned.1.call-start = ((), (), s32[]{:S(2)}) async-start(), calls=%async_computation.7 | async-start | bytes 3276800 | tf_op jit(solution)/shard_map/all_gather | solution.py:32
  107.3 96.0 %all-reduce.9.cloned.1.call-start = ((), (), s32[]{:S(2)}) async-start(), calls=%async_computation.8 | async-start | bytes 1179648 | tf_op jit(solution)/shard_map/psum | solution.py:19
  167.3 1.0 copy-start.5
  170.9 90.9 %reduce-scatter.8.cloned.1.call-start = ((), (), s32[]{:S(2)}) async-start(), calls=%async_computation.9 | async-start | bytes 3276800 | tf_op jit(solution)/shard_map/reduce_scatter | solution.py:28
  205.7 56.0 %copy-start.3 = (f32[256,640]{0,1:T(8,128)S(1)}, f32[256,640]{0,1:T(8,128)}, u32[]{:S(2)}) copy-start(f32[256,640]{0,1:T(8,128)} %reduce-scatter.6.cloned.1.call-done) | copy-start | bytes 1966084
  209.5 175.3 %all-gather.7.cloned.1.call-start = ((), (), s32[]{:S(2)}) async-start(), calls=%async_computation.10 | async-start | bytes 3276800 | tf_op jit(solution)/shard_map/all_gather | solution.py:32
  332.6 92.1 %all-reduce.11.cloned.1.call-start = ((), (), s32[]{:S(2)}) async-start(), calls=%async_computation.11 | async-start | bytes 1179648 | tf_op jit(solution)/shard_map/psum | solution.py:19
  388.7 1.0 copy-start.6
  392.3 90.9 %reduce-scatter.10.cloned.1.call-start = ((), (), s32[]{:S(2)}) async-start(), calls=%async_computation.12 | async-start | bytes 3276800 | tf_op jit(solution)/shard_map/reduce_scatter | solution.py:28
  430.9 176.7 %all-gather.9.cloned.1.call-start = ((), (), s32[]{:S(2)}) async-start(), calls=%async_computation.13 | async-start | bytes 3276800 | tf_op jit(solution)/shard_map/all_gather | solution.py:32
  555.5 92.1 %all-reduce.13.cloned.1.call-start = ((), (), s32[]{:S(2)}) async-start(), calls=%async_computation.14 | async-start | bytes 1179648 | tf_op jit(solution)/shard_map/psum | solution.py:19
  611.6 1.0 copy-start.7
  615.2 90.9 %reduce-scatter.12.cloned.1.call-start = ((), (), s32[]{:S(2)}) async-start(), calls=%async_computation.15 | async-start | bytes 3276800 | tf_op jit(solution)/shard_map/reduce_scatter | solution.py:28
  653.8 176.4 %all-gather.11.cloned.1.call-start = ((), (), s32[]{:S(2)}) async-start(), calls=%async_computation.16 | async-start | bytes 3276800 | tf_op jit(solution)/shard_map/all_gather | solution.py:32
  778.1 92.1 %all-reduce.15.cloned.1.call-start = ((), (), s32[]{:S(2)}) async-start(), calls=%async_computation.17 | async-start | bytes 1179648 | tf_op jit(solution)/shard_map/psum | solution.py:19
  834.2 1.0 copy-start.8
  837.7 90.9 %reduce-scatter.14.cloned.1.call-start = ((), (), s32[]{:S(2)}) async-start(), calls=%async_computation.18 | async-start | bytes 3276800 | tf_op jit(solution)/shard_map/reduce_scatter | solution.py:28
  876.3 88.4 %copy-start.4 = (f32[256,640]{0,1:T(8,128)S(1)}, f32[256,640]{0,1:T(8,128)}, u32[]{:S(2)}) copy-start(f32[256,640]{0,1:T(8,128)} %multiply_add_fusion.3) | copy-start | bytes 1966084
Sparse Core Ops, SparseCore 0:
  12.7 36.1 all-reduce.6
  55.2 52.0 reduce-scatter.5
  108.9 54.4 all-gather.4
  171.0 32.2 all-reduce.8
  209.6 52.0 reduce-scatter.7
  332.8 52.0 all-gather.6
  392.4 32.2 all-reduce.10
  431.1 52.0 reduce-scatter.9
  555.6 51.9 all-gather.8
  615.3 32.2 all-reduce.12
  653.9 52.0 reduce-scatter.11
  778.2 51.9 all-gather.10
  837.9 32.2 all-reduce.14
  876.5 52.0 reduce-scatter.13
where the time goes:
time: 984 us; the launch traced here: 976 us
  waiting for transfers between devices  629 us (64%)
  blocking collectives  221 us (22%)
  matrix products  60.5 us (6%)
  other arithmetic  24.1 us (2%)
  between operations  22.7 us (2%)
  local copies, waits for them, and re-layouts  18.3 us (2%)
    reduce_scatter x5, waiting for transfers between devices, combine(): return lax.psum_scatter(term, 'site', scatter_dimension=0, tiled=True)  261 us
    all_gather x4, waiting for transfers between devices, spread(): return lax.all_gather(vector, 'site', axis=0, tiled=True)  212 us
    psum x5, waiting for transfers between devices, local_term(): token_pair = lax.psum(partial_value, 'inner')  156 us
    psum x4, blocking collectives, square_sum(): return lax.psum(jnp.sum(residual * residual), ('site', 'inner'))  123 us
    psum x3, blocking collectives, per_device(): inner_prod = lax.psum(jnp.sum(direction * image), ('site', 'inner'))  97.7 us
  transfers between devices with their start and end apart: 14, of which 14 were waited for; matrix products, arithmetic and copies ran while one was open for 1% of the time, Pallas kernels for 0%

commit v1 on v0

v1 whole, which is shorter than its diff:
```python
import jax
import jax.numpy as jnp
from jax import lax
from jax.sharding import PartitionSpec as P

ITERS = 4

damping = 1.0
f32 = jnp.float32
bf16 = jnp.bfloat16


def pieces(x):
    hi = lax.reduce_precision(x, exponent_bits=8, mantissa_bits=7)
    rest = x - hi
    mid = lax.reduce_precision(rest, exponent_bits=8, mantissa_bits=7)
    lo = rest - mid
    return hi.astype(bf16), mid.astype(bf16), lo.astype(bf16)


def exact_dot(spec, exact, value, exact_first=True):
    hi, mid, lo = pieces(value)

    def one(part):
        if exact_first:
            return jnp.einsum(spec, exact, part, preferred_element_type=f32)
        return jnp.einsum(spec, part, exact, preferred_element_type=f32)

    return one(hi) + (one(mid) + one(lo))


def site_gather(x):
    return lax.optimization_barrier(lax.all_gather(lax.optimization_barrier(x), "site"))


def inner_sum(x, size):
    if size & (size - 1):
        return lax.psum(x, "inner")
    bit = 1
    while bit < size:
        x = x + lax.ppermute(x, "inner", [(i, i ^ bit) for i in range(size)])
        bit *= 2
    return x


def per_device(activations, out_grads, site_weights):
    sites = lax.axis_size("site")
    inner = lax.axis_size("inner")
    me = lax.axis_index("site")
    inputs = activations[0]
    grads = out_grads[0]
    count = inputs.shape[0]
    rows = grads.shape[1] // sites

    every_input = (site_gather(inputs.astype(f32) * 2.0) * 0.5).astype(bf16)
    every_grad = (site_gather(grads.astype(f32) * 2.0) * 0.5).astype(bf16)

    def mixed_of(left, pair):
        return exact_dot("tu,uc->tc", inputs, pair, exact_first=False) / (count * count) + damping * left / count

    def token_pair(left):
        return inner_sum(exact_dot("tc,uc->tu", inputs, left, exact_first=False), inner)

    def image_of(mixed_all):
        return exact_dot("std,stc->dc", every_grad, mixed_all)

    left_w = jnp.dot(grads, site_weights[0], preferred_element_type=f32)
    mixed_w = mixed_of(left_w, token_pair(left_w))
    rhs = image_of(site_gather(mixed_w))

    def square_sum(x):
        return inner_sum(jnp.sum(x * x), inner)

    def apply_operator(direction):
        left_all = exact_dot("std,dc->stc", every_grad, direction)
        left_own = lax.dynamic_index_in_dim(left_all, me, 0, keepdims=False)
        pair_all = site_gather(token_pair(left_own))
        mixed_all = (
            exact_dot("stu,suc->stc", every_input, pair_all, exact_first=False) / (count * count)
            + damping * left_all / count
        )
        return image_of(mixed_all)

    merged = jnp.zeros_like(rhs)
    residual = rhs
    direction = rhs
    norm_now = square_sum(residual)
    for count_step in range(ITERS):
        image = apply_operator(direction)
        alpha = norm_now / inner_sum(jnp.sum(direction * image), inner)
        merged = merged + alpha * direction
        residual = residual - alpha * image
        norm_next = square_sum(residual)
        direction = residual + norm_next / norm_now * direction
        norm_now = norm_next
    return lax.dynamic_slice_in_dim(merged, me * rows, rows, 0)


def solution(mesh):
    return jax.shard_map(
        per_device,
        mesh=mesh,
        in_specs=(
            P(("group", "site"), None, "inner"),
            P(("group", "site"), None, None),
            P(("group", "site"), None, "inner"),
        ),
        out_specs=P(("group", "site"), "inner"),
        check_vma=False,
    )
```

time: 984 us -> 746 us (0.76)
  blocking collectives: 221 us -> 0 us
  waiting for transfers between devices: 629 us -> 509 us
  matrix products: 60.5 us -> 117 us
  starting transfers between devices: 0.97 us -> 30.9 us
  other arithmetic: 24.1 us -> 38.8 us
    reduce_scatter x5 -> x0, waiting for transfers between devices: 261 us -> none  [combine(): return lax.psum_scatter(term, 'site', scatter_dimension=0, tiled=True)]
    psum x7 -> x0, blocking collectives: 221 us -> none  [the longest x4 123 us: square_sum(): return lax.psum(jnp.sum(residual * residual), ('site', 'inner'))]
    all_gather x4 -> x7, waiting for transfers between devices: 212 us -> 414 us  [site_gather(): lax.all_gather(lax.optimization_barrier(x), 'site')]
    psum x5 -> x0, waiting for transfers between devices: 156 us -> none  [local_term(): token_pair = lax.psum(partial_value, 'inner')]
    ppermute x0 -> x26, waiting for transfers between devices: none -> 95 us  [inner_sum(): x = x + lax.ppermute(x, 'inner', [(i, i ^ bit) for i in range(size)])]
    dot_general x20 -> x58, matrix products: 60.5 us -> 117 us  [the longest x27 81.2 us: one(): return jnp.einsum(spec, exact, part, preferred_element_type=f32)]
    ppermute x0 -> x26, starting transfers between devices: none -> 30.2 us  [inner_sum(): x = x + lax.ppermute(x, 'inner', [(i, i ^ bit) for i in range(size)])]
    dot_general x4 -> x0, local copies, waits for them, and re-layouts: 10.1 us -> none  [local_term(): left_prod = jnp.dot(grad_float, columns, precision=highest)]
  transfers between devices with their start and end apart: 14 -> 33, of which waited for: 14 -> 31; matrix products, arithmetic and copies ran while one was open for 1% -> 5% of each run, Pallas kernels for 0% -> 0%
where the time goes in v1:
time: 746 us; the launch traced here: 741 us
  waiting for transfers between devices  509 us (68%)
  matrix products  117 us (16%)
  other arithmetic  38.8 us (5%)
  starting transfers between devices  30.9 us (4%)
  between operations  29.7 us (4%)
  local copies, waits for them, and re-layouts  15.6 us (2%)
    all_gather x7, waiting for transfers between devices, site_gather(): lax.all_gather(lax.optimization_barrier(x), 'site')  414 us
    ppermute x26, waiting for transfers between devices, inner_sum(): x = x + lax.ppermute(x, 'inner', [(i, i ^ bit) for i in range(size)])  95 us
    dot_general x27, matrix products, one(): return jnp.einsum(spec, exact, part, preferred_element_type=f32)  81.2 us
    dot_general x30, matrix products, one(): return jnp.einsum(spec, part, exact, preferred_element_type=f32)  34 us
    ppermute x26, starting transfers between devices, inner_sum(): x = x + lax.ppermute(x, 'inner', [(i, i ^ bit) for i in range(size)])  30.2 us
  transfers between devices with their start and end apart: 33, of which 31 were waited for; matrix products, arithmetic and copies ran while one was open for 5% of the time, Pallas kernels for 0%

profile of v1, /device:TPU:0, one launch (start us, length us, event | category | flops | bytes accessed | tf_op | source)
XLA Modules:
  0.0 741.3 jit_solution(9180307714067609143)
XLA Ops:
  16.3 13.6 %collective-permute-done.1 = f32[384,384]{1,0:T(8,128)S(1)} collective-permute-done((f32[384,384]{1,0:T(8,128)S(1)}, f32[384,384]{1,0:T(8,128)S(1)}, u32[]{:S(2)}, u32[]{:S(2)}) %collective-permute-start.1) | collective-permute-done | bytes 589856 | tf_op jit(solution)/shard_map/ppermute | solution.py:41
  35.0 75.4 %all-gather.17.cloned.1.call-done = f32[1536,640]{1,0:T(8,128)} async-done(((f32[384,640]{1,0:T(8,128)}), f32[1536,640]{1,0:T(8,128)}) %all-gather.17.cloned.1.call-update) | async-done | bytes 3932176 | tf_op jit(solution)/shard_map/all_gather | solution.py:33
  110.4 115.5 %all-gather.15.cloned.1.call-done = f32[1536,1024]{1,0:T(8,128)} async-done(((f32[384,1024]{1,0:T(8,128)}), f32[1536,1024]{1,0:T(8,128)}) %all-gather.15.cloned.1.call-update) | async-done | bytes 6291472 | tf_op jit(solution)/shard_map/all_gather | solution.py:33
  225.9 6.8 copy.4
  232.8 4.0 multiply_convert_fusion
  250.7 3.2 add_add_fusion.3
  259.5 13.8 %collective-permute-done.5 = f32[384,384]{1,0:T(8,128)S(1)} collective-permute-done((f32[384,384]{1,0:T(8,128)S(1)}, f32[384,384]{1,0:T(8,128)S(1)}, u32[]{:S(2)}, u32[]{:S(2)}) %collective-permute-start.5) | collective-permute-done | bytes 589856 | tf_op jit(solution)/shard_map/ppermute | solution.py:41
  274.2 28.0 %all-gather.21.cloned.1.call-done = f32[1536,640]{1,0:T(8,128)} async-done(((f32[384,640]{1,0:T(8,128)}), f32[1536,640]{1,0:T(8,128)}) %all-gather.21.cloned.1.call-update) | async-done | bytes 3932176 | tf_op jit(solution)/shard_map/all_gather | solution.py:33
  304.6 48.1 %all-gather.19.cloned.1.call-done = f32[1536,384]{1,0:T(8,128)} async-done(((f32[384,384]{1,0:T(8,128)}), f32[1536,384]{1,0:T(8,128)}) %all-gather.19.cloned.1.call-update) | async-done | bytes 2359312 | tf_op jit(solution)/shard_map/all_gather | solution.py:33
  365.1 5.0 multiply_reduce_fusion.5
  381.2 3.8 multiply_reduce_fusion.4
  408.5 14.8 %collective-permute-done.11 = f32[384,384]{1,0:T(8,128)S(1)} collective-permute-done((f32[384,384]{1,0:T(8,128)S(1)}, f32[384,384]{1,0:T(8,128)S(1)}, u32[]{:S(2)}, u32[]{:S(2)}) %collective-permute-start.11) | collective-permute-done | bytes 589856 | tf_op jit(solution)/shard_map/ppermute | solution.py:41
  424.5 48.3 %all-gather.23.cloned.1.call-done = f32[1536,384]{1,0:T(8,128)} async-done(((f32[384,384]{1,0:T(8,128)}), f32[1536,384]{1,0:T(8,128)}) %all-gather.23.cloned.1.call-update) | async-done | bytes 2359312 | tf_op jit(solution)/shard_map/all_gather | solution.py:33
  485.2 4.9 multiply_reduce_fusion.3
  496.8 6.0 multiply_reduce_fusion.2
  513.2 3.1 fusion.66
  527.3 13.9 %collective-permute-done.17 = f32[384,384]{1,0:T(8,128)S(1)} collective-permute-done((f32[384,384]{1,0:T(8,128)S(1)}, f32[384,384]{1,0:T(8,128)S(1)}, u32[]{:S(2)}, u32[]{:S(2)}) %collective-permute-start.17) | collective-permute-done | bytes 589856 | tf_op jit(solution)/shard_map/ppermute | solution.py:41
  542.4 49.2 %all-gather.25.cloned.1.call-done = f32[1536,384]{1,0:T(8,128)} async-done(((f32[384,384]{1,0:T(8,128)}), f32[1536,384]{1,0:T(8,128)}) %all-gather.25.cloned.1.call-update) | async-done | bytes 2359312 | tf_op jit(solution)/shard_map/all_gather | solution.py:33
  604.0 4.9 multiply_reduce_fusion.1
  615.6 3.8 multiply_reduce_fusion
  626.2 3.8 multiply_add_fusion.4
  644.3 13.9 %collective-permute-done.23 = f32[384,384]{1,0:T(8,128)S(1)} collective-permute-done((f32[384,384]{1,0:T(8,128)S(1)}, f32[384,384]{1,0:T(8,128)S(1)}, u32[]{:S(2)}, u32[]{:S(2)}) %collective-permute-start.23) | collective-permute-done | bytes 589856 | tf_op jit(solution)/shard_map/ppermute | solution.py:41
  659.1 49.5 %all-gather.27.cloned.1.call-done = f32[1536,384]{1,0:T(8,128)} async-done(((f32[384,384]{1,0:T(8,128)}), f32[1536,384]{1,0:T(8,128)}) %all-gather.27.cloned.1.call-update) | async-done | bytes 2359312 | tf_op jit(solution)/shard_map/all_gather | solution.py:33
  721.1 3.5 fusion.11
  (194 shorter events, 174.7 us)
Async XLA Ops:
  6.5 103.9 %all-gather.17.cloned.1.call-start = ((), (), s32[]{:S(2)}) async-start(), calls=%async_computation.1 | async-start | bytes 4915200 | tf_op jit(solution)/shard_map/all_gather | solution.py:33
  11.2 2.2 collective-permute-start
  13.4 16.5 %collective-permute-start.1 = (f32[384,384]{1,0:T(8,128)S(1)}, f32[384,384]{1,0:T(8,128)S(1)}, u32[]{:S(2)}, u32[]{:S(2)}) collective-permute-start(f32[384,384]{1,0:T(8,128)S(1)} %add.237), channel_id=1, source_target_pairs={{0,2},{1,3},{2,0},{3,1},{4,6},{5,7},{6,4},{7,5},{8,10},{9,11},{10,... | collective-permute-start | bytes 1769480 | tf_op jit(solution)/shard_map/ppermute | solution.py:41
  32.3 193.6 %all-gather.15.cloned.1.call-start = ((), (), s32[]{:S(2)}) async-start(), calls=%async_computation | async-start | bytes 7864320 | tf_op jit(solution)/shard_map/all_gather | solution.py:33
  33.8 268.4 %all-gather.21.cloned.1.call-start = ((), (), s32[]{:S(2)}) async-start(), calls=%async_computation.3 | async-start | bytes 4915200 | tf_op jit(solution)/shard_map/all_gather | solution.py:33
  35.0 317.8 %all-gather.19.cloned.1.call-start = ((), (), s32[]{:S(2)}) async-start(), calls=%async_computation.2 | async-start | bytes 2949120 | tf_op jit(solution)/shard_map/all_gather | solution.py:33
  255.8 2.0 collective-permute-start.4
  257.8 15.4 %collective-permute-start.5 = (f32[384,384]{1,0:T(8,128)S(1)}, f32[384,384]{1,0:T(8,128)S(1)}, u32[]{:S(2)}, u32[]{:S(2)}) collective-permute-start(f32[384,384]{1,0:T(8,128)S(1)} %add.251), channel_id=1, source_target_pairs={{0,2},{1,3},{2,0},{3,1},{4,6},{5,7},{6,4},{7,5},{8,10},{9,11},{10,... | collective-permute-start | bytes 1769480 | tf_op jit(solution)/shard_map/ppermute | solution.py:41
  274.2 198.6 %all-gather.23.cloned.1.call-start = ((), (), s32[]{:S(2)}) async-start(), calls=%async_computation.4 | async-start | bytes 2949120 | tf_op jit(solution)/shard_map/all_gather | solution.py:33
  370.2 5.3 collective-permute-start.2
  372.7 6.0 collective-permute-start.7
  376.8 3.7 collective-permute-start.3
  387.6 3.7 collective-permute-start.9
  405.8 2.0 collective-permute-start.10
  407.9 15.4 %collective-permute-start.11 = (f32[384,384]{1,0:T(8,128)S(1)}, f32[384,384]{1,0:T(8,128)S(1)}, u32[]{:S(2)}, u32[]{:S(2)}) collective-permute-start(f32[384,384]{1,0:T(8,128)S(1)} %add.267), channel_id=1, source_target_pairs={{0,2},{1,3},{2,0},{3,1},{4,6},{5,7},{6,4},{7,5},{8,10},{9,11},{10,... | collective-permute-start | bytes 1769480 | tf_op jit(solution)/shard_map/ppermute | solution.py:41
  424.2 167.4 %all-gather.25.cloned.1.call-start = ((), (), s32[]{:S(2)}) async-start(), calls=%async_computation.5 | async-start | bytes 2949120 | tf_op jit(solution)/shard_map/all_gather | solution.py:33
  492.5 3.6 collective-permute-start.13
  505.4 3.7 collective-permute-start.15
  525.8 15.4 %collective-permute-start.17 = (f32[384,384]{1,0:T(8,128)S(1)}, f32[384,384]{1,0:T(8,128)S(1)}, u32[]{:S(2)}, u32[]{:S(2)}) collective-permute-start(f32[384,384]{1,0:T(8,128)S(1)} %add.284), channel_id=1, source_target_pairs={{0,2},{1,3},{2,0},{3,1},{4,6},{5,7},{6,4},{7,5},{8,10},{9,11},{10,... | collective-permute-start | bytes 1769480 | tf_op jit(solution)/shard_map/ppermute | solution.py:41
  542.1 166.4 %all-gather.27.cloned.1.call-start = ((), (), s32[]{:S(2)}) async-start(), calls=%async_computation.6 | async-start | bytes 2949120 | tf_op jit(solution)/shard_map/all_gather | solution.py:33
  611.4 3.6 collective-permute-start.19
  621.9 3.6 collective-permute-start.21
  642.8 15.4 %collective-permute-start.23 = (f32[384,384]{1,0:T(8,128)S(1)}, f32[384,384]{1,0:T(8,128)S(1)}, u32[]{:S(2)}, u32[]{:S(2)}) collective-permute-start(f32[384,384]{1,0:T(8,128)S(1)} %add.301), channel_id=1, source_target_pairs={{0,2},{1,3},{2,0},{3,1},{4,6},{5,7},{6,4},{7,5},{8,10},{9,11},{10,... | collective-permute-start | bytes 1769480 | tf_op jit(solution)/shard_map/ppermute | solution.py:41
  727.2 3.7 collective-permute-start.25
  (42 other events, 130.5 us)
Sparse Core Ops, SparseCore 0:
  32.4 77.9 all-gather.16
  112.0 113.9 all-gather.14
  227.5 74.6 all-gather.20
  303.6 49.0 all-gather.18
  424.3 48.3 all-gather.22
  542.3 49.2 all-gather.24
  659.2 49.2 all-gather.26

commit v2 on v1

--- a/solution.py
+++ b/solution.py
@@ -43,6 +43,27 @@
     return x
 
 
+def halves(x, full, finish=lambda v: v):
+    core = lax.axis_index("inner") % 2
+    half = x.shape[1]
+    other = lax.ppermute(x, "inner", [(i, i ^ 1) for i in range(lax.axis_size("inner"))])
+    full = lax.dynamic_update_slice_in_dim(full, finish(x), core * half, 1)
+    return lax.dynamic_update_slice_in_dim(full, finish(other), (1 - core) * half, 1)
+
+
+def half_sum(x, size):
+    core = lax.axis_index("inner") % 2
+    half = x.shape[0] // 2
+    mine = lax.dynamic_slice_in_dim(x, core * half, half, 0)
+    theirs = lax.dynamic_slice_in_dim(x, (1 - core) * half, half, 0)
+    part = mine + lax.ppermute(theirs, "inner", [(i, i ^ 1) for i in range(size)])
+    bit = 2
+    while bit < size:
+        part = part + lax.ppermute(part, "inner", [(i, i ^ bit) for i in range(size)])
+        bit *= 2
+    return part
+
+
 def per_device(activations, out_grads, site_weights):
     sites = lax.axis_size("site")
     inner = lax.axis_size("inner")
@@ -53,7 +74,14 @@
     rows = grads.shape[1] // sites
 
     every_input = (site_gather(inputs.astype(f32) * 2.0) * 0.5).astype(bf16)
-    every_grad = (site_gather(grads.astype(f32) * 2.0) * 0.5).astype(bf16)
+    core = lax.axis_index("inner") % 2
+    split = inner % 2 == 0 and count % 16 == 0
+    if split:
+        own_rows = lax.dynamic_slice_in_dim(grads, core * (count // 2), count // 2, 0)
+        wide = site_gather(own_rows.astype(f32) * 2.0)
+        every_grad = halves(wide, jnp.zeros((sites,) + grads.shape, bf16), lambda v: (v * 0.5).astype(bf16))
+    else:
+        every_grad = (site_gather(grads.astype(f32) * 2.0) * 0.5).astype(bf16)
 
     def mixed_of(left, pair):
         return exact_dot("tu,uc->tc", inputs, pair, exact_first=False) / (count * count) + damping * left / count
@@ -71,10 +99,16 @@
     def square_sum(x):
         return inner_sum(jnp.sum(x * x), inner)
 
+    def pair_gather(left):
+        partial = exact_dot("tc,uc->tu", inputs, left, exact_first=False)
+        if not split:
+            return site_gather(inner_sum(partial, inner))
+        return halves(site_gather(half_sum(partial, inner)), jnp.zeros((sites, count, count), f32))
+
     def apply_operator(direction):
+        left_own = exact_dot("td,dc->tc", grads, direction)
+        pair_all = pair_gather(left_own)
         left_all = exact_dot("std,dc->stc", every_grad, direction)
-        left_own = lax.dynamic_index_in_dim(left_all, me, 0, keepdims=False)
-        pair_all = site_gather(token_pair(left_own))
         mixed_all = (
             exact_dot("stu,suc->stc", every_input, pair_all, exact_first=False) / (count * count)
             + damping * left_all / count

time: 746 us -> 633 us (0.85)
  waiting for transfers between devices: 509 us -> 295 us
  matrix products: 117 us -> 171 us
  local copies, waits for them, and re-layouts: 15.6 us -> 55.2 us
    all_gather x7, waiting for transfers between devices: 414 us -> 228 us  [site_gather(): lax.all_gather(lax.optimization_barrier(x), 'site')]
    ppermute x26 -> x18, waiting for transfers between devices: 95 us -> 29.3 us  [inner_sum(): x = x + lax.ppermute(x, 'inner', [(i, i ^ bit) for i in range(size)])]
    dot_general x27 -> x39, matrix products: 81.2 us -> 144 us  [one(): return jnp.einsum(spec, exact, part, preferred_element_type=f32)]
    dynamic_update_slice x0 -> x10, local copies, waits for them, and re-layouts: none -> 43 us  [the longest x5 22.8 us: halves(): lax.dynamic_update_slice_in_dim(full, finish(other), (1 - core) * half, 1)]
    ppermute x0 -> x13, waiting for transfers between devices: none -> 37.5 us  [the longest x4 31.2 us: half_sum(): lax.ppermute(part, 'inner', [(i, i ^ bit) for i in range(size)])]
    dot_general x30, matrix products: 34 us -> 25.4 us  [one(): return jnp.einsum(spec, part, exact, preferred_element_type=f32)]
    ppermute x26 -> x18, starting transfers between devices: 30.2 us -> 27.5 us  [inner_sum(): x = x + lax.ppermute(x, 'inner', [(i, i ^ bit) for i in range(size)])]
  transfers between devices with their start and end apart: 33 -> 38, of which waited for: 31 -> 31; matrix products, arithmetic and copies ran while one was open for 5% -> 20% of each run, Pallas kernels for 0% -> 0%
where the time goes in v2:
time: 633 us; the launch traced here: 626 us
  waiting for transfers between devices  295 us (47%)
  matrix products  171 us (27%)
  local copies, waits for them, and re-layouts  55.2 us (9%)
  other arithmetic  39.1 us (6%)
  starting transfers between devices  34.3 us (5%)
  between operations  30.9 us (5%)
    all_gather x7, waiting for transfers between devices, site_gather(): lax.all_gather(lax.optimization_barrier(x), 'site')  228 us
    dot_general x39, matrix products, one(): return jnp.einsum(spec, exact, part, preferred_element_type=f32)  144 us
    ppermute x4, waiting for transfers between devices, half_sum(): lax.ppermute(part, 'inner', [(i, i ^ bit) for i in range(size)])  31.2 us
    ppermute x18, waiting for transfers between devices, inner_sum(): x = x + lax.ppermute(x, 'inner', [(i, i ^ bit) for i in range(size)])  29.3 us
    ppermute x18, starting transfers between devices, inner_sum(): x = x + lax.ppermute(x, 'inner', [(i, i ^ bit) for i in range(size)])  27.5 us
    dot_general x30, matrix products, one(): return jnp.einsum(spec, part, exact, preferred_element_type=f32)  25.4 us
    dynamic_update_slice x5, local copies, waits for them, and re-layouts, halves(): lax.dynamic_update_slice_in_dim(full, finish(other), (1 - core) * half, 1)  22.8 us
    dynamic_update_slice x5, local copies, waits for them, and re-layouts, halves(): full = lax.dynamic_update_slice_in_dim(full, finish(x), core * half, 1)  20.2 us
  transfers between devices with their start and end apart: 38, of which 31 were waited for; matrix products, arithmetic and copies ran while one was open for 20% of the time, Pallas kernels for 0%

profile of v2, /device:TPU:0, one launch (start us, length us, event | category | flops | bytes accessed | tf_op | source)
XLA Modules:
  0.0 625.6 jit_solution(5695755390333516180)
XLA Ops:
  17.2 13.6 %collective-permute-done.2 = f32[384,384]{1,0:T(8,128)S(1)} collective-permute-done((f32[384,384]{1,0:T(8,128)S(1)}, f32[384,384]{1,0:T(8,128)S(1)}, u32[]{:S(2)}, u32[]{:S(2)}) %collective-permute-start.2) | collective-permute-done | bytes 589856 | tf_op jit(solution)/shard_map/ppermute | solution.py:41
  33.2 42.0 %all-gather.15.cloned.1.call-done = f32[768,1024]{1,0:T(8,128)} async-done(((f32[192,1024]{1,0:T(8,128)}), f32[768,1024]{1,0:T(8,128)}) %all-gather.15.cloned.1.call-update) | async-done | bytes 3145744 | tf_op jit(solution)/shard_map/all_gather | solution.py:33
  83.0 19.9 %dynamic_update_slice.30 = bf16[4,384,1024]{1,2,0:T(8,128)(2,1)} dynamic-update-slice(bf16[4,384,1024]{1,2,0:T(8,128)(2,1)} %broadcast_in_dim.3, bf16[4,192,1024]{1,2,0:T(8,128)(2,1)} %copy.18, s32[]{:T(128)} %constant.62.clone.1, s32[]{:T(128)S(6)} %select_n.52, s32[]{:T(128)} %constant.62.clone.1) | dynamic-update-slice | bytes 3145732 | tf_op jit(solution)/shard_map/dynamic_update_slice | solution.py:50
  102.9 48.9 %all-gather.17.cloned.1.call-done = f32[1536,640]{1,0:T(8,128)} async-done(((f32[384,640]{1,0:T(8,128)}), f32[1536,640]{1,0:T(8,128)}) %all-gather.17.cloned.1.call-update) | async-done | bytes 3932176 | tf_op jit(solution)/shard_map/all_gather | solution.py:33
  156.7 22.5 %dynamic_update_slice.31 = bf16[4,384,1024]{1,2,0:T(8,128)(2,1)} dynamic-update-slice(bf16[4,384,1024]{1,2,0:T(8,128)(2,1)} %dynamic_update_slice.30, bf16[4,192,1024]{1,2,0:T(8,128)(2,1)} %copy.19, s32[]{:T(128)} %constant.62.clone.1, s32[]{:T(128)S(6)} %select_n.53, s32[]{:T(128)} %constant.62.clone.1) | dynamic-update-slice | bytes 3145732 | tf_op jit(solution)/shard_map/dynamic_update_slice | solution.py:51
  179.2 5.8 fusion.30
  197.9 7.5 %collective-permute-done.6 = f32[192,384]{1,0:T(8,128)S(1)} collective-permute-done((f32[192,384]{1,0:T(8,128)S(1)}, f32[192,384]{1,0:T(8,128)S(1)}, u32[]{:S(2)}, u32[]{:S(2)}) %collective-permute-start.6) | collective-permute-done | bytes 294944 | tf_op jit(solution)/shard_map/ppermute | solution.py:62
  206.8 21.7 %all-gather.21.cloned.1.call-done = f32[1536,640]{1,0:T(8,128)} async-done(((f32[384,640]{1,0:T(8,128)}), f32[1536,640]{1,0:T(8,128)}) %all-gather.21.cloned.1.call-update) | async-done | bytes 3932176 | tf_op jit(solution)/shard_map/all_gather | solution.py:33
  230.9 28.0 %all-gather.19.cloned.1.call-done = f32[768,384]{1,0:T(8,128)} async-done(((f32[192,384]{1,0:T(8,128)}), f32[768,384]{1,0:T(8,128)}) %all-gather.19.cloned.1.call-update) | async-done | bytes 1179664 | tf_op jit(solution)/shard_map/all_gather | solution.py:33
  259.0 7.4 %fusion.75 = f32[4,384,640]{2,1,0:T(8,128)} fusion(bf16[4,384,1024]{1,2,0:T(8,128)(2,1)} %dynamic_update_slice.31, f32[1024,640]{1,0:T(8,128)} %copy-done.8), kind=kOutput, calls=%fused_computation.165 | convolution fusion | flops 2015887360 | bytes 9699328 | tf_op jit(solution)/shard_map/std,dc->stc/dot_general | solution.py:26
  276.3 7.0 %multiply_add_fusion.3 = f32[4,384,640]{2,1,0:T(8,128)} fusion(f32[4,384,640]{2,1,0:T(8,128)} %fusion.75, f32[4,384,640]{2,1,0:T(8,128)} %fusion.73, f32[4,384,640]{2,1,0:T(8,128)S(1)} %fusion.90, f32[4,384,640]{2,1,0:T(8,128)S(1)} %fusion.91, f32[4,384,640]{2,1,0:T(8,128)S(1)} %fusion.88, bf16[4,384,1024]{1,2,0:T(8,128)(2,1)S(1)} %copy-done.4, ...), kind=kOutput, calls=%fused_computation.28 | convolution fusion | flops 2021457920 | bytes 29360128 | tf_op jit(solution)/shard_map/std,dc->stc/dot_general | solution.py:26
  327.9 8.5 %collective-permute-done.13 = f32[192,384]{1,0:T(8,128)S(1)} collective-permute-done((f32[192,384]{1,0:T(8,128)S(1)}, f32[192,384]{1,0:T(8,128)S(1)}, u32[]{:S(2)}, u32[]{:S(2)}) %collective-permute-start.13) | collective-permute-done | bytes 294944 | tf_op jit(solution)/shard_map/ppermute | solution.py:62
  337.4 28.4 %all-gather.23.cloned.1.call-done = f32[768,384]{1,0:T(8,128)} async-done(((f32[192,384]{1,0:T(8,128)}), f32[768,384]{1,0:T(8,128)}) %all-gather.23.cloned.1.call-update) | async-done | bytes 1179664 | tf_op jit(solution)/shard_map/all_gather | solution.py:33
  365.8 7.4 %fusion.70 = f32[4,384,640]{2,1,0:T(8,128)} fusion(bf16[4,384,1024]{1,2,0:T(8,128)(2,1)} %dynamic_update_slice.31, f32[1024,640]{1,0:T(8,128)} %copy-done.10), kind=kOutput, calls=%fused_computation.160 | convolution fusion | flops 2015887360 | bytes 9699328 | tf_op jit(solution)/shard_map/std,dc->stc/dot_general | solution.py:26
  383.2 7.2 %multiply_add_fusion.2 = f32[4,384,640]{2,1,0:T(8,128)} fusion(f32[4,384,640]{2,1,0:T(8,128)} %fusion.70, f32[4,384,640]{2,1,0:T(8,128)} %fusion.68, f32[4,384,640]{2,1,0:T(8,128)S(1)} %fusion.92, f32[4,384,640]{2,1,0:T(8,128)S(1)} %fusion.93, f32[4,384,640]{2,1,0:T(8,128)S(1)} %fusion.86, bf16[4,384,1024]{1,2,0:T(8,128)(2,1)S(1)} %copy-done.5, ...), kind=kOutput, calls=%fused_computation.27 | convolution fusion | flops 2021457920 | bytes 29360128 | tf_op jit(solution)/shard_map/std,dc->stc/dot_general | solution.py:26
  410.2 6.1 multiply_reduce_fusion.2
  433.6 7.6 %collective-permute-done.20 = f32[192,384]{1,0:T(8,128)S(1)} collective-permute-done((f32[192,384]{1,0:T(8,128)S(1)}, f32[192,384]{1,0:T(8,128)S(1)}, u32[]{:S(2)}, u32[]{:S(2)}) %collective-permute-start.20) | collective-permute-done | bytes 294944 | tf_op jit(solution)/shard_map/ppermute | solution.py:62
  442.2 29.4 %all-gather.25.cloned.1.call-done = f32[768,384]{1,0:T(8,128)} async-done(((f32[192,384]{1,0:T(8,128)}), f32[768,384]{1,0:T(8,128)}) %all-gather.25.cloned.1.call-update) | async-done | bytes 1179664 | tf_op jit(solution)/shard_map/all_gather | solution.py:33
  471.5 7.4 %fusion.65 = f32[4,384,640]{2,1,0:T(8,128)} fusion(bf16[4,384,1024]{1,2,0:T(8,128)(2,1)} %dynamic_update_slice.31, f32[1024,640]{1,0:T(8,128)} %copy-done.12), kind=kOutput, calls=%fused_computation.155 | convolution fusion | flops 2015887360 | bytes 9699328 | tf_op jit(solution)/shard_map/std,dc->stc/dot_general | solution.py:26
  488.9 7.1 %multiply_add_fusion.1 = f32[4,384,640]{2,1,0:T(8,128)} fusion(f32[4,384,640]{2,1,0:T(8,128)} %fusion.65, f32[4,384,640]{2,1,0:T(8,128)} %fusion.63, f32[4,384,640]{2,1,0:T(8,128)S(1)} %fusion.94, f32[4,384,640]{2,1,0:T(8,128)S(1)} %fusion.95, f32[4,384,640]{2,1,0:T(8,128)S(1)} %fusion.84, bf16[4,384,1024]{1,2,0:T(8,128)(2,1)S(1)} %copy-done.6, ...), kind=kOutput, calls=%fused_computation.26 | convolution fusion | flops 2021457920 | bytes 29360128 | tf_op jit(solution)/shard_map/std,dc->stc/dot_general | solution.py:26
  537.8 7.6 %collective-permute-done.27 = f32[192,384]{1,0:T(8,128)S(1)} collective-permute-done((f32[192,384]{1,0:T(8,128)S(1)}, f32[192,384]{1,0:T(8,128)S(1)}, u32[]{:S(2)}, u32[]{:S(2)}) %collective-permute-start.27) | collective-permute-done | bytes 294944 | tf_op jit(solution)/shard_map/ppermute | solution.py:62
  546.1 29.6 %all-gather.27.cloned.1.call-done = f32[768,384]{1,0:T(8,128)} async-done(((f32[192,384]{1,0:T(8,128)}), f32[768,384]{1,0:T(8,128)}) %all-gather.27.cloned.1.call-update) | async-done | bytes 1179664 | tf_op jit(solution)/shard_map/all_gather | solution.py:33
  575.7 5.9 fusion.60
  602.5 5.8 fusion.11
  (223 shorter events, 212.4 us)
Async XLA Ops:
  6.5 68.6 %all-gather.15.cloned.1.call-start = ((), (), s32[]{:S(2)}) async-start(), calls=%async_computation | async-start | bytes 3932160 | tf_op jit(solution)/shard_map/all_gather | solution.py:33
  8.7 143.2 %all-gather.17.cloned.1.call-start = ((), (), s32[]{:S(2)}) async-start(), calls=%async_computation.1 | async-start | bytes 4915200 | tf_op jit(solution)/shard_map/all_gather | solution.py:33
  14.3 16.6 %collective-permute-start.2 = (f32[384,384]{1,0:T(8,128)S(1)}, f32[384,384]{1,0:T(8,128)S(1)}, u32[]{:S(2)}, u32[]{:S(2)}) collective-permute-start(f32[384,384]{1,0:T(8,128)S(1)} %add.309), channel_id=1, source_target_pairs={{0,2},{1,3},{2,0},{3,1},{4,6},{5,7},{6,4},{7,5},{8,10},{9,11},{10,... | collective-permute-start | bytes 1769480 | tf_op jit(solution)/shard_map/ppermute | solution.py:41
  33.1 195.3 %all-gather.21.cloned.1.call-start = ((), (), s32[]{:S(2)}) async-start(), calls=%async_computation.3 | async-start | bytes 4915200 | tf_op jit(solution)/shard_map/all_gather | solution.py:33
  75.2 76.7 %collective-permute-start = (f32[4,192,1024]{2,1,0:T(8,128)}, f32[4,192,1024]{2,1,0:T(8,128)}, u32[]{:S(2)}, u32[]{:S(2)}) collective-permute-start(f32[4,192,1024]{2,1,0:T(8,128)} %bitcast.205), channel_id=1, source_target_pairs={{0,1},{1,0},{2,3},{3,2},{4,5},{5,4},{6,7},{7,6},{8,9},{9,8},{10,11... | collective-permute-start | bytes 9437192 | tf_op jit(solution)/shard_map/ppermute | solution.py:49
  76.2 182.7 %all-gather.19.cloned.1.call-start = ((), (), s32[]{:S(2)}) async-start(), calls=%async_computation.2 | async-start | bytes 1474560 | tf_op jit(solution)/shard_map/all_gather | solution.py:33
  196.3 9.1 %collective-permute-start.6 = (f32[192,384]{1,0:T(8,128)S(1)}, f32[192,384]{1,0:T(8,128)S(1)}, u32[]{:S(2)}, u32[]{:S(2)}) collective-permute-start(f32[192,384]{1,0:T(8,128)S(1)} %dynamic-slice_add_fusion.3), channel_id=1, source_target_pairs={{0,2},{1,3},{2,0},{3,1},{4,6},{5,7},{6,4},{7,5},{8,10},{9,11},{10,... | collective-permute-start | bytes 884744 | tf_op jit(solution)/shard_map/ppermute | solution.py:62
  206.2 159.6 %all-gather.23.cloned.1.call-start = ((), (), s32[]{:S(2)}) async-start(), calls=%async_computation.4 | async-start | bytes 1474560 | tf_op jit(solution)/shard_map/all_gather | solution.py:33
  258.9 13.4 %collective-permute-start.7 = (f32[4,192,384]{2,1,0:T(8,128)}, f32[4,192,384]{2,1,0:T(8,128)S(1)}, u32[]{:S(2)}, u32[]{:S(2)}) collective-permute-start(f32[4,192,384]{2,1,0:T(8,128)} %bitcast.209), channel_id=1, source_target_pairs={{0,1},{1,0},{2,3},{3,2},{4,5},{5,4},{6,7},{7,6},{8,9},{9,8},{10,11... | collective-permute-start | bytes 3538952 | tf_op jit(solution)/shard_map/ppermute | solution.py:49
  296.8 5.1 collective-permute-start.3
  299.1 6.1 collective-permute-start.9
  303.3 3.6 collective-permute-start.4
  314.0 3.6 collective-permute-start.11
  327.2 9.1 %collective-permute-start.13 = (f32[192,384]{1,0:T(8,128)S(1)}, f32[192,384]{1,0:T(8,128)S(1)}, u32[]{:S(2)}, u32[]{:S(2)}) collective-permute-start(f32[192,384]{1,0:T(8,128)S(1)} %dynamic-slice_add_fusion.2), channel_id=1, source_target_pairs={{0,2},{1,3},{2,0},{3,1},{4,6},{5,7},{6,4},{7,5},{8,10},{9,11},{10,... | collective-permute-start | bytes 884744 | tf_op jit(solution)/shard_map/ppermute | solution.py:62
  337.1 134.4 %all-gather.25.cloned.1.call-start = ((), (), s32[]{:S(2)}) async-start(), calls=%async_computation.5 | async-start | bytes 1474560 | tf_op jit(solution)/shard_map/all_gather | solution.py:33
  365.8 13.4 %collective-permute-start.14 = (f32[4,192,384]{2,1,0:T(8,128)}, f32[4,192,384]{2,1,0:T(8,128)S(1)}, u32[]{:S(2)}, u32[]{:S(2)}) collective-permute-start(f32[4,192,384]{2,1,0:T(8,128)} %bitcast.211), channel_id=1, source_target_pairs={{0,1},{1,0},{2,3},{3,2},{4,5},{5,4},{6,7},{7,6},{8,9},{9,8},{10,11... | collective-permute-start | bytes 3538952 | tf_op jit(solution)/shard_map/ppermute | solution.py:49
  405.9 3.6 collective-permute-start.16
  418.9 3.6 collective-permute-start.18
  432.1 9.1 %collective-permute-start.20 = (f32[192,384]{1,0:T(8,128)S(1)}, f32[192,384]{1,0:T(8,128)S(1)}, u32[]{:S(2)}, u32[]{:S(2)}) collective-permute-start(f32[192,384]{1,0:T(8,128)S(1)} %dynamic-slice_add_fusion.1), channel_id=1, source_target_pairs={{0,2},{1,3},{2,0},{3,1},{4,6},{5,7},{6,4},{7,5},{8,10},{9,11},{10,... | collective-permute-start | bytes 884744 | tf_op jit(solution)/shard_map/ppermute | solution.py:62
  441.9 133.8 %all-gather.27.cloned.1.call-start = ((), (), s32[]{:S(2)}) async-start(), calls=%async_computation.6 | async-start | bytes 1474560 | tf_op jit(solution)/shard_map/all_gather | solution.py:33
  471.5 13.4 %collective-permute-start.21 = (f32[4,192,384]{2,1,0:T(8,128)}, f32[4,192,384]{2,1,0:T(8,128)S(1)}, u32[]{:S(2)}, u32[]{:S(2)}) collective-permute-start(f32[4,192,384]{2,1,0:T(8,128)} %bitcast.213), channel_id=1, source_target_pairs={{0,1},{1,0},{2,3},{3,2},{4,5},{5,4},{6,7},{7,6},{8,9},{9,8},{10,11... | collective-permute-start | bytes 3538952 | tf_op jit(solution)/shard_map/ppermute | solution.py:49
  536.3 9.1 %collective-permute-start.27 = (f32[192,384]{1,0:T(8,128)S(1)}, f32[192,384]{1,0:T(8,128)S(1)}, u32[]{:S(2)}, u32[]{:S(2)}) collective-permute-start(f32[192,384]{1,0:T(8,128)S(1)} %dynamic-slice_add_fusion), channel_id=1, source_target_pairs={{0,2},{1,3},{2,0},{3,1},{4,6},{5,7},{6,4},{7,5},{8,10},{9,11},{10,... | collective-permute-start | bytes 884744 | tf_op jit(solution)/shard_map/ppermute | solution.py:62
  575.7 11.9 %collective-permute-start.28 = (f32[4,192,384]{2,1,0:T(8,128)}, f32[4,192,384]{2,1,0:T(8,128)S(1)}, u32[]{:S(2)}, u32[]{:S(2)}) collective-permute-start(f32[4,192,384]{2,1,0:T(8,128)} %bitcast.207), channel_id=1, source_target_pairs={{0,1},{1,0},{2,3},{3,2},{4,5},{5,4},{6,7},{7,6},{8,9},{9,8},{10,11... | collective-permute-start | bytes 3538952 | tf_op jit(solution)/shard_map/ppermute | solution.py:49
  611.5 3.7 collective-permute-start.30
  (40 other events, 154.2 us)
Sparse Core Ops, SparseCore 0:
  8.9 66.1 all-gather.14
  76.7 75.0 all-gather.16
  153.4 74.9 all-gather.20
  229.9 28.9 all-gather.18
  337.2 28.5 all-gather.22
  442.1 29.4 all-gather.24
  546.3 29.4 all-gather.26

commit v3 on v2

--- a/solution.py
+++ b/solution.py
@@ -109,6 +109,7 @@
         left_own = exact_dot("td,dc->tc", grads, direction)
         pair_all = pair_gather(left_own)
         left_all = exact_dot("std,dc->stc", every_grad, direction)
+        pair_all, left_all = lax.optimization_barrier((pair_all, left_all))
         mixed_all = (
             exact_dot("stu,suc->stc", every_input, pair_all, exact_first=False) / (count * count)
             + damping * left_all / count

time: 633 us -> 634 us (level)
  waiting for transfers between devices: 295 us -> 267 us
  other arithmetic: 39.1 us -> 62 us
    all_gather x7, waiting for transfers between devices: 228 us -> 200 us  [site_gather(): lax.all_gather(lax.optimization_barrier(x), 'site')]
    add x0 -> x4, other arithmetic: none -> 22.8 us  [apply_operator(): exact_dot('stu,suc->stc', every_input, pair_all, exact_first=False)]
  transfers between devices with their start and end apart: 38 -> 38, of which waited for: 31 -> 31; matrix products, arithmetic and copies ran while one was open for 20% -> 24% of each run, Pallas kernels for 0% -> 0%
where the time goes in v3:
time: 634 us; the launch traced here: 627 us
  waiting for transfers between devices  267 us (42%)
  matrix products  177 us (28%)
  other arithmetic  62 us (10%)
  local copies, waits for them, and re-layouts  56.5 us (9%)
  starting transfers between devices  34.5 us (5%)
  between operations  30 us (5%)
    all_gather x7, waiting for transfers between devices, site_gather(): lax.all_gather(lax.optimization_barrier(x), 'site')  200 us
    dot_general x39, matrix products, one(): return jnp.einsum(spec, exact, part, preferred_element_type=f32)  143 us
    dot_general x30, matrix products, one(): return jnp.einsum(spec, part, exact, preferred_element_type=f32)  31.7 us
    ppermute x4, waiting for transfers between devices, half_sum(): lax.ppermute(part, 'inner', [(i, i ^ bit) for i in range(size)])  31.2 us
    ppermute x18, waiting for transfers between devices, inner_sum(): x = x + lax.ppermute(x, 'inner', [(i, i ^ bit) for i in range(size)])  30.2 us
    ppermute x18, starting transfers between devices, inner_sum(): x = x + lax.ppermute(x, 'inner', [(i, i ^ bit) for i in range(size)])  28 us
    add x4, other arithmetic, apply_operator(): exact_dot('stu,suc->stc', every_input, pair_all, exact_first=False)  22.8 us
    dynamic_update_slice x5, local copies, waits for them, and re-layouts, halves(): lax.dynamic_update_slice_in_dim(full, finish(other), (1 - core) * half, 1)  22.8 us
  transfers between devices with their start and end apart: 38, of which 31 were waited for; matrix products, arithmetic and copies ran while one was open for 24% of the time, Pallas kernels for 0%

profile of v3, /device:TPU:0, one launch (start us, length us, event | category | flops | bytes accessed | tf_op | source)
XLA Modules:
  0.0 627.1 jit_solution(4606591214399362279)
XLA Ops:
  17.2 13.6 %collective-permute-done.2 = f32[384,384]{1,0:T(8,128)S(1)} collective-permute-done((f32[384,384]{1,0:T(8,128)S(1)}, f32[384,384]{1,0:T(8,128)S(1)}, u32[]{:S(2)}, u32[]{:S(2)}) %collective-permute-start.2) | collective-permute-done | bytes 589856 | tf_op jit(solution)/shard_map/ppermute | solution.py:41
  33.2 42.0 %all-gather.15.cloned.1.call-done = f32[768,1024]{1,0:T(8,128)} async-done(((f32[192,1024]{1,0:T(8,128)}), f32[768,1024]{1,0:T(8,128)}) %all-gather.15.cloned.1.call-update) | async-done | bytes 3145744 | tf_op jit(solution)/shard_map/all_gather | solution.py:33
  83.0 19.9 %dynamic_update_slice.30 = bf16[4,384,1024]{1,2,0:T(8,128)(2,1)} dynamic-update-slice(bf16[4,384,1024]{1,2,0:T(8,128)(2,1)} %broadcast_in_dim.3, bf16[4,192,1024]{1,2,0:T(8,128)(2,1)} %copy.18, s32[]{:T(128)} %constant.62.clone.1, s32[]{:T(128)S(6)} %select_n.52, s32[]{:T(128)} %constant.62.clone.1) | dynamic-update-slice | bytes 3145732 | tf_op jit(solution)/shard_map/dynamic_update_slice | solution.py:50
  102.9 48.9 %all-gather.17.cloned.1.call-done = f32[1536,640]{1,0:T(8,128)} async-done(((f32[384,640]{1,0:T(8,128)}), f32[1536,640]{1,0:T(8,128)}) %all-gather.17.cloned.1.call-update) | async-done | bytes 3932176 | tf_op jit(solution)/shard_map/all_gather | solution.py:33
  156.7 22.4 %dynamic_update_slice.31 = bf16[4,384,1024]{1,2,0:T(8,128)(2,1)} dynamic-update-slice(bf16[4,384,1024]{1,2,0:T(8,128)(2,1)} %dynamic_update_slice.30, bf16[4,192,1024]{1,2,0:T(8,128)(2,1)} %copy.19, s32[]{:T(128)} %constant.62.clone.1, s32[]{:T(128)S(6)} %select_n.53, s32[]{:T(128)} %constant.62.clone.1) | dynamic-update-slice | bytes 3145732 | tf_op jit(solution)/shard_map/dynamic_update_slice | solution.py:51
  179.2 5.8 fusion.30
  197.9 7.6 %collective-permute-done.6 = f32[192,384]{1,0:T(8,128)S(1)} collective-permute-done((f32[192,384]{1,0:T(8,128)S(1)}, f32[192,384]{1,0:T(8,128)S(1)}, u32[]{:S(2)}, u32[]{:S(2)}) %collective-permute-start.6) | collective-permute-done | bytes 294944 | tf_op jit(solution)/shard_map/ppermute | solution.py:62
  206.8 21.7 %all-gather.21.cloned.1.call-done = f32[1536,640]{1,0:T(8,128)} async-done(((f32[384,640]{1,0:T(8,128)}), f32[1536,640]{1,0:T(8,128)}) %all-gather.21.cloned.1.call-update) | async-done | bytes 3932176 | tf_op jit(solution)/shard_map/all_gather | solution.py:33
  237.0 21.9 %all-gather.19.cloned.1.call-done = f32[768,384]{1,0:T(8,128)} async-done(((f32[192,384]{1,0:T(8,128)}), f32[768,384]{1,0:T(8,128)}) %all-gather.19.cloned.1.call-update) | async-done | bytes 1179664 | tf_op jit(solution)/shard_map/all_gather | solution.py:33
  276.8 6.4 %multiply_add_fusion.3 = f32[4,384,640]{2,1,0:T(8,128)} fusion(f32[4,384,640]{2,1,0:T(8,128)} %add_add_fusion.3, f32[4,384,640]{2,1,0:T(8,128)S(1)} %fusion.90, f32[4,384,640]{2,1,0:T(8,128)S(1)} %fusion.91, f32[4,384,640]{2,1,0:T(8,128)} %fusion.88), kind=kLoop, calls=%fused_computation.31 | loop fusion | flops 4915200 | bytes 19660800 | tf_op jit(solution)/shard_map/add | solution.py:114
  283.3 5.8 fusion.33
  329.3 8.5 %collective-permute-done.13 = f32[192,384]{1,0:T(8,128)S(1)} collective-permute-done((f32[192,384]{1,0:T(8,128)S(1)}, f32[192,384]{1,0:T(8,128)S(1)}, u32[]{:S(2)}, u32[]{:S(2)}) %collective-permute-start.13) | collective-permute-done | bytes 294944 | tf_op jit(solution)/shard_map/ppermute | solution.py:62
  338.6 7.3 %fusion.68 = f32[4,384,640]{2,1,0:T(8,128)} fusion(bf16[4,384,1024]{1,2,0:T(8,128)(2,1)} %dynamic_update_slice.31, f32[1024,640]{1,0:T(8,128)} %copy-done.6), kind=kOutput, calls=%fused_computation.162 | convolution fusion | flops 2016542720 | bytes 9699328 | tf_op jit(solution)/shard_map/std,dc->stc/dot_general | solution.py:26
  345.9 21.2 %all-gather.23.cloned.1.call-done = f32[768,384]{1,0:T(8,128)} async-done(((f32[192,384]{1,0:T(8,128)}), f32[768,384]{1,0:T(8,128)}) %all-gather.23.cloned.1.call-update) | async-done | bytes 1179664 | tf_op jit(solution)/shard_map/all_gather | solution.py:33
  384.9 6.4 %multiply_add_fusion.2 = f32[4,384,640]{2,1,0:T(8,128)} fusion(f32[4,384,640]{2,1,0:T(8,128)} %add_add_fusion.2, f32[4,384,640]{2,1,0:T(8,128)S(1)} %fusion.92, f32[4,384,640]{2,1,0:T(8,128)S(1)} %fusion.93, f32[4,384,640]{2,1,0:T(8,128)} %fusion.86), kind=kLoop, calls=%fused_computation.29 | loop fusion | flops 4915200 | bytes 19660800 | tf_op jit(solution)/shard_map/add | solution.py:114
  411.2 6.1 multiply_reduce_fusion.2
  434.4 7.6 %collective-permute-done.20 = f32[192,384]{1,0:T(8,128)S(1)} collective-permute-done((f32[192,384]{1,0:T(8,128)S(1)}, f32[192,384]{1,0:T(8,128)S(1)}, u32[]{:S(2)}, u32[]{:S(2)}) %collective-permute-start.20) | collective-permute-done | bytes 294944 | tf_op jit(solution)/shard_map/ppermute | solution.py:62
  443.0 7.3 %fusion.63 = f32[4,384,640]{2,1,0:T(8,128)} fusion(bf16[4,384,1024]{1,2,0:T(8,128)(2,1)} %dynamic_update_slice.31, f32[1024,640]{1,0:T(8,128)} %copy-done.8), kind=kOutput, calls=%fused_computation.157 | convolution fusion | flops 2016542720 | bytes 9699328 | tf_op jit(solution)/shard_map/std,dc->stc/dot_general | solution.py:26
  450.3 21.9 %all-gather.25.cloned.1.call-done = f32[768,384]{1,0:T(8,128)} async-done(((f32[192,384]{1,0:T(8,128)}), f32[768,384]{1,0:T(8,128)}) %all-gather.25.cloned.1.call-update) | async-done | bytes 1179664 | tf_op jit(solution)/shard_map/all_gather | solution.py:33
  490.0 6.6 %multiply_add_fusion.1 = f32[4,384,640]{2,1,0:T(8,128)} fusion(f32[4,384,640]{2,1,0:T(8,128)} %add_add_fusion.1, f32[4,384,640]{2,1,0:T(8,128)S(1)} %fusion.94, f32[4,384,640]{2,1,0:T(8,128)S(1)} %fusion.95, f32[4,384,640]{2,1,0:T(8,128)} %fusion.84), kind=kLoop, calls=%fused_computation.27 | loop fusion | flops 4915200 | bytes 19660800 | tf_op jit(solution)/shard_map/add | solution.py:114
  538.5 7.6 %collective-permute-done.27 = f32[192,384]{1,0:T(8,128)S(1)} collective-permute-done((f32[192,384]{1,0:T(8,128)S(1)}, f32[192,384]{1,0:T(8,128)S(1)}, u32[]{:S(2)}, u32[]{:S(2)}) %collective-permute-start.27) | collective-permute-done | bytes 294944 | tf_op jit(solution)/shard_map/ppermute | solution.py:62
  546.8 7.5 %fusion.58 = f32[4,384,640]{2,1,0:T(8,128)} fusion(bf16[4,384,1024]{1,2,0:T(8,128)(2,1)} %dynamic_update_slice.31, f32[1024,640]{1,0:T(8,128)} %copy-done.11), kind=kOutput, calls=%fused_computation.152 | convolution fusion | flops 2016542720 | bytes 9699328 | tf_op jit(solution)/shard_map/std,dc->stc/dot_general | solution.py:26
  554.3 22.0 %all-gather.27.cloned.1.call-done = f32[768,384]{1,0:T(8,128)} async-done(((f32[192,384]{1,0:T(8,128)}), f32[768,384]{1,0:T(8,128)}) %all-gather.27.cloned.1.call-update) | async-done | bytes 1179664 | tf_op jit(solution)/shard_map/all_gather | solution.py:33
  595.5 6.0 fusion.39
  (245 shorter events, 245.1 us)
Async XLA Ops:
  6.5 68.6 %all-gather.15.cloned.1.call-start = ((), (), s32[]{:S(2)}) async-start(), calls=%async_computation | async-start | bytes 3932160 | tf_op jit(solution)/shard_map/all_gather | solution.py:33
  8.7 143.2 %all-gather.17.cloned.1.call-start = ((), (), s32[]{:S(2)}) async-start(), calls=%async_computation.1 | async-start | bytes 4915200 | tf_op jit(solution)/shard_map/all_gather | solution.py:33
  14.3 16.6 %collective-permute-start.2 = (f32[384,384]{1,0:T(8,128)S(1)}, f32[384,384]{1,0:T(8,128)S(1)}, u32[]{:S(2)}, u32[]{:S(2)}) collective-permute-start(f32[384,384]{1,0:T(8,128)S(1)} %add.309), channel_id=1, source_target_pairs={{0,2},{1,3},{2,0},{3,1},{4,6},{5,7},{6,4},{7,5},{8,10},{9,11},{10,... | collective-permute-start | bytes 1769480 | tf_op jit(solution)/shard_map/ppermute | solution.py:41
  33.1 195.3 %all-gather.21.cloned.1.call-start = ((), (), s32[]{:S(2)}) async-start(), calls=%async_computation.3 | async-start | bytes 4915200 | tf_op jit(solution)/shard_map/all_gather | solution.py:33
  75.2 76.7 %collective-permute-start = (f32[4,192,1024]{2,1,0:T(8,128)}, f32[4,192,1024]{2,1,0:T(8,128)}, u32[]{:S(2)}, u32[]{:S(2)}) collective-permute-start(f32[4,192,1024]{2,1,0:T(8,128)} %bitcast.205), channel_id=1, source_target_pairs={{0,1},{1,0},{2,3},{3,2},{4,5},{5,4},{6,7},{7,6},{8,9},{9,8},{10,11... | collective-permute-start | bytes 9437192 | tf_op jit(solution)/shard_map/ppermute | solution.py:49
  76.2 182.7 %all-gather.19.cloned.1.call-start = ((), (), s32[]{:S(2)}) async-start(), calls=%async_computation.2 | async-start | bytes 1474560 | tf_op jit(solution)/shard_map/all_gather | solution.py:33
  196.3 9.1 %collective-permute-start.6 = (f32[192,384]{1,0:T(8,128)S(1)}, f32[192,384]{1,0:T(8,128)S(1)}, u32[]{:S(2)}, u32[]{:S(2)}) collective-permute-start(f32[192,384]{1,0:T(8,128)S(1)} %dynamic-slice_add_fusion.3), channel_id=1, source_target_pairs={{0,2},{1,3},{2,0},{3,1},{4,6},{5,7},{6,4},{7,5},{8,10},{9,11},{10,... | collective-permute-start | bytes 884744 | tf_op jit(solution)/shard_map/ppermute | solution.py:62
  206.2 160.9 %all-gather.23.cloned.1.call-start = ((), (), s32[]{:S(2)}) async-start(), calls=%async_computation.4 | async-start | bytes 1474560 | tf_op jit(solution)/shard_map/all_gather | solution.py:33
  259.0 11.9 %collective-permute-start.7 = (f32[4,192,384]{2,1,0:T(8,128)}, f32[4,192,384]{2,1,0:T(8,128)S(1)}, u32[]{:S(2)}, u32[]{:S(2)}) collective-permute-start(f32[4,192,384]{2,1,0:T(8,128)} %bitcast.209), channel_id=1, source_target_pairs={{0,1},{1,0},{2,3},{3,2},{4,5},{5,4},{6,7},{7,6},{8,9},{9,8},{10,11... | collective-permute-start | bytes 3538952 | tf_op jit(solution)/shard_map/ppermute | solution.py:49
  297.7 5.3 collective-permute-start.8
  300.1 6.1 collective-permute-start.4
  304.3 3.6 collective-permute-start.9
  315.0 3.7 collective-permute-start.11
  328.7 9.1 %collective-permute-start.13 = (f32[192,384]{1,0:T(8,128)S(1)}, f32[192,384]{1,0:T(8,128)S(1)}, u32[]{:S(2)}, u32[]{:S(2)}) collective-permute-start(f32[192,384]{1,0:T(8,128)S(1)} %dynamic-slice_add_fusion.2), channel_id=1, source_target_pairs={{0,2},{1,3},{2,0},{3,1},{4,6},{5,7},{6,4},{7,5},{8,10},{9,11},{10,... | collective-permute-start | bytes 884744 | tf_op jit(solution)/shard_map/ppermute | solution.py:62
  338.6 133.7 %all-gather.25.cloned.1.call-start = ((), (), s32[]{:S(2)}) async-start(), calls=%async_computation.5 | async-start | bytes 1474560 | tf_op jit(solution)/shard_map/all_gather | solution.py:33
  367.2 11.8 %collective-permute-start.14 = (f32[4,192,384]{2,1,0:T(8,128)}, f32[4,192,384]{2,1,0:T(8,128)S(1)}, u32[]{:S(2)}, u32[]{:S(2)}) collective-permute-start(f32[4,192,384]{2,1,0:T(8,128)} %bitcast.211), channel_id=1, source_target_pairs={{0,1},{1,0},{2,3},{3,2},{4,5},{5,4},{6,7},{7,6},{8,9},{9,8},{10,11... | collective-permute-start | bytes 3538952 | tf_op jit(solution)/shard_map/ppermute | solution.py:49
  406.9 3.7 collective-permute-start.16
  432.9 9.1 %collective-permute-start.20 = (f32[192,384]{1,0:T(8,128)S(1)}, f32[192,384]{1,0:T(8,128)S(1)}, u32[]{:S(2)}, u32[]{:S(2)}) collective-permute-start(f32[192,384]{1,0:T(8,128)S(1)} %dynamic-slice_add_fusion.1), channel_id=1, source_target_pairs={{0,2},{1,3},{2,0},{3,1},{4,6},{5,7},{6,4},{7,5},{8,10},{9,11},{10,... | collective-permute-start | bytes 884744 | tf_op jit(solution)/shard_map/ppermute | solution.py:62
  442.8 133.5 %all-gather.27.cloned.1.call-start = ((), (), s32[]{:S(2)}) async-start(), calls=%async_computation.6 | async-start | bytes 1474560 | tf_op jit(solution)/shard_map/all_gather | solution.py:33
  472.2 11.8 %collective-permute-start.21 = (f32[4,192,384]{2,1,0:T(8,128)}, f32[4,192,384]{2,1,0:T(8,128)S(1)}, u32[]{:S(2)}, u32[]{:S(2)}) collective-permute-start(f32[4,192,384]{2,1,0:T(8,128)} %bitcast.213), channel_id=1, source_target_pairs={{0,1},{1,0},{2,3},{3,2},{4,5},{5,4},{6,7},{7,6},{8,9},{9,8},{10,11... | collective-permute-start | bytes 3538952 | tf_op jit(solution)/shard_map/ppermute | solution.py:49
  522.9 3.6 collective-permute-start.25
  536.9 9.1 %collective-permute-start.27 = (f32[192,384]{1,0:T(8,128)S(1)}, f32[192,384]{1,0:T(8,128)S(1)}, u32[]{:S(2)}, u32[]{:S(2)}) collective-permute-start(f32[192,384]{1,0:T(8,128)S(1)} %dynamic-slice_add_fusion), channel_id=1, source_target_pairs={{0,2},{1,3},{2,0},{3,1},{4,6},{5,7},{6,4},{7,5},{8,10},{9,11},{10,... | collective-permute-start | bytes 884744 | tf_op jit(solution)/shard_map/ppermute | solution.py:62
  576.3 11.8 %collective-permute-start.28 = (f32[4,192,384]{2,1,0:T(8,128)}, f32[4,192,384]{2,1,0:T(8,128)S(1)}, u32[]{:S(2)}, u32[]{:S(2)}) collective-permute-start(f32[4,192,384]{2,1,0:T(8,128)} %bitcast.207), channel_id=1, source_target_pairs={{0,1},{1,0},{2,3},{3,2},{4,5},{5,4},{6,7},{7,6},{8,9},{9,8},{10,11... | collective-permute-start | bytes 3538952 | tf_op jit(solution)/shard_map/ppermute | solution.py:49
  613.0 3.7 collective-permute-start.30
  (49 other events, 191.0 us)
Sparse Core Ops, SparseCore 0:
  8.9 66.1 all-gather.14
  76.7 75.0 all-gather.16
  153.4 74.9 all-gather.20
  229.9 28.9 all-gather.18
  338.7 28.3 all-gather.22
  442.9 29.2 all-gather.24
  546.9 29.2 all-gather.26

commit v4 on v3

--- a/solution.py
+++ b/solution.py
@@ -99,15 +99,29 @@
     def square_sum(x):
         return inner_sum(jnp.sum(x * x), inner)
 
-    def pair_gather(left):
+    def pair_sum(left, scalar):
         partial = exact_dot("tc,uc->tu", inputs, left, exact_first=False)
+        extra = jnp.full((8, count), scalar, f32)
         if not split:
-            return site_gather(inner_sum(partial, inner))
-        return halves(site_gather(half_sum(partial, inner)), jnp.zeros((sites, count, count), f32))
+            total = inner_sum(jnp.concatenate([partial, extra]), inner)
+            return total[:count], total[count, 0]
+        half = count // 2
+        mine = jnp.concatenate([lax.dynamic_slice_in_dim(partial, core * half, half, 0), extra])
+        theirs = jnp.concatenate([lax.dynamic_slice_in_dim(partial, (1 - core) * half, half, 0), extra])
+        part = mine + lax.ppermute(theirs, "inner", [(i, i ^ 1) for i in range(inner)])
+        bit = 2
+        while bit < inner:
+            part = part + lax.ppermute(part, "inner", [(i, i ^ bit) for i in range(inner)])
+            bit *= 2
+        return part[:half], part[half, 0]
 
-    def apply_operator(direction):
-        left_own = exact_dot("td,dc->tc", grads, direction)
-        pair_all = pair_gather(left_own)
+    def pair_spread(pair_part):
+        if not split:
+            return site_gather(pair_part)
+        return halves(site_gather(pair_part), jnp.zeros((sites, count, count), f32))
+
+    def apply_operator(pair_part, direction):
+        pair_all = pair_spread(pair_part)
         left_all = exact_dot("std,dc->stc", every_grad, direction)
         pair_all, left_all = lax.optimization_barrier((pair_all, left_all))
         mixed_all = (
@@ -119,15 +133,20 @@
     merged = jnp.zeros_like(rhs)
     residual = rhs
     direction = rhs
-    norm_now = square_sum(residual)
+    pair_part, norm_now = pair_sum(exact_dot("td,dc->tc", grads, rhs), jnp.sum(rhs * rhs))
     for count_step in range(ITERS):
-        image = apply_operator(direction)
+        if count_step:
+            pair_r, norm_next = pair_sum(exact_dot("td,dc->tc", grads, residual), jnp.sum(residual * residual))
+            beta = norm_next / norm_now
+            pair_part = pair_r + beta * pair_part
+            direction = residual + beta * direction
+            norm_now = norm_next
+        image = apply_operator(pair_part, direction)
         alpha = norm_now / inner_sum(jnp.sum(direction * image), inner)
         merged = merged + alpha * direction
         residual = residual - alpha * image
-        norm_next = square_sum(residual)
-        direction = residual + norm_next / norm_now * direction
-        norm_now = norm_next
+    norm_next = square_sum(residual)
+    direction = residual + norm_next / norm_now * direction
     return lax.dynamic_slice_in_dim(merged, me * rows, rows, 0)
 
 

time: 634 us -> 609 us (0.961)
  waiting for transfers between devices: 267 us -> 253 us
  local copies, waits for them, and re-layouts: 56.5 us -> 67.6 us
  matrix products: 177 us -> 166 us
  starting transfers between devices: 34.5 us -> 26.1 us
    ppermute x18 -> x10, starting transfers between devices: 28 us -> 18.5 us  [inner_sum(): x = x + lax.ppermute(x, 'inner', [(i, i ^ bit) for i in range(size)])]
    ppermute x18 -> x10, waiting for transfers between devices: 30.2 us -> 22.8 us  [inner_sum(): x = x + lax.ppermute(x, 'inner', [(i, i ^ bit) for i in range(size)])]
    all_gather x7, waiting for transfers between devices: 200 us -> 192 us  [site_gather(): lax.all_gather(lax.optimization_barrier(x), 'site')]
    dot_general x39, matrix products: 143 us -> 136 us  [one(): return jnp.einsum(spec, exact, part, preferred_element_type=f32)]
    add x11 -> x14, other arithmetic: 12.4 us -> 15.8 us  [the longest x3 8.81 us: per_device(): direction = residual + beta * direction]
  transfers between devices with their start and end apart: 38 -> 30, of which waited for: 31 -> 25; matrix products, arithmetic and copies ran while one was open for 24% -> 25% of each run, Pallas kernels for 0% -> 0%
where the time goes in v4:
time: 609 us; the launch traced here: 602 us
  waiting for transfers between devices  253 us (42%)
  matrix products  166 us (27%)
  local copies, waits for them, and re-layouts  67.6 us (11%)
  other arithmetic  60.9 us (10%)
  between operations  28.4 us (5%)
  starting transfers between devices  26.1 us (4%)
    all_gather x7, waiting for transfers between devices, site_gather(): lax.all_gather(lax.optimization_barrier(x), 'site')  192 us
    dot_general x39, matrix products, one(): return jnp.einsum(spec, exact, part, preferred_element_type=f32)  136 us
    ppermute x4, waiting for transfers between devices, pair_sum(): lax.ppermute(part, 'inner', [(i, i ^ bit) for i in range(inner)])  31.4 us
    dot_general x30, matrix products, one(): return jnp.einsum(spec, part, exact, preferred_element_type=f32)  27.4 us
    ppermute x10, waiting for transfers between devices, inner_sum(): x = x + lax.ppermute(x, 'inner', [(i, i ^ bit) for i in range(size)])  22.8 us
    dynamic_update_slice x5, local copies, waits for them, and re-layouts, halves(): lax.dynamic_update_slice_in_dim(full, finish(other), (1 - core) * half, 1)  22.8 us
    add x4, other arithmetic, apply_operator(): exact_dot('stu,suc->stc', every_input, pair_all, exact_first=False)  20.6 us
    dynamic_update_slice x5, local copies, waits for them, and re-layouts, halves(): full = lax.dynamic_update_slice_in_dim(full, finish(x), core * half, 1)  20.2 us
  transfers between devices with their start and end apart: 30, of which 25 were waited for; matrix products, arithmetic and copies ran while one was open for 25% of the time, Pallas kernels for 0%

profile of v4, /device:TPU:0, one launch (start us, length us, event | category | flops | bytes accessed | tf_op | source)
XLA Modules:
  0.0 601.8 jit_solution(7248758497935214900)
XLA Ops:
  17.2 13.6 %collective-permute-done.2 = f32[384,384]{1,0:T(8,128)S(1)} collective-permute-done((f32[384,384]{1,0:T(8,128)S(1)}, f32[384,384]{1,0:T(8,128)S(1)}, u32[]{:S(2)}, u32[]{:S(2)}) %collective-permute-start.2) | collective-permute-done | bytes 589856 | tf_op jit(solution)/shard_map/ppermute | solution.py:41
  33.2 42.0 %all-gather.15.cloned.1.call-done = f32[768,1024]{1,0:T(8,128)} async-done(((f32[192,1024]{1,0:T(8,128)}), f32[768,1024]{1,0:T(8,128)}) %all-gather.15.cloned.1.call-update) | async-done | bytes 3145744 | tf_op jit(solution)/shard_map/all_gather | solution.py:33
  83.0 19.9 %dynamic_update_slice.30 = bf16[4,384,1024]{1,2,0:T(8,128)(2,1)} dynamic-update-slice(bf16[4,384,1024]{1,2,0:T(8,128)(2,1)} %broadcast_in_dim.2, bf16[4,192,1024]{1,2,0:T(8,128)(2,1)} %copy.18, s32[]{:T(128)} %constant.54.clone.1, s32[]{:T(128)S(6)} %select_n.44, s32[]{:T(128)} %constant.54.clone.1) | dynamic-update-slice | bytes 3145732 | tf_op jit(solution)/shard_map/dynamic_update_slice | solution.py:50
  102.9 48.9 %all-gather.17.cloned.1.call-done = f32[1536,640]{1,0:T(8,128)} async-done(((f32[384,640]{1,0:T(8,128)}), f32[1536,640]{1,0:T(8,128)}) %all-gather.17.cloned.1.call-update) | async-done | bytes 3932176 | tf_op jit(solution)/shard_map/all_gather | solution.py:33
  156.7 22.4 %dynamic_update_slice.31 = bf16[4,384,1024]{1,2,0:T(8,128)(2,1)} dynamic-update-slice(bf16[4,384,1024]{1,2,0:T(8,128)(2,1)} %dynamic_update_slice.30, bf16[4,192,1024]{1,2,0:T(8,128)(2,1)} %copy.19, s32[]{:T(128)} %constant.54.clone.1, s32[]{:T(128)S(6)} %select_n.45, s32[]{:T(128)} %constant.54.clone.1) | dynamic-update-slice | bytes 3145732 | tf_op jit(solution)/shard_map/dynamic_update_slice | solution.py:51
  179.2 5.8 fusion.33
  199.8 7.8 %collective-permute-done.4 = f32[200,384]{1,0:T(8,128)S(1)} collective-permute-done((f32[200,384]{1,0:T(8,128)S(1)}, f32[200,384]{1,0:T(8,128)S(1)}, u32[]{:S(2)}, u32[]{:S(2)}) %collective-permute-start.4) | collective-permute-done | bytes 307232 | tf_op jit(solution)/shard_map/ppermute | solution.py:114
  209.0 19.5 %all-gather.21.cloned.1.call-done = f32[1536,640]{1,0:T(8,128)} async-done(((f32[384,640]{1,0:T(8,128)}), f32[1536,640]{1,0:T(8,128)}) %all-gather.21.cloned.1.call-update) | async-done | bytes 3932176 | tf_op jit(solution)/shard_map/all_gather | solution.py:33
  237.0 22.0 %all-gather.19.cloned.1.call-done = f32[768,384]{1,0:T(8,128)} async-done(((f32[192,384]{1,0:T(8,128)}), f32[768,384]{1,0:T(8,128)}) %all-gather.19.cloned.1.call-update) | async-done | bytes 1179664 | tf_op jit(solution)/shard_map/all_gather | solution.py:33
  259.0 5.6 fusion.96
  276.7 6.4 %multiply_add_fusion.3 = f32[4,384,640]{2,1,0:T(8,128)} fusion(f32[4,384,640]{2,1,0:T(8,128)} %add_add_fusion.3, f32[4,384,640]{2,1,0:T(8,128)S(1)} %fusion.111, f32[4,384,640]{2,1,0:T(8,128)S(1)} %fusion.112, f32[4,384,640]{2,1,0:T(8,128)} %fusion.109), kind=kLoop, calls=%fused_computation.31 | loop fusion | flops 4915200 | bytes 19660800 | tf_op jit(solution)/shard_map/add | solution.py:128
  316.6 7.9 %collective-permute-done.9 = f32[200,384]{1,0:T(8,128)S(1)} collective-permute-done((f32[200,384]{1,0:T(8,128)S(1)}, f32[200,384]{1,0:T(8,128)S(1)}, u32[]{:S(2)}, u32[]{:S(2)}) %collective-permute-start.9) | collective-permute-done | bytes 307232 | tf_op jit(solution)/shard_map/ppermute | solution.py:114
  338.2 20.0 %all-gather.23.cloned.1.call-done = f32[768,384]{1,0:T(8,128)} async-done(((f32[192,384]{1,0:T(8,128)}), f32[768,384]{1,0:T(8,128)}) %all-gather.23.cloned.1.call-update) | async-done | bytes 1179664 | tf_op jit(solution)/shard_map/all_gather | solution.py:33
  358.2 5.6 fusion.78
  379.5 5.8 fusion.38
  413.6 7.8 %collective-permute-done.14 = f32[200,384]{1,0:T(8,128)S(1)} collective-permute-done((f32[200,384]{1,0:T(8,128)S(1)}, f32[200,384]{1,0:T(8,128)S(1)}, u32[]{:S(2)}, u32[]{:S(2)}) %collective-permute-start.14) | collective-permute-done | bytes 307232 | tf_op jit(solution)/shard_map/ppermute | solution.py:114
  435.1 20.1 %all-gather.25.cloned.1.call-done = f32[768,384]{1,0:T(8,128)} async-done(((f32[192,384]{1,0:T(8,128)}), f32[768,384]{1,0:T(8,128)}) %all-gather.25.cloned.1.call-update) | async-done | bytes 1179664 | tf_op jit(solution)/shard_map/all_gather | solution.py:33
  455.3 5.6 fusion.85
  476.4 5.8 fusion.40
  510.6 7.8 %collective-permute-done.19 = f32[200,384]{1,0:T(8,128)S(1)} collective-permute-done((f32[200,384]{1,0:T(8,128)S(1)}, f32[200,384]{1,0:T(8,128)S(1)}, u32[]{:S(2)}, u32[]{:S(2)}) %collective-permute-start.19) | collective-permute-done | bytes 307232 | tf_op jit(solution)/shard_map/ppermute | solution.py:114
  530.6 20.0 %all-gather.27.cloned.1.call-done = f32[768,384]{1,0:T(8,128)} async-done(((f32[192,384]{1,0:T(8,128)}), f32[768,384]{1,0:T(8,128)}) %all-gather.27.cloned.1.call-update) | async-done | bytes 1179664 | tf_op jit(solution)/shard_map/all_gather | solution.py:33
  550.6 5.6 fusion.92
  569.7 6.0 fusion.42
  578.4 5.6 fusion.14
  (267 shorter events, 235.9 us)
Async XLA Ops:
  6.5 68.6 %all-gather.15.cloned.1.call-start = ((), (), s32[]{:S(2)}) async-start(), calls=%async_computation | async-start | bytes 3932160 | tf_op jit(solution)/shard_map/all_gather | solution.py:33
  8.7 143.2 %all-gather.17.cloned.1.call-start = ((), (), s32[]{:S(2)}) async-start(), calls=%async_computation.1 | async-start | bytes 4915200 | tf_op jit(solution)/shard_map/all_gather | solution.py:33
  12.1 2.1 collective-permute-start.1
  14.3 16.6 %collective-permute-start.2 = (f32[384,384]{1,0:T(8,128)S(1)}, f32[384,384]{1,0:T(8,128)S(1)}, u32[]{:S(2)}, u32[]{:S(2)}) collective-permute-start(f32[384,384]{1,0:T(8,128)S(1)} %add.306), channel_id=1, source_target_pairs={{0,2},{1,3},{2,0},{3,1},{4,6},{5,7},{6,4},{7,5},{8,10},{9,11},{10,... | collective-permute-start | bytes 1769480 | tf_op jit(solution)/shard_map/ppermute | solution.py:41
  33.2 195.3 %all-gather.21.cloned.1.call-start = ((), (), s32[]{:S(2)}) async-start(), calls=%async_computation.3 | async-start | bytes 4915200 | tf_op jit(solution)/shard_map/all_gather | solution.py:33
  75.2 76.7 %collective-permute-start = (f32[4,192,1024]{2,1,0:T(8,128)}, f32[4,192,1024]{2,1,0:T(8,128)}, u32[]{:S(2)}, u32[]{:S(2)}) collective-permute-start(f32[4,192,1024]{2,1,0:T(8,128)} %bitcast.209), channel_id=1, source_target_pairs={{0,1},{1,0},{2,3},{3,2},{4,5},{5,4},{6,7},{7,6},{8,9},{9,8},{10,11... | collective-permute-start | bytes 9437192 | tf_op jit(solution)/shard_map/ppermute | solution.py:49
  76.2 182.7 %all-gather.19.cloned.1.call-start = ((), (), s32[]{:S(2)}) async-start(), calls=%async_computation.2 | async-start | bytes 1474560 | tf_op jit(solution)/shard_map/all_gather | solution.py:33
  198.3 9.4 %collective-permute-start.4 = (f32[200,384]{1,0:T(8,128)S(1)}, f32[200,384]{1,0:T(8,128)S(1)}, u32[]{:S(2)}, u32[]{:S(2)}) collective-permute-start(f32[200,384]{1,0:T(8,128)S(1)} %pad_add_fusion.3), channel_id=1, source_target_pairs={{0,2},{1,3},{2,0},{3,1},{4,6},{5,7},{6,4},{7,5},{8,10},{9,11},{10,... | collective-permute-start | bytes 921608 | tf_op jit(solution)/shard_map/ppermute | solution.py:114
  208.4 149.8 %all-gather.23.cloned.1.call-start = ((), (), s32[]{:S(2)}) async-start(), calls=%async_computation.4 | async-start | bytes 1474560 | tf_op jit(solution)/shard_map/all_gather | solution.py:33
  259.0 11.8 %collective-permute-start.5 = (f32[4,192,384]{2,1,0:T(8,128)}, f32[4,192,384]{2,1,0:T(8,128)S(1)}, u32[]{:S(2)}, u32[]{:S(2)}) collective-permute-start(f32[4,192,384]{2,1,0:T(8,128)} %bitcast.213), channel_id=1, source_target_pairs={{0,1},{1,0},{2,3},{3,2},{4,5},{5,4},{6,7},{7,6},{8,9},{9,8},{10,11... | collective-permute-start | bytes 3538952 | tf_op jit(solution)/shard_map/ppermute | solution.py:49
  298.9 3.6 collective-permute-start.7
  315.1 9.4 %collective-permute-start.9 = (f32[200,384]{1,0:T(8,128)S(1)}, f32[200,384]{1,0:T(8,128)S(1)}, u32[]{:S(2)}, u32[]{:S(2)}) collective-permute-start(f32[200,384]{1,0:T(8,128)S(1)} %pad_add_fusion.2), channel_id=1, source_target_pairs={{0,2},{1,3},{2,0},{3,1},{4,6},{5,7},{6,4},{7,5},{8,10},{9,11},{10,... | collective-permute-start | bytes 921608 | tf_op jit(solution)/shard_map/ppermute | solution.py:114
  328.7 126.6 %all-gather.25.cloned.1.call-start = ((), (), s32[]{:S(2)}) async-start(), calls=%async_computation.5 | async-start | bytes 1474560 | tf_op jit(solution)/shard_map/all_gather | solution.py:33
  358.2 11.8 %collective-permute-start.10 = (f32[4,192,384]{2,1,0:T(8,128)}, f32[4,192,384]{2,1,0:T(8,128)S(1)}, u32[]{:S(2)}, u32[]{:S(2)}) collective-permute-start(f32[4,192,384]{2,1,0:T(8,128)} %bitcast.215), channel_id=1, source_target_pairs={{0,1},{1,0},{2,3},{3,2},{4,5},{5,4},{6,7},{7,6},{8,9},{9,8},{10,11... | collective-permute-start | bytes 3538952 | tf_op jit(solution)/shard_map/ppermute | solution.py:49
  392.8 2.0 collective-permute-start.11
  396.0 3.7 collective-permute-start.12
  412.1 9.4 %collective-permute-start.14 = (f32[200,384]{1,0:T(8,128)S(1)}, f32[200,384]{1,0:T(8,128)S(1)}, u32[]{:S(2)}, u32[]{:S(2)}) collective-permute-start(f32[200,384]{1,0:T(8,128)S(1)} %pad_add_fusion.1), channel_id=1, source_target_pairs={{0,2},{1,3},{2,0},{3,1},{4,6},{5,7},{6,4},{7,5},{8,10},{9,11},{10,... | collective-permute-start | bytes 921608 | tf_op jit(solution)/shard_map/ppermute | solution.py:114
  425.8 124.7 %all-gather.27.cloned.1.call-start = ((), (), s32[]{:S(2)}) async-start(), calls=%async_computation.6 | async-start | bytes 1474560 | tf_op jit(solution)/shard_map/all_gather | solution.py:33
  455.3 11.8 %collective-permute-start.15 = (f32[4,192,384]{2,1,0:T(8,128)}, f32[4,192,384]{2,1,0:T(8,128)S(1)}, u32[]{:S(2)}, u32[]{:S(2)}) collective-permute-start(f32[4,192,384]{2,1,0:T(8,128)} %bitcast.217), channel_id=1, source_target_pairs={{0,1},{1,0},{2,3},{3,2},{4,5},{5,4},{6,7},{7,6},{8,9},{9,8},{10,11... | collective-permute-start | bytes 3538952 | tf_op jit(solution)/shard_map/ppermute | solution.py:49
  489.7 2.0 collective-permute-start.16
  492.9 3.7 collective-permute-start.17
  509.1 9.4 %collective-permute-start.19 = (f32[200,384]{1,0:T(8,128)S(1)}, f32[200,384]{1,0:T(8,128)S(1)}, u32[]{:S(2)}, u32[]{:S(2)}) collective-permute-start(f32[200,384]{1,0:T(8,128)S(1)} %pad_add_fusion), channel_id=1, source_target_pairs={{0,2},{1,3},{2,0},{3,1},{4,6},{5,7},{6,4},{7,5},{8,10},{9,11},{10,... | collective-permute-start | bytes 921608 | tf_op jit(solution)/shard_map/ppermute | solution.py:114
  550.6 11.8 %collective-permute-start.20 = (f32[4,192,384]{2,1,0:T(8,128)}, f32[4,192,384]{2,1,0:T(8,128)S(1)}, u32[]{:S(2)}, u32[]{:S(2)}) collective-permute-start(f32[4,192,384]{2,1,0:T(8,128)} %bitcast.211), channel_id=1, source_target_pairs={{0,1},{1,0},{2,3},{3,2},{4,5},{5,4},{6,7},{7,6},{8,9},{9,8},{10,11... | collective-permute-start | bytes 3538952 | tf_op jit(solution)/shard_map/ppermute | solution.py:49
  587.2 3.7 collective-permute-start.22
  (54 other events, 238.1 us)
Sparse Core Ops, SparseCore 0:
  8.9 66.1 all-gather.14
  76.7 75.0 all-gather.16
  153.4 74.9 all-gather.20
  229.9 28.9 all-gather.18
  328.9 29.2 all-gather.22
  425.9 29.2 all-gather.24
  521.2 29.2 all-gather.26

commit v5 on v4

--- a/solution.py
+++ b/solution.py
@@ -31,6 +31,20 @@
 
 def site_gather(x):
     return lax.optimization_barrier(lax.all_gather(lax.optimization_barrier(x), "site"))
+
+
+def line_gather(x):
+    sites = lax.axis_size("site")
+    me = lax.axis_index("site")
+    out = lax.dynamic_update_slice_in_dim(jnp.zeros((sites,) + x.shape, x.dtype), x[None], me, 0)
+    right = left = x
+    for step in range(1, sites):
+        right = lax.ppermute(right, "site", [(i, i + 1) for i in range(sites - 1)])
+        left = lax.ppermute(left, "site", [(i + 1, i) for i in range(sites - 1)])
+        for block, at in ((right, (me - step) % sites), (left, (me + step) % sites)):
+            now = lax.dynamic_index_in_dim(out, at, 0)
+            out = lax.dynamic_update_slice_in_dim(out, now + block[None], at, 0)
+    return out
 
 
 def inner_sum(x, size):
@@ -73,7 +87,7 @@
     count = inputs.shape[0]
     rows = grads.shape[1] // sites
 
-    every_input = (site_gather(inputs.astype(f32) * 2.0) * 0.5).astype(bf16)
+    every_input = (line_gather(inputs.astype(f32) * 2.0) * 0.5).astype(bf16)
     core = lax.axis_index("inner") % 2
     split = inner % 2 == 0 and count % 16 == 0
     if split:

time: 609 us -> 594 us (0.975)
  starting transfers between devices: 26.1 us -> 59.3 us
  waiting for transfers between devices: 253 us -> 229 us
  matrix products: 166 us -> 144 us
    all_gather x7 -> x6, waiting for transfers between devices: 192 us -> 125 us  [site_gather(): lax.all_gather(lax.optimization_barrier(x), 'site')]
    ppermute x0 -> x6, waiting for transfers between devices: none -> 50.5 us  [the longest x3 40 us: line_gather(): right = lax.ppermute(right, 'site', [(i, i + 1) for i in range(sites - 1)])]
    ppermute x0 -> x6, starting transfers between devices: none -> 33.3 us  [the longest x3 29.4 us: line_gather(): right = lax.ppermute(right, 'site', [(i, i + 1) for i in range(sites - 1)])]
    dot_general x39, matrix products: 136 us -> 114 us  [one(): return jnp.einsum(spec, exact, part, preferred_element_type=f32)]
    add x4 -> x0, other arithmetic: 20.6 us -> none  [apply_operator(): exact_dot('stu,suc->stc', every_input, pair_all, exact_first=False)]
    dynamic_update_slice x0 -> x7, other arithmetic: none -> 16.2 us  [the longest x6 15.1 us: line_gather(): out = lax.dynamic_update_slice_in_dim(out, now + block[None], at, 0)]
  transfers between devices with their start and end apart: 30 -> 35, of which waited for: 25 -> 27; matrix products, arithmetic and copies ran while one was open for 25% -> 27% of each run, Pallas kernels for 0% -> 0%
where the time goes in v5:
time: 594 us; the launch traced here: 586 us
  waiting for transfers between devices  229 us (39%)
  matrix products  144 us (24%)
  local copies, waits for them, and re-layouts  69.3 us (12%)
  starting transfers between devices  59.3 us (10%)
  other arithmetic  55.6 us (9%)
  between operations  28.2 us (5%)
    all_gather x6, waiting for transfers between devices, site_gather(): lax.all_gather(lax.optimization_barrier(x), 'site')  125 us
    dot_general x39, matrix products, one(): return jnp.einsum(spec, exact, part, preferred_element_type=f32)  114 us
    ppermute x3, waiting for transfers between devices, line_gather(): right = lax.ppermute(right, 'site', [(i, i + 1) for i in range(sites - 1)])  40 us
    ppermute x3, starting transfers between devices, line_gather(): right = lax.ppermute(right, 'site', [(i, i + 1) for i in range(sites - 1)])  29.4 us
    dot_general x30, matrix products, one(): return jnp.einsum(spec, part, exact, preferred_element_type=f32)  28.3 us
    ppermute x4, waiting for transfers between devices, pair_sum(): lax.ppermute(part, 'inner', [(i, i ^ bit) for i in range(inner)])  26 us
    ppermute x10, waiting for transfers between devices, inner_sum(): x = x + lax.ppermute(x, 'inner', [(i, i ^ bit) for i in range(size)])  23 us
    dynamic_update_slice x5, local copies, waits for them, and re-layouts, halves(): lax.dynamic_update_slice_in_dim(full, finish(other), (1 - core) * half, 1)  22.5 us
  transfers between devices with their start and end apart: 35, of which 27 were waited for; matrix products, arithmetic and copies ran while one was open for 27% of the time, Pallas kernels for 0%

profile of v5, /device:TPU:0, one launch (start us, length us, event | category | flops | bytes accessed | tf_op | source)
XLA Modules:
  0.0 586.3 jit_solution(7747198288563707131)
XLA Ops:
  17.2 13.6 %collective-permute-done.2 = f32[384,384]{1,0:T(8,128)S(1)} collective-permute-done((f32[384,384]{1,0:T(8,128)S(1)}, f32[384,384]{1,0:T(8,128)S(1)}, u32[]{:S(2)}, u32[]{:S(2)}) %collective-permute-start.2) | collective-permute-done | bytes 589856 | tf_op jit(solution)/shard_map/ppermute | solution.py:55
  33.2 41.9 %all-gather.13.cloned.1.call-done = f32[768,1024]{1,0:T(8,128)} async-done(((f32[192,1024]{1,0:T(8,128)}), f32[768,1024]{1,0:T(8,128)}) %all-gather.13.cloned.1.call-update) | async-done | bytes 3145744 | tf_op jit(solution)/shard_map/all_gather | solution.py:33
  78.8 34.1 %collective-permute-done.6 = f32[384,640]{1,0:T(8,128)} collective-permute-done((f32[384,640]{1,0:T(8,128)S(1)}, f32[384,640]{1,0:T(8,128)}, u32[]{:S(2)}, u32[]{:S(2)}) %collective-permute-start.6) | collective-permute-done | bytes 983072 | tf_op jit(solution)/shard_map/ppermute | solution.py:42
  112.9 20.9 %collective-permute-start.8 = (f32[384,640]{1,0:T(8,128)}, f32[384,640]{1,0:T(8,128)}, u32[]{:S(2)}, u32[]{:S(2)}) collective-permute-start(f32[384,640]{1,0:T(8,128)} %collective-permute-done.6), channel_id=1, source_target_pairs={{0,4},{4,8},{8,12},{1,5},{5,9},{9,13},{2,6},{6,10},{10,14},{3,7},{... | collective-permute-start | bytes 2949128 | tf_op jit(solution)/shard_map/ppermute | solution.py:42
  145.3 19.8 %dynamic_update_slice.51 = bf16[4,384,1024]{1,2,0:T(8,128)(2,1)} dynamic-update-slice(bf16[4,384,1024]{1,2,0:T(8,128)(2,1)} %broadcast_in_dim.29, bf16[4,192,1024]{1,2,0:T(8,128)(2,1)} %copy.18, s32[]{:T(128)} %constant.101.clone.1, s32[]{:T(128)S(6)} %select_n.96, s32[]{:T(128)} %constant.101.clone.1) | dynamic-update-slice | bytes 3145732 | tf_op jit(solution)/shard_map/dynamic_update_slice | solution.py:64
  165.1 17.9 %all-gather.15.cloned.1.call-done = f32[1536,640]{1,0:T(8,128)} async-done(((f32[384,640]{1,0:T(8,128)}), f32[1536,640]{1,0:T(8,128)}) %all-gather.15.cloned.1.call-update) | async-done | bytes 3932176 | tf_op jit(solution)/shard_map/all_gather | solution.py:33
  187.9 22.2 %dynamic_update_slice.52 = bf16[4,384,1024]{1,2,0:T(8,128)(2,1)} dynamic-update-slice(bf16[4,384,1024]{1,2,0:T(8,128)(2,1)} %dynamic_update_slice.51, bf16[4,192,1024]{1,2,0:T(8,128)(2,1)} %copy.19, s32[]{:T(128)} %constant.101.clone.1, s32[]{:T(128)S(6)} %select_n.97, s32[]{:T(128)} %constant.101.clone.1) | dynamic-update-slice | bytes 3145732 | tf_op jit(solution)/shard_map/dynamic_update_slice | solution.py:65
  210.1 5.8 fusion.34
  232.7 6.3 %collective-permute-start.10 = (f32[384,640]{1,0:T(8,128)}, f32[384,640]{1,0:T(8,128)}, u32[]{:S(2)}, u32[]{:S(2)}) collective-permute-start(f32[384,640]{1,0:T(8,128)} %collective-permute-done.8), channel_id=1, source_target_pairs={{0,4},{4,8},{8,12},{1,5},{5,9},{9,13},{2,6},{6,10},{10,14},{3,7},{... | collective-permute-start | bytes 2949128 | tf_op jit(solution)/shard_map/ppermute | solution.py:42
  254.1 5.9 %collective-permute-done.10 = f32[384,640]{1,0:T(8,128)} collective-permute-done((f32[384,640]{1,0:T(8,128)}, f32[384,640]{1,0:T(8,128)}, u32[]{:S(2)}, u32[]{:S(2)}) %collective-permute-start.10) | collective-permute-done | bytes 983072 | tf_op jit(solution)/shard_map/ppermute | solution.py:42
  262.6 7.0 %collective-permute-done.11 = f32[384,640]{1,0:T(8,128)S(1)} collective-permute-done((f32[384,640]{1,0:T(8,128)}, f32[384,640]{1,0:T(8,128)S(1)}, u32[]{:S(2)}, u32[]{:S(2)}) %collective-permute-start.11) | collective-permute-done | bytes 983072 | tf_op jit(solution)/shard_map/ppermute | solution.py:43
  280.4 5.5 all-gather.17.cloned.1.call-done
  286.0 5.6 fusion.96
  306.0 5.0 multiply_reduce_fusion.5
  331.8 7.7 %collective-permute-done.15 = f32[200,384]{1,0:T(8,128)S(1)} collective-permute-done((f32[200,384]{1,0:T(8,128)S(1)}, f32[200,384]{1,0:T(8,128)S(1)}, u32[]{:S(2)}, u32[]{:S(2)}) %collective-permute-start.15) | collective-permute-done | bytes 307232 | tf_op jit(solution)/shard_map/ppermute | solution.py:128
  353.0 19.6 %all-gather.19.cloned.1.call-done = f32[768,384]{1,0:T(8,128)} async-done(((f32[192,384]{1,0:T(8,128)}), f32[768,384]{1,0:T(8,128)}) %all-gather.19.cloned.1.call-update) | async-done | bytes 1179664 | tf_op jit(solution)/shard_map/all_gather | solution.py:33
  372.6 5.6 fusion.78
  418.2 7.8 %collective-permute-done.20 = f32[200,384]{1,0:T(8,128)S(1)} collective-permute-done((f32[200,384]{1,0:T(8,128)S(1)}, f32[200,384]{1,0:T(8,128)S(1)}, u32[]{:S(2)}, u32[]{:S(2)}) %collective-permute-start.20) | collective-permute-done | bytes 307232 | tf_op jit(solution)/shard_map/ppermute | solution.py:128
  439.7 20.0 %all-gather.21.cloned.1.call-done = f32[768,384]{1,0:T(8,128)} async-done(((f32[192,384]{1,0:T(8,128)}), f32[768,384]{1,0:T(8,128)}) %all-gather.21.cloned.1.call-update) | async-done | bytes 1179664 | tf_op jit(solution)/shard_map/all_gather | solution.py:33
  459.7 5.6 fusion.85
  505.2 7.8 %collective-permute-done.25 = f32[200,384]{1,0:T(8,128)S(1)} collective-permute-done((f32[200,384]{1,0:T(8,128)S(1)}, f32[200,384]{1,0:T(8,128)S(1)}, u32[]{:S(2)}, u32[]{:S(2)}) %collective-permute-start.25) | collective-permute-done | bytes 307232 | tf_op jit(solution)/shard_map/ppermute | solution.py:128
  520.0 4.9 fusion.62
  524.9 20.1 %all-gather.23.cloned.1.call-done = f32[768,384]{1,0:T(8,128)} async-done(((f32[192,384]{1,0:T(8,128)}), f32[768,384]{1,0:T(8,128)}) %all-gather.23.cloned.1.call-update) | async-done | bytes 1179664 | tf_op jit(solution)/shard_map/all_gather | solution.py:33
  545.0 5.6 fusion.92
  (260 shorter events, 241.9 us)
Async XLA Ops:
  6.5 68.6 %all-gather.13.cloned.1.call-start = ((), (), s32[]{:S(2)}) async-start(), calls=%async_computation | async-start | bytes 3932160 | tf_op jit(solution)/shard_map/all_gather | solution.py:33
  8.7 174.3 %all-gather.15.cloned.1.call-start = ((), (), s32[]{:S(2)}) async-start(), calls=%async_computation.1 | async-start | bytes 4915200 | tf_op jit(solution)/shard_map/all_gather | solution.py:33
  14.3 16.5 %collective-permute-start.2 = (f32[384,384]{1,0:T(8,128)S(1)}, f32[384,384]{1,0:T(8,128)S(1)}, u32[]{:S(2)}, u32[]{:S(2)}) collective-permute-start(f32[384,384]{1,0:T(8,128)S(1)} %add.382), channel_id=1, source_target_pairs={{0,2},{1,3},{2,0},{3,1},{4,6},{5,7},{6,4},{7,5},{8,10},{9,11},{10,... | collective-permute-start | bytes 1769480 | tf_op jit(solution)/shard_map/ppermute | solution.py:55
  33.2 252.8 %all-gather.17.cloned.1.call-start = ((), (), s32[]{:S(2)}) async-start(), calls=%async_computation.2 | async-start | bytes 1474560 | tf_op jit(solution)/shard_map/all_gather | solution.py:33
  75.2 107.9 %collective-permute-start = (f32[4,192,1024]{2,1,0:T(8,128)}, f32[4,192,1024]{2,1,0:T(8,128)}, u32[]{:S(2)}, u32[]{:S(2)}) collective-permute-start(f32[4,192,1024]{2,1,0:T(8,128)} %bitcast.231), channel_id=1, source_target_pairs={{0,1},{1,0},{2,3},{3,2},{4,5},{5,4},{6,7},{7,6},{8,9},{9,8},{10,11... | collective-permute-start | bytes 9437192 | tf_op jit(solution)/shard_map/ppermute | solution.py:63
  75.2 37.6 %collective-permute-start.6 = (f32[384,640]{1,0:T(8,128)S(1)}, f32[384,640]{1,0:T(8,128)}, u32[]{:S(2)}, u32[]{:S(2)}) collective-permute-start(f32[384,640]{1,0:T(8,128)S(1)} %convert_multiply_fusion), channel_id=1, source_target_pairs={{0,4},{4,8},{8,12},{1,5},{5,9},{9,13},{2,6},{6,10},{10,14},{3,7},{... | collective-permute-start | bytes 2949128 | tf_op jit(solution)/shard_map/ppermute | solution.py:42
  77.5 59.7 %collective-permute-start.7 = (f32[384,640]{1,0:T(8,128)S(1)}, f32[384,640]{1,0:T(8,128)}, u32[]{:S(2)}, u32[]{:S(2)}) collective-permute-start(f32[384,640]{1,0:T(8,128)S(1)} %convert_multiply_fusion), channel_id=1, source_target_pairs={{4,0},{8,4},{12,8},{5,1},{9,5},{13,9},{6,2},{10,6},{14,10},{7,3},{... | collective-permute-start | bytes 2949128 | tf_op jit(solution)/shard_map/ppermute | solution.py:43
  112.9 119.8 %collective-permute-start.8 = (f32[384,640]{1,0:T(8,128)}, f32[384,640]{1,0:T(8,128)}, u32[]{:S(2)}, u32[]{:S(2)}) collective-permute-start(f32[384,640]{1,0:T(8,128)} %collective-permute-done.6), channel_id=1, source_target_pairs={{0,4},{4,8},{8,12},{1,5},{5,9},{9,13},{2,6},{6,10},{10,14},{3,7},{... | collective-permute-start | bytes 2949128 | tf_op jit(solution)/shard_map/ppermute | solution.py:42
  137.2 101.9 %collective-permute-start.9 = (f32[384,640]{1,0:T(8,128)}, f32[384,640]{1,0:T(8,128)}, u32[]{:S(2)}, u32[]{:S(2)}) collective-permute-start(f32[384,640]{1,0:T(8,128)} %collective-permute-done.7), channel_id=1, source_target_pairs={{4,0},{8,4},{12,8},{5,1},{9,5},{13,9},{6,2},{10,6},{14,10},{7,3},{... | collective-permute-start | bytes 2949128 | tf_op jit(solution)/shard_map/ppermute | solution.py:43
  226.9 13.4 %collective-permute-start.3 = (f32[200,384]{1,0:T(8,128)S(1)}, f32[200,384]{1,0:T(8,128)S(1)}, u32[]{:S(2)}, u32[]{:S(2)}) collective-permute-start(f32[200,384]{1,0:T(8,128)S(1)} %concatenate.25), channel_id=1, source_target_pairs={{0,1},{1,0},{2,3},{3,2},{4,5},{5,4},{6,7},{7,6},{8,9},{9,8},{10,11... | collective-permute-start | bytes 921608 | tf_op jit(solution)/shard_map/ppermute | solution.py:125
  232.7 27.3 %collective-permute-start.10 = (f32[384,640]{1,0:T(8,128)}, f32[384,640]{1,0:T(8,128)}, u32[]{:S(2)}, u32[]{:S(2)}) collective-permute-start(f32[384,640]{1,0:T(8,128)} %collective-permute-done.8), channel_id=1, source_target_pairs={{0,4},{4,8},{8,12},{1,5},{5,9},{9,13},{2,6},{6,10},{10,14},{3,7},{... | collective-permute-start | bytes 2949128 | tf_op jit(solution)/shard_map/ppermute | solution.py:42
  239.0 30.6 %collective-permute-start.11 = (f32[384,640]{1,0:T(8,128)}, f32[384,640]{1,0:T(8,128)S(1)}, u32[]{:S(2)}, u32[]{:S(2)}) collective-permute-start(f32[384,640]{1,0:T(8,128)} %collective-permute-done.9), channel_id=1, source_target_pairs={{4,0},{8,4},{12,8},{5,1},{9,5},{13,9},{6,2},{10,6},{14,10},{7,3},{... | collective-permute-start | bytes 2949128 | tf_op jit(solution)/shard_map/ppermute | solution.py:43
  241.0 9.5 %collective-permute-start.4 = (f32[200,384]{1,0:T(8,128)S(1)}, f32[200,384]{1,0:T(8,128)S(1)}, u32[]{:S(2)}, u32[]{:S(2)}) collective-permute-start(f32[200,384]{1,0:T(8,128)S(1)} %pad_add_fusion.3), channel_id=1, source_target_pairs={{0,2},{1,3},{2,0},{3,1},{4,6},{5,7},{6,4},{7,5},{8,10},{9,11},{10,... | collective-permute-start | bytes 921608 | tf_op jit(solution)/shard_map/ppermute | solution.py:128
  251.3 121.3 %all-gather.19.cloned.1.call-start = ((), (), s32[]{:S(2)}) async-start(), calls=%async_computation.3 | async-start | bytes 1474560 | tf_op jit(solution)/shard_map/all_gather | solution.py:33
  286.0 9.9 %collective-permute-start.5 = (f32[4,192,384]{2,1,0:T(8,128)}, f32[4,192,384]{2,1,0:T(8,128)S(1)}, u32[]{:S(2)}, u32[]{:S(2)}) collective-permute-start(f32[4,192,384]{2,1,0:T(8,128)} %bitcast.233), channel_id=1, source_target_pairs={{0,1},{1,0},{2,3},{3,2},{4,5},{5,4},{6,7},{7,6},{8,9},{9,8},{10,11... | collective-permute-start | bytes 3538952 | tf_op jit(solution)/shard_map/ppermute | solution.py:63
  314.0 3.7 collective-permute-start.13
  330.1 9.4 %collective-permute-start.15 = (f32[200,384]{1,0:T(8,128)S(1)}, f32[200,384]{1,0:T(8,128)S(1)}, u32[]{:S(2)}, u32[]{:S(2)}) collective-permute-start(f32[200,384]{1,0:T(8,128)S(1)} %pad_add_fusion.2), channel_id=1, source_target_pairs={{0,2},{1,3},{2,0},{3,1},{4,6},{5,7},{6,4},{7,5},{8,10},{9,11},{10,... | collective-permute-start | bytes 921608 | tf_op jit(solution)/shard_map/ppermute | solution.py:128
  343.6 116.1 %all-gather.21.cloned.1.call-start = ((), (), s32[]{:S(2)}) async-start(), calls=%async_computation.4 | async-start | bytes 1474560 | tf_op jit(solution)/shard_map/all_gather | solution.py:33
  372.6 9.9 %collective-permute-start.16 = (f32[4,192,384]{2,1,0:T(8,128)}, f32[4,192,384]{2,1,0:T(8,128)S(1)}, u32[]{:S(2)}, u32[]{:S(2)}) collective-permute-start(f32[4,192,384]{2,1,0:T(8,128)} %bitcast.237), channel_id=1, source_target_pairs={{0,1},{1,0},{2,3},{3,2},{4,5},{5,4},{6,7},{7,6},{8,9},{9,8},{10,11... | collective-permute-start | bytes 3538952 | tf_op jit(solution)/shard_map/ppermute | solution.py:63
  416.6 9.4 %collective-permute-start.20 = (f32[200,384]{1,0:T(8,128)S(1)}, f32[200,384]{1,0:T(8,128)S(1)}, u32[]{:S(2)}, u32[]{:S(2)}) collective-permute-start(f32[200,384]{1,0:T(8,128)S(1)} %pad_add_fusion.1), channel_id=1, source_target_pairs={{0,2},{1,3},{2,0},{3,1},{4,6},{5,7},{6,4},{7,5},{8,10},{9,11},{10,... | collective-permute-start | bytes 921608 | tf_op jit(solution)/shard_map/ppermute | solution.py:128
  430.2 114.8 %all-gather.23.cloned.1.call-start = ((), (), s32[]{:S(2)}) async-start(), calls=%async_computation.5 | async-start | bytes 1474560 | tf_op jit(solution)/shard_map/all_gather | solution.py:33
  459.7 9.9 %collective-permute-start.21 = (f32[4,192,384]{2,1,0:T(8,128)}, f32[4,192,384]{2,1,0:T(8,128)S(1)}, u32[]{:S(2)}, u32[]{:S(2)}) collective-permute-start(f32[4,192,384]{2,1,0:T(8,128)} %bitcast.239), channel_id=1, source_target_pairs={{0,1},{1,0},{2,3},{3,2},{4,5},{5,4},{6,7},{7,6},{8,9},{9,8},{10,11... | collective-permute-start | bytes 3538952 | tf_op jit(solution)/shard_map/ppermute | solution.py:63
  503.6 9.4 %collective-permute-start.25 = (f32[200,384]{1,0:T(8,128)S(1)}, f32[200,384]{1,0:T(8,128)S(1)}, u32[]{:S(2)}, u32[]{:S(2)}) collective-permute-start(f32[200,384]{1,0:T(8,128)S(1)} %pad_add_fusion), channel_id=1, source_target_pairs={{0,2},{1,3},{2,0},{3,1},{4,6},{5,7},{6,4},{7,5},{8,10},{9,11},{10,... | collective-permute-start | bytes 921608 | tf_op jit(solution)/shard_map/ppermute | solution.py:128
  545.0 9.9 %collective-permute-start.26 = (f32[4,192,384]{2,1,0:T(8,128)}, f32[4,192,384]{2,1,0:T(8,128)S(1)}, u32[]{:S(2)}, u32[]{:S(2)}) collective-permute-start(f32[4,192,384]{2,1,0:T(8,128)} %bitcast.235), channel_id=1, source_target_pairs={{0,1},{1,0},{2,3},{3,2},{4,5},{5,4},{6,7},{7,6},{8,9},{9,8},{10,11... | collective-permute-start | bytes 3538952 | tf_op jit(solution)/shard_map/ppermute | solution.py:63
  (49 other events, 203.1 us)
Sparse Core Ops, SparseCore 0:
  8.9 66.1 all-gather.12
  76.7 106.2 all-gather.14
  251.4 34.5 all-gather.16
  343.8 28.7 all-gather.18
  430.4 29.2 all-gather.20
  515.7 29.2 all-gather.22

commit v6 on v5

--- a/solution.py
+++ b/solution.py
@@ -57,12 +57,9 @@
     return x
 
 
-def halves(x, full, finish=lambda v: v):
-    core = lax.axis_index("inner") % 2
-    half = x.shape[1]
+def halves(x, finish=lambda v: v):
     other = lax.ppermute(x, "inner", [(i, i ^ 1) for i in range(lax.axis_size("inner"))])
-    full = lax.dynamic_update_slice_in_dim(full, finish(x), core * half, 1)
-    return lax.dynamic_update_slice_in_dim(full, finish(other), (1 - core) * half, 1)
+    return jnp.concatenate([finish(x), finish(other)], axis=1)
 
 
 def half_sum(x, size):
@@ -93,7 +90,7 @@
     if split:
         own_rows = lax.dynamic_slice_in_dim(grads, core * (count // 2), count // 2, 0)
         wide = site_gather(own_rows.astype(f32) * 2.0)
-        every_grad = halves(wide, jnp.zeros((sites,) + grads.shape, bf16), lambda v: (v * 0.5).astype(bf16))
+        every_grad = halves(wide, lambda v: (v * 0.5).astype(bf16))
     else:
         every_grad = (site_gather(grads.astype(f32) * 2.0) * 0.5).astype(bf16)
 
@@ -108,7 +105,12 @@
 
     left_w = jnp.dot(grads, site_weights[0], preferred_element_type=f32)
     mixed_w = mixed_of(left_w, token_pair(left_w))
-    rhs = image_of(site_gather(mixed_w))
+    mixed_w_all = site_gather(mixed_w)
+    if split:
+        half = count // 2
+        turned = jnp.concatenate([mixed_w_all[:, half:], mixed_w_all[:, :half]], axis=1)
+        mixed_w_all = jnp.where(core == 0, mixed_w_all, turned)
+    rhs = image_of(mixed_w_all)
 
     def square_sum(x):
         return inner_sum(jnp.sum(x * x), inner)
@@ -132,7 +134,7 @@
     def pair_spread(pair_part):
         if not split:
             return site_gather(pair_part)
-        return halves(site_gather(pair_part), jnp.zeros((sites, count, count), f32))
+        return halves(site_gather(pair_part))
 
     def apply_operator(pair_part, direction):
         pair_all = pair_spread(pair_part)

time: 594 us -> 577 us (0.971)
  waiting for transfers between devices: 229 us -> 282 us
  local copies, waits for them, and re-layouts: 69.3 us -> 18.5 us
  starting transfers between devices: 59.3 us -> 42.8 us
    ppermute x3, waiting for transfers between devices: 10.4 us -> 73 us  [line_gather(): left = lax.ppermute(left, 'site', [(i + 1, i) for i in range(sites - 1)])]
    dynamic_update_slice x10 -> x0, local copies, waits for them, and re-layouts: 42.6 us -> none  [the longest x5 22.5 us: halves(): lax.dynamic_update_slice_in_dim(full, finish(other), (1 - core) * half, 1)]
    ppermute x3, waiting for transfers between devices: 40 us -> 10.7 us  [line_gather(): right = lax.ppermute(right, 'site', [(i, i + 1) for i in range(sites - 1)])]
    all_gather x6, waiting for transfers between devices: 125 us -> 144 us  [site_gather(): lax.all_gather(lax.optimization_barrier(x), 'site')]
    ppermute x3, starting transfers between devices: 29.4 us -> 16.3 us  [line_gather(): right = lax.ppermute(right, 'site', [(i, i + 1) for i in range(sites - 1)])]
  transfers between devices with their start and end apart: 35 -> 35, of which waited for: 27 -> 25; matrix products, arithmetic and copies ran while one was open for 27% -> 19% of each run, Pallas kernels for 0% -> 0%
where the time goes in v6:
time: 577 us; the launch traced here: 572 us
  waiting for transfers between devices  282 us (49%)
  matrix products  143 us (25%)
  other arithmetic  56.5 us (10%)
  starting transfers between devices  42.8 us (7%)
  between operations  28.6 us (5%)
  local copies, waits for them, and re-layouts  18.5 us (3%)
    all_gather x6, waiting for transfers between devices, site_gather(): lax.all_gather(lax.optimization_barrier(x), 'site')  144 us
    dot_general x39, matrix products, one(): return jnp.einsum(spec, exact, part, preferred_element_type=f32)  114 us
    ppermute x3, waiting for transfers between devices, line_gather(): left = lax.ppermute(left, 'site', [(i + 1, i) for i in range(sites - 1)])  73 us
    dot_general x30, matrix products, one(): return jnp.einsum(spec, part, exact, preferred_element_type=f32)  27.4 us
    ppermute x4, waiting for transfers between devices, pair_sum(): lax.ppermute(part, 'inner', [(i, i ^ bit) for i in range(inner)])  25.8 us
    ppermute x10, waiting for transfers between devices, inner_sum(): x = x + lax.ppermute(x, 'inner', [(i, i ^ bit) for i in range(size)])  23.9 us
    ppermute x10, starting transfers between devices, inner_sum(): x = x + lax.ppermute(x, 'inner', [(i, i ^ bit) for i in range(size)])  16.7 us
    ppermute x3, starting transfers between devices, line_gather(): right = lax.ppermute(right, 'site', [(i, i + 1) for i in range(sites - 1)])  16.3 us
  transfers between devices with their start and end apart: 35, of which 25 were waited for; matrix products, arithmetic and copies ran while one was open for 19% of the time, Pallas kernels for 0%

profile of v6, /device:TPU:0, one launch (start us, length us, event | category | flops | bytes accessed | tf_op | source)
XLA Modules:
  0.0 572.1 jit_solution(1043211600204612041)
XLA Ops:
  17.2 13.6 %collective-permute-done.2 = f32[384,384]{1,0:T(8,128)S(1)} collective-permute-done((f32[384,384]{1,0:T(8,128)S(1)}, f32[384,384]{1,0:T(8,128)S(1)}, u32[]{:S(2)}, u32[]{:S(2)}) %collective-permute-start.2) | collective-permute-done | bytes 589856 | tf_op jit(solution)/shard_map/ppermute | solution.py:55
  33.2 42.0 %all-gather.13.cloned.1.call-done = f32[768,1024]{1,0:T(8,128)} async-done(((f32[192,1024]{1,0:T(8,128)}), f32[768,1024]{1,0:T(8,128)}) %all-gather.13.cloned.1.call-update) | async-done | bytes 3145744 | tf_op jit(solution)/shard_map/all_gather | solution.py:33
  76.5 5.5 collective-permute-start.6
  82.0 52.5 %collective-permute-done.7 = f32[384,640]{1,0:T(8,128)} collective-permute-done((f32[384,640]{1,0:T(8,128)S(1)}, f32[384,640]{1,0:T(8,128)}, u32[]{:S(2)}, u32[]{:S(2)}) %collective-permute-start.7) | collective-permute-done | bytes 983072 | tf_op jit(solution)/shard_map/ppermute | solution.py:43
  135.8 6.1 %collective-permute-start.8 = (f32[384,640]{1,0:T(8,128)}, f32[384,640]{1,0:T(8,128)}, u32[]{:S(2)}, u32[]{:S(2)}) collective-permute-start(f32[384,640]{1,0:T(8,128)} %collective-permute-done.6), channel_id=1, source_target_pairs={{0,4},{4,8},{8,12},{1,5},{5,9},{9,13},{2,6},{6,10},{10,14},{3,7},{... | collective-permute-start | bytes 2949128 | tf_op jit(solution)/shard_map/ppermute | solution.py:42
  144.3 42.8 %all-gather.15.cloned.1.call-done = f32[1536,640]{1,0:T(8,128)} async-done(((f32[384,640]{1,0:T(8,128)}), f32[1536,640]{1,0:T(8,128)}) %all-gather.15.cloned.1.call-update) | async-done | bytes 3932176 | tf_op jit(solution)/shard_map/all_gather | solution.py:33
  211.1 4.7 collective-permute-start.10
  231.8 10.7 %collective-permute-done.10 = f32[384,640]{1,0:T(8,128)S(1)} collective-permute-done((f32[384,640]{1,0:T(8,128)}, f32[384,640]{1,0:T(8,128)S(1)}, u32[]{:S(2)}, u32[]{:S(2)}) %collective-permute-start.10) | collective-permute-done | bytes 983072 | tf_op jit(solution)/shard_map/ppermute | solution.py:42
  244.7 20.5 %collective-permute-done.11 = f32[384,640]{1,0:T(8,128)} collective-permute-done((f32[384,640]{1,0:T(8,128)}, f32[384,640]{1,0:T(8,128)}, u32[]{:S(2)}, u32[]{:S(2)}) %collective-permute-start.11) | collective-permute-done | bytes 983072 | tf_op jit(solution)/shard_map/ppermute | solution.py:43
  276.3 5.7 fusion.96
  295.4 5.4 multiply_reduce_fusion.5
  320.2 8.8 %collective-permute-done.15 = f32[200,384]{1,0:T(8,128)S(1)} collective-permute-done((f32[200,384]{1,0:T(8,128)S(1)}, f32[200,384]{1,0:T(8,128)S(1)}, u32[]{:S(2)}, u32[]{:S(2)}) %collective-permute-start.15) | collective-permute-done | bytes 307232 | tf_op jit(solution)/shard_map/ppermute | solution.py:130
  337.7 4.6 fusion.70
  342.3 18.6 %all-gather.19.cloned.1.call-done = f32[768,384]{1,0:T(8,128)} async-done(((f32[192,384]{1,0:T(8,128)}), f32[768,384]{1,0:T(8,128)}) %all-gather.19.cloned.1.call-update) | async-done | bytes 1179664 | tf_op jit(solution)/shard_map/all_gather | solution.py:33
  361.0 5.6 fusion.78
  379.5 5.2 multiply_reduce_fusion.3
  405.6 7.8 %collective-permute-done.20 = f32[200,384]{1,0:T(8,128)S(1)} collective-permute-done((f32[200,384]{1,0:T(8,128)S(1)}, f32[200,384]{1,0:T(8,128)S(1)}, u32[]{:S(2)}, u32[]{:S(2)}) %collective-permute-start.20) | collective-permute-done | bytes 307232 | tf_op jit(solution)/shard_map/ppermute | solution.py:130
  422.3 4.6 fusion.66
  426.9 20.3 %all-gather.21.cloned.1.call-done = f32[768,384]{1,0:T(8,128)} async-done(((f32[192,384]{1,0:T(8,128)}), f32[768,384]{1,0:T(8,128)}) %all-gather.21.cloned.1.call-update) | async-done | bytes 1179664 | tf_op jit(solution)/shard_map/all_gather | solution.py:33
  447.3 5.8 %fusion.85 = f32[4,384,640]{2,1,0:T(8,128)S(1)} fusion(f32[1024,640]{1,0:T(8,128)} %copy-done.13, bf16[4,192,1024]{2,1,0:T(8,128)(2,1)} %copy-done.27, bf16[4,192,1024]{2,1,0:T(8,128)(2,1)} %copy-done.19), kind=kOutput, calls=%fused_computation.188 | convolution fusion | flops 2022178816 | bytes 9699328 | tf_op jit(solution)/shard_map/std,dc->stc/dot_general | solution.py:26
  466.0 5.1 multiply_reduce_fusion.1
  492.0 7.8 %collective-permute-done.25 = f32[200,384]{1,0:T(8,128)S(1)} collective-permute-done((f32[200,384]{1,0:T(8,128)S(1)}, f32[200,384]{1,0:T(8,128)S(1)}, u32[]{:S(2)}, u32[]{:S(2)}) %collective-permute-start.25) | collective-permute-done | bytes 307232 | tf_op jit(solution)/shard_map/ppermute | solution.py:130
  511.5 20.4 %all-gather.23.cloned.1.call-done = f32[768,384]{1,0:T(8,128)} async-done(((f32[192,384]{1,0:T(8,128)}), f32[768,384]{1,0:T(8,128)}) %all-gather.23.cloned.1.call-update) | async-done | bytes 1179664 | tf_op jit(solution)/shard_map/all_gather | solution.py:33
  531.9 5.3 fusion.92
  (265 shorter events, 214.3 us)
Async XLA Ops:
  6.5 68.6 %all-gather.13.cloned.1.call-start = ((), (), s32[]{:S(2)}) async-start(), calls=%async_computation | async-start | bytes 3932160 | tf_op jit(solution)/shard_map/all_gather | solution.py:33
  8.7 178.3 %all-gather.15.cloned.1.call-start = ((), (), s32[]{:S(2)}) async-start(), calls=%async_computation.1 | async-start | bytes 4915200 | tf_op jit(solution)/shard_map/all_gather | solution.py:33
  14.3 16.5 %collective-permute-start.2 = (f32[384,384]{1,0:T(8,128)S(1)}, f32[384,384]{1,0:T(8,128)S(1)}, u32[]{:S(2)}, u32[]{:S(2)}) collective-permute-start(f32[384,384]{1,0:T(8,128)S(1)} %add.366), channel_id=1, source_target_pairs={{0,2},{1,3},{2,0},{3,1},{4,6},{5,7},{6,4},{7,5},{8,10},{9,11},{10,... | collective-permute-start | bytes 1769480 | tf_op jit(solution)/shard_map/ppermute | solution.py:55
  33.2 243.1 %all-gather.17.cloned.1.call-start = ((), (), s32[]{:S(2)}) async-start(), calls=%async_computation.2 | async-start | bytes 1474560 | tf_op jit(solution)/shard_map/all_gather | solution.py:33
  75.2 115.5 %collective-permute-start = (f32[4,192,1024]{2,1,0:T(8,128)}, f32[4,192,1024]{2,1,0:T(8,128)}, u32[]{:S(2)}, u32[]{:S(2)}) collective-permute-start(f32[4,192,1024]{2,1,0:T(8,128)} %bitcast.206), channel_id=1, source_target_pairs={{0,1},{1,0},{2,3},{3,2},{4,5},{5,4},{6,7},{7,6},{8,9},{9,8},{10,11... | collective-permute-start | bytes 9437192 | tf_op jit(solution)/shard_map/ppermute | solution.py:61
  75.2 59.3 %collective-permute-start.7 = (f32[384,640]{1,0:T(8,128)S(1)}, f32[384,640]{1,0:T(8,128)}, u32[]{:S(2)}, u32[]{:S(2)}) collective-permute-start(f32[384,640]{1,0:T(8,128)S(1)} %convert_multiply_fusion), channel_id=1, source_target_pairs={{4,0},{8,4},{12,8},{5,1},{9,5},{13,9},{6,2},{10,6},{14,10},{7,3},{... | collective-permute-start | bytes 2949128 | tf_op jit(solution)/shard_map/ppermute | solution.py:43
  76.5 59.3 %collective-permute-start.6 = (f32[384,640]{1,0:T(8,128)S(1)}, f32[384,640]{1,0:T(8,128)}, u32[]{:S(2)}, u32[]{:S(2)}) collective-permute-start(f32[384,640]{1,0:T(8,128)S(1)} %convert_multiply_fusion), channel_id=1, source_target_pairs={{0,4},{4,8},{8,12},{1,5},{5,9},{9,13},{2,6},{6,10},{10,14},{3,7},{... | collective-permute-start | bytes 2949128 | tf_op jit(solution)/shard_map/ppermute | solution.py:42
  134.5 86.1 %collective-permute-start.9 = (f32[384,640]{1,0:T(8,128)}, f32[384,640]{1,0:T(8,128)}, u32[]{:S(2)}, u32[]{:S(2)}) collective-permute-start(f32[384,640]{1,0:T(8,128)} %collective-permute-done.7), channel_id=1, source_target_pairs={{4,0},{8,4},{12,8},{5,1},{9,5},{13,9},{6,2},{10,6},{14,10},{7,3},{... | collective-permute-start | bytes 2949128 | tf_op jit(solution)/shard_map/ppermute | solution.py:43
  135.8 75.3 %collective-permute-start.8 = (f32[384,640]{1,0:T(8,128)}, f32[384,640]{1,0:T(8,128)}, u32[]{:S(2)}, u32[]{:S(2)}) collective-permute-start(f32[384,640]{1,0:T(8,128)} %collective-permute-done.6), channel_id=1, source_target_pairs={{0,4},{4,8},{8,12},{1,5},{5,9},{9,13},{2,6},{6,10},{10,14},{3,7},{... | collective-permute-start | bytes 2949128 | tf_op jit(solution)/shard_map/ppermute | solution.py:42
  207.7 8.1 %collective-permute-start.3 = (f32[200,384]{1,0:T(8,128)S(1)}, f32[200,384]{1,0:T(8,128)S(1)}, u32[]{:S(2)}, u32[]{:S(2)}) collective-permute-start(f32[200,384]{1,0:T(8,128)S(1)} %concatenate.45), channel_id=1, source_target_pairs={{0,1},{1,0},{2,3},{3,2},{4,5},{5,4},{6,7},{7,6},{8,9},{9,8},{10,11... | collective-permute-start | bytes 921608 | tf_op jit(solution)/shard_map/ppermute | solution.py:127
  211.1 31.4 %collective-permute-start.10 = (f32[384,640]{1,0:T(8,128)}, f32[384,640]{1,0:T(8,128)S(1)}, u32[]{:S(2)}, u32[]{:S(2)}) collective-permute-start(f32[384,640]{1,0:T(8,128)} %collective-permute-done.8), channel_id=1, source_target_pairs={{0,4},{4,8},{8,12},{1,5},{5,9},{9,13},{2,6},{6,10},{10,14},{3,7},{... | collective-permute-start | bytes 2949128 | tf_op jit(solution)/shard_map/ppermute | solution.py:42
  216.5 9.3 %collective-permute-start.4 = (f32[200,384]{1,0:T(8,128)S(1)}, f32[200,384]{1,0:T(8,128)S(1)}, u32[]{:S(2)}, u32[]{:S(2)}) collective-permute-start(f32[200,384]{1,0:T(8,128)S(1)} %pad_add_fusion.3), channel_id=1, source_target_pairs={{0,2},{1,3},{2,0},{3,1},{4,6},{5,7},{6,4},{7,5},{8,10},{9,11},{10,... | collective-permute-start | bytes 921608 | tf_op jit(solution)/shard_map/ppermute | solution.py:130
  220.6 44.6 %collective-permute-start.11 = (f32[384,640]{1,0:T(8,128)}, f32[384,640]{1,0:T(8,128)}, u32[]{:S(2)}, u32[]{:S(2)}) collective-permute-start(f32[384,640]{1,0:T(8,128)} %collective-permute-done.9), channel_id=1, source_target_pairs={{4,0},{8,4},{12,8},{5,1},{9,5},{13,9},{6,2},{10,6},{14,10},{7,3},{... | collective-permute-start | bytes 2949128 | tf_op jit(solution)/shard_map/ppermute | solution.py:43
  226.6 134.3 %all-gather.19.cloned.1.call-start = ((), (), s32[]{:S(2)}) async-start(), calls=%async_computation.3 | async-start | bytes 1474560 | tf_op jit(solution)/shard_map/all_gather | solution.py:33
  276.2 9.1 %collective-permute-start.5 = (f32[4,192,384]{2,1,0:T(8,128)}, f32[4,192,384]{2,1,0:T(8,128)S(1)}, u32[]{:S(2)}, u32[]{:S(2)}) collective-permute-start(f32[4,192,384]{2,1,0:T(8,128)} %bitcast.208), channel_id=1, source_target_pairs={{0,1},{1,0},{2,3},{3,2},{4,5},{5,4},{6,7},{7,6},{8,9},{9,8},{10,11... | collective-permute-start | bytes 3538952 | tf_op jit(solution)/shard_map/ppermute | solution.py:61
  303.4 3.7 collective-permute-start.13
  319.6 9.4 %collective-permute-start.15 = (f32[200,384]{1,0:T(8,128)S(1)}, f32[200,384]{1,0:T(8,128)S(1)}, u32[]{:S(2)}, u32[]{:S(2)}) collective-permute-start(f32[200,384]{1,0:T(8,128)S(1)} %pad_add_fusion.2), channel_id=1, source_target_pairs={{0,2},{1,3},{2,0},{3,1},{4,6},{5,7},{6,4},{7,5},{8,10},{9,11},{10,... | collective-permute-start | bytes 921608 | tf_op jit(solution)/shard_map/ppermute | solution.py:130
  333.1 114.1 %all-gather.21.cloned.1.call-start = ((), (), s32[]{:S(2)}) async-start(), calls=%async_computation.4 | async-start | bytes 1474560 | tf_op jit(solution)/shard_map/all_gather | solution.py:33
  361.0 8.5 %collective-permute-start.16 = (f32[4,192,384]{2,1,0:T(8,128)}, f32[4,192,384]{2,1,0:T(8,128)S(1)}, u32[]{:S(2)}, u32[]{:S(2)}) collective-permute-start(f32[4,192,384]{2,1,0:T(8,128)} %bitcast.212), channel_id=1, source_target_pairs={{0,1},{1,0},{2,3},{3,2},{4,5},{5,4},{6,7},{7,6},{8,9},{9,8},{10,11... | collective-permute-start | bytes 3538952 | tf_op jit(solution)/shard_map/ppermute | solution.py:61
  404.1 9.4 %collective-permute-start.20 = (f32[200,384]{1,0:T(8,128)S(1)}, f32[200,384]{1,0:T(8,128)S(1)}, u32[]{:S(2)}, u32[]{:S(2)}) collective-permute-start(f32[200,384]{1,0:T(8,128)S(1)} %pad_add_fusion.1), channel_id=1, source_target_pairs={{0,2},{1,3},{2,0},{3,1},{4,6},{5,7},{6,4},{7,5},{8,10},{9,11},{10,... | collective-permute-start | bytes 921608 | tf_op jit(solution)/shard_map/ppermute | solution.py:130
  417.8 114.2 %all-gather.23.cloned.1.call-start = ((), (), s32[]{:S(2)}) async-start(), calls=%async_computation.5 | async-start | bytes 1474560 | tf_op jit(solution)/shard_map/all_gather | solution.py:33
  447.2 8.7 %collective-permute-start.21 = (f32[4,192,384]{2,1,0:T(8,128)}, f32[4,192,384]{2,1,0:T(8,128)S(1)}, u32[]{:S(2)}, u32[]{:S(2)}) collective-permute-start(f32[4,192,384]{2,1,0:T(8,128)} %bitcast.214), channel_id=1, source_target_pairs={{0,1},{1,0},{2,3},{3,2},{4,5},{5,4},{6,7},{7,6},{8,9},{9,8},{10,11... | collective-permute-start | bytes 3538952 | tf_op jit(solution)/shard_map/ppermute | solution.py:61
  490.4 9.4 %collective-permute-start.25 = (f32[200,384]{1,0:T(8,128)S(1)}, f32[200,384]{1,0:T(8,128)S(1)}, u32[]{:S(2)}, u32[]{:S(2)}) collective-permute-start(f32[200,384]{1,0:T(8,128)S(1)} %pad_add_fusion), channel_id=1, source_target_pairs={{0,2},{1,3},{2,0},{3,1},{4,6},{5,7},{6,4},{7,5},{8,10},{9,11},{10,... | collective-permute-start | bytes 921608 | tf_op jit(solution)/shard_map/ppermute | solution.py:130
  531.9 8.1 %collective-permute-start.26 = (f32[4,192,384]{2,1,0:T(8,128)}, f32[4,192,384]{2,1,0:T(8,128)S(1)}, u32[]{:S(2)}, u32[]{:S(2)}) collective-permute-start(f32[4,192,384]{2,1,0:T(8,128)} %bitcast.210), channel_id=1, source_target_pairs={{0,1},{1,0},{2,3},{3,2},{4,5},{5,4},{6,7},{7,6},{8,9},{9,8},{10,11... | collective-permute-start | bytes 3538952 | tf_op jit(solution)/shard_map/ppermute | solution.py:61
  (57 other events, 297.1 us)
Sparse Core Ops, SparseCore 0:
  8.9 66.1 all-gather.12
  76.7 110.2 all-gather.14
  226.7 38.1 all-gather.16
  333.2 27.6 all-gather.18
  417.9 29.2 all-gather.20
  502.6 29.2 all-gather.22

commit v7 on v6

--- a/solution.py
+++ b/solution.py
@@ -136,10 +136,8 @@
             return site_gather(pair_part)
         return halves(site_gather(pair_part))
 
-    def apply_operator(pair_part, direction):
+    def apply_operator(pair_part, left_all):
         pair_all = pair_spread(pair_part)
-        left_all = exact_dot("std,dc->stc", every_grad, direction)
-        pair_all, left_all = lax.optimization_barrier((pair_all, left_all))
         mixed_all = (
             exact_dot("stu,suc->stc", every_input, pair_all, exact_first=False) / (count * count)
             + damping * left_all / count
@@ -150,14 +148,17 @@
     residual = rhs
     direction = rhs
     pair_part, norm_now = pair_sum(exact_dot("td,dc->tc", grads, rhs), jnp.sum(rhs * rhs))
+    left_all = exact_dot("std,dc->stc", every_grad, rhs)
     for count_step in range(ITERS):
         if count_step:
+            left_r = exact_dot("std,dc->stc", every_grad, residual)
             pair_r, norm_next = pair_sum(exact_dot("td,dc->tc", grads, residual), jnp.sum(residual * residual))
             beta = norm_next / norm_now
             pair_part = pair_r + beta * pair_part
+            left_all = left_r + beta * left_all
             direction = residual + beta * direction
             norm_now = norm_next
-        image = apply_operator(pair_part, direction)
+        image = apply_operator(pair_part, left_all)
         alpha = norm_now / inner_sum(jnp.sum(direction * image), inner)
         merged = merged + alpha * direction
         residual = residual - alpha * image

time: 577 us -> 598 us (1.036)
  matrix products: 143 us -> 162 us
  starting transfers between devices: 42.8 us -> 52.1 us
  other arithmetic: 56.5 us -> 50 us
    ppermute x3, waiting for transfers between devices: 73 us -> 27.8 us  [line_gather(): left = lax.ppermute(left, 'site', [(i + 1, i) for i in range(sites - 1)])]
    ppermute x3, waiting for transfers between devices: 10.7 us -> 41.9 us  [line_gather(): right = lax.ppermute(right, 'site', [(i, i + 1) for i in range(sites - 1)])]
    dot_general x39, matrix products: 114 us -> 129 us  [one(): return jnp.einsum(spec, exact, part, preferred_element_type=f32)]
    all_gather x6, waiting for transfers between devices: 144 us -> 158 us  [site_gather(): lax.all_gather(lax.optimization_barrier(x), 'site')]
    ppermute x3, starting transfers between devices: 16.3 us -> 28.5 us  [line_gather(): right = lax.ppermute(right, 'site', [(i, i + 1) for i in range(sites - 1)])]
    add x3 -> x1, other arithmetic: 8.81 us -> 1.78 us  [per_device(): direction = residual + beta * direction]
  transfers between devices with their start and end apart: 35 -> 35, of which waited for: 25 -> 26; matrix products, arithmetic and copies ran while one was open for 19% -> 18% of each run, Pallas kernels for 0% -> 0%
where the time goes in v7:
time: 598 us; the launch traced here: 594 us
  waiting for transfers between devices  284 us (47%)
  matrix products  162 us (27%)
  starting transfers between devices  52.1 us (9%)
  other arithmetic  50 us (8%)
  between operations  28.9 us (5%)
  local copies, waits for them, and re-layouts  17 us (3%)
    all_gather x6, waiting for transfers between devices, site_gather(): lax.all_gather(lax.optimization_barrier(x), 'site')  158 us
    dot_general x39, matrix products, one(): return jnp.einsum(spec, exact, part, preferred_element_type=f32)  129 us
    ppermute x3, waiting for transfers between devices, line_gather(): right = lax.ppermute(right, 'site', [(i, i + 1) for i in range(sites - 1)])  41.9 us
    dot_general x30, matrix products, one(): return jnp.einsum(spec, part, exact, preferred_element_type=f32)  30.7 us
    ppermute x3, starting transfers between devices, line_gather(): right = lax.ppermute(right, 'site', [(i, i + 1) for i in range(sites - 1)])  28.5 us
    ppermute x3, waiting for transfers between devices, line_gather(): left = lax.ppermute(left, 'site', [(i + 1, i) for i in range(sites - 1)])  27.8 us
    ppermute x4, waiting for transfers between devices, pair_sum(): lax.ppermute(part, 'inner', [(i, i ^ bit) for i in range(inner)])  26.2 us
    ppermute x10, waiting for transfers between devices, inner_sum(): x = x + lax.ppermute(x, 'inner', [(i, i ^ bit) for i in range(size)])  24.6 us
  transfers between devices with their start and end apart: 35, of which 26 were waited for; matrix products, arithmetic and copies ran while one was open for 18% of the time, Pallas kernels for 0%

profile of v7, /device:TPU:0, one launch (start us, length us, event | category | flops | bytes accessed | tf_op | source)
XLA Modules:
  0.0 593.7 jit_solution(10482660239240701776)
XLA Ops:
  17.2 13.6 %collective-permute-done.2 = f32[384,384]{1,0:T(8,128)S(1)} collective-permute-done((f32[384,384]{1,0:T(8,128)S(1)}, f32[384,384]{1,0:T(8,128)S(1)}, u32[]{:S(2)}, u32[]{:S(2)}) %collective-permute-start.2) | collective-permute-done | bytes 589856 | tf_op jit(solution)/shard_map/ppermute | solution.py:55
  33.2 42.0 %all-gather.13.cloned.1.call-done = f32[768,1024]{1,0:T(8,128)} async-done(((f32[192,1024]{1,0:T(8,128)}), f32[768,1024]{1,0:T(8,128)}) %all-gather.13.cloned.1.call-update) | async-done | bytes 3145744 | tf_op jit(solution)/shard_map/all_gather | solution.py:33
  78.8 34.1 %collective-permute-done.6 = f32[384,640]{1,0:T(8,128)} collective-permute-done((f32[384,640]{1,0:T(8,128)S(1)}, f32[384,640]{1,0:T(8,128)}, u32[]{:S(2)}, u32[]{:S(2)}) %collective-permute-start.6) | collective-permute-done | bytes 983072 | tf_op jit(solution)/shard_map/ppermute | solution.py:42
  112.9 20.8 %collective-permute-start.8 = (f32[384,640]{1,0:T(8,128)}, f32[384,640]{1,0:T(8,128)}, u32[]{:S(2)}, u32[]{:S(2)}) collective-permute-start(f32[384,640]{1,0:T(8,128)} %collective-permute-done.6), channel_id=1, source_target_pairs={{0,4},{4,8},{8,12},{1,5},{5,9},{9,13},{2,6},{6,10},{10,14},{3,7},{... | collective-permute-start | bytes 2949128 | tf_op jit(solution)/shard_map/ppermute | solution.py:42
  141.1 41.9 %all-gather.15.cloned.1.call-done = f32[1536,640]{1,0:T(8,128)} async-done(((f32[384,640]{1,0:T(8,128)}), f32[1536,640]{1,0:T(8,128)}) %all-gather.15.cloned.1.call-update) | async-done | bytes 3932176 | tf_op jit(solution)/shard_map/all_gather | solution.py:33
  207.5 5.4 collective-permute-start.10
  228.9 7.8 %collective-permute-done.10 = f32[384,640]{1,0:T(8,128)S(1)} collective-permute-done((f32[384,640]{1,0:T(8,128)}, f32[384,640]{1,0:T(8,128)S(1)}, u32[]{:S(2)}, u32[]{:S(2)}) %collective-permute-start.10) | collective-permute-done | bytes 983072 | tf_op jit(solution)/shard_map/ppermute | solution.py:42
  239.0 24.3 %collective-permute-done.11 = f32[384,640]{1,0:T(8,128)} collective-permute-done((f32[384,640]{1,0:T(8,128)}, f32[384,640]{1,0:T(8,128)}, u32[]{:S(2)}, u32[]{:S(2)}) %collective-permute-start.11) | collective-permute-done | bytes 983072 | tf_op jit(solution)/shard_map/ppermute | solution.py:43
  274.4 5.5 fusion.75
  317.6 9.3 %collective-permute-done.15 = f32[200,384]{1,0:T(8,128)S(1)} collective-permute-done((f32[200,384]{1,0:T(8,128)S(1)}, f32[200,384]{1,0:T(8,128)S(1)}, u32[]{:S(2)}, u32[]{:S(2)}) %collective-permute-start.15) | collective-permute-done | bytes 307232 | tf_op jit(solution)/shard_map/ppermute | solution.py:130
  331.4 7.3 %fusion.68 = f32[4,384,640]{2,1,0:T(8,128)} fusion(f32[1024,640]{1,0:T(8,128)} %copy-done.7, bf16[4,192,1024]{2,1,0:T(8,128)(2,1)} %copy-done.19, bf16[4,192,1024]{2,1,0:T(8,128)(2,1)} %copy-done.13), kind=kOutput, calls=%fused_computation.167 | convolution fusion | flops 2022834176 | bytes 9699328 | tf_op jit(solution)/shard_map/std,dc->stc/dot_general | solution.py:26
  338.7 22.2 %all-gather.19.cloned.1.call-done = f32[768,384]{1,0:T(8,128)} async-done(((f32[192,384]{1,0:T(8,128)}), f32[768,384]{1,0:T(8,128)}) %all-gather.19.cloned.1.call-update) | async-done | bytes 1179664 | tf_op jit(solution)/shard_map/all_gather | solution.py:33
  361.0 5.7 fusion.70
  380.3 5.7 multiply_reduce_fusion.3
  406.0 7.9 %collective-permute-done.20 = f32[200,384]{1,0:T(8,128)S(1)} collective-permute-done((f32[200,384]{1,0:T(8,128)S(1)}, f32[200,384]{1,0:T(8,128)S(1)}, u32[]{:S(2)}, u32[]{:S(2)}) %collective-permute-start.20) | collective-permute-done | bytes 307232 | tf_op jit(solution)/shard_map/ppermute | solution.py:130
  418.3 7.3 %fusion.63 = f32[4,384,640]{2,1,0:T(8,128)} fusion(f32[1024,640]{1,0:T(8,128)} %copy-done.5, bf16[4,192,1024]{2,1,0:T(8,128)(2,1)} %copy-done.19, bf16[4,192,1024]{2,1,0:T(8,128)(2,1)} %copy-done.13), kind=kOutput, calls=%fused_computation.162 | convolution fusion | flops 2022834176 | bytes 9699328 | tf_op jit(solution)/shard_map/std,dc->stc/dot_general | solution.py:26
  425.6 22.4 %all-gather.21.cloned.1.call-done = f32[768,384]{1,0:T(8,128)} async-done(((f32[192,384]{1,0:T(8,128)}), f32[768,384]{1,0:T(8,128)}) %all-gather.21.cloned.1.call-update) | async-done | bytes 1179664 | tf_op jit(solution)/shard_map/all_gather | solution.py:33
  448.0 5.5 fusion.65
  467.3 6.0 %multiply_reduce_fusion.1 = (f32[]{:T(128)}, f32[1024,640]{1,0:T(8,128)}, f32[1024,640]{1,0:T(8,128)}) fusion(f32[1024,640]{1,0:T(8,128)S(1)} %copy-done.6, f32[1024,640]{1,0:T(8,128)S(1)} %copy-done.46, f32[]{:T(128)S(6)} %div.68, f32[4,384,640]{2,1,0:T(8,128)S(1)} %multiply_add_fusion.1, bf16[4,192,1024]{2,1,0:T(8,128)(2,1)S(1)} %copy-done.23, ...), kind=kOutput, calls=%fused_computation.88 | convolution fusion | flops 2028404736 | bytes 22806536 | tf_op jit(solution)/shard_map/std,stc->dc/dot_general | solution.py:26
  493.5 7.8 %collective-permute-done.25 = f32[200,384]{1,0:T(8,128)S(1)} collective-permute-done((f32[200,384]{1,0:T(8,128)S(1)}, f32[200,384]{1,0:T(8,128)S(1)}, u32[]{:S(2)}, u32[]{:S(2)}) %collective-permute-start.25) | collective-permute-done | bytes 307232 | tf_op jit(solution)/shard_map/ppermute | solution.py:130
  505.8 29.7 %all-gather.23.cloned.1.call-done = f32[768,384]{1,0:T(8,128)} async-done(((f32[192,384]{1,0:T(8,128)}), f32[768,384]{1,0:T(8,128)}) %all-gather.23.cloned.1.call-update) | async-done | bytes 1179664 | tf_op jit(solution)/shard_map/all_gather | solution.py:33
  535.5 6.9 %fusion.60 = f32[4,384,640]{2,1,0:T(8,128)} fusion(f32[1024,640]{1,0:T(8,128)} %copy-done.3, bf16[4,192,1024]{2,1,0:T(8,128)(2,1)} %copy-done.19, bf16[4,192,1024]{2,1,0:T(8,128)(2,1)S(1)} %copy-done.18), kind=kOutput, calls=%fused_computation.159 | convolution fusion | flops 2022178816 | bytes 9699328 | tf_op jit(solution)/shard_map/std,dc->stc/dot_general | solution.py:26
  556.7 7.8 %multiply_add_fusion = f32[4,384,640]{2,1,0:T(8,128)S(1)} fusion(f32[4,384,640]{2,1,0:T(8,128)S(1)} %copy-done.10, f32[4,384,640]{2,1,0:T(8,128)} %fusion.60, f32[4,384,640]{2,1,0:T(8,128)} %fusion.58, f32[4,384,640]{2,1,0:T(8,128)} %fusion.93, f32[4,384,640]{2,1,0:T(8,128)} %fusion.94, f32[4,384,640]{2,1,0:T(8,128)S(1)} %fusion.82, f32[]{:T(128)S(6)} %div.72, ...), kind=kOutput, calls=%fused_computation.26 | convolution fusion | flops 2029715456 | bytes 33292292 | tf_op jit(solution)/shard_map/std,dc->stc/dot_general | solution.py:26
  570.1 6.1 %fusion.11 = f32[]{:T(128)} fusion(f32[1024,640]{1,0:T(8,128)S(1)} %copy-done.38, f32[1024,640,1]{1,0,2:T(8,128)S(1)} %fusion.39, f32[1024,640,1]{1,0,2:T(8,128)S(1)} %fusion.38, f32[4,384,640]{2,1,0:T(8,128)} %copy-done.39, bf16[4,192,1024]{2,1,0:T(8,128)(2,1)S(1)} %copy-done.24, bf16[4,192,1024]{2,1,0:T(8,128)(2,1)S(1)} %copy-done.18), kind=kOutput, calls=%fused_computation.76 | convolution fusion | flops 2027094016 | bytes 14942212 | tf_op jit(solution)/shard_map/std,stc->dc/dot_general | solution.py:26
  (263 shorter events, 211.7 us)
Async XLA Ops:
  6.5 68.6 %all-gather.13.cloned.1.call-start = ((), (), s32[]{:S(2)}) async-start(), calls=%async_computation | async-start | bytes 3932160 | tf_op jit(solution)/shard_map/all_gather | solution.py:33
  8.7 174.3 %all-gather.15.cloned.1.call-start = ((), (), s32[]{:S(2)}) async-start(), calls=%async_computation.1 | async-start | bytes 4915200 | tf_op jit(solution)/shard_map/all_gather | solution.py:33
  14.3 16.6 %collective-permute-start.2 = (f32[384,384]{1,0:T(8,128)S(1)}, f32[384,384]{1,0:T(8,128)S(1)}, u32[]{:S(2)}, u32[]{:S(2)}) collective-permute-start(f32[384,384]{1,0:T(8,128)S(1)} %add.375), channel_id=1, source_target_pairs={{0,2},{1,3},{2,0},{3,1},{4,6},{5,7},{6,4},{7,5},{8,10},{9,11},{10,... | collective-permute-start | bytes 1769480 | tf_op jit(solution)/shard_map/ppermute | solution.py:55
  33.1 241.2 %all-gather.17.cloned.1.call-start = ((), (), s32[]{:S(2)}) async-start(), calls=%async_computation.2 | async-start | bytes 1474560 | tf_op jit(solution)/shard_map/all_gather | solution.py:33
  75.2 111.6 %collective-permute-start = (f32[4,192,1024]{2,1,0:T(8,128)}, f32[4,192,1024]{2,1,0:T(8,128)}, u32[]{:S(2)}, u32[]{:S(2)}) collective-permute-start(f32[4,192,1024]{2,1,0:T(8,128)} %bitcast.222), channel_id=1, source_target_pairs={{0,1},{1,0},{2,3},{3,2},{4,5},{5,4},{6,7},{7,6},{8,9},{9,8},{10,11... | collective-permute-start | bytes 9437192 | tf_op jit(solution)/shard_map/ppermute | solution.py:61
  75.2 37.6 %collective-permute-start.6 = (f32[384,640]{1,0:T(8,128)S(1)}, f32[384,640]{1,0:T(8,128)}, u32[]{:S(2)}, u32[]{:S(2)}) collective-permute-start(f32[384,640]{1,0:T(8,128)S(1)} %convert_multiply_fusion), channel_id=1, source_target_pairs={{0,4},{4,8},{8,12},{1,5},{5,9},{9,13},{2,6},{6,10},{10,14},{3,7},{... | collective-permute-start | bytes 2949128 | tf_op jit(solution)/shard_map/ppermute | solution.py:42
  77.5 59.7 %collective-permute-start.7 = (f32[384,640]{1,0:T(8,128)S(1)}, f32[384,640]{1,0:T(8,128)}, u32[]{:S(2)}, u32[]{:S(2)}) collective-permute-start(f32[384,640]{1,0:T(8,128)S(1)} %convert_multiply_fusion), channel_id=1, source_target_pairs={{4,0},{8,4},{12,8},{5,1},{9,5},{13,9},{6,2},{10,6},{14,10},{7,3},{... | collective-permute-start | bytes 2949128 | tf_op jit(solution)/shard_map/ppermute | solution.py:43
  112.9 94.6 %collective-permute-start.8 = (f32[384,640]{1,0:T(8,128)}, f32[384,640]{1,0:T(8,128)}, u32[]{:S(2)}, u32[]{:S(2)}) collective-permute-start(f32[384,640]{1,0:T(8,128)} %collective-permute-done.6), channel_id=1, source_target_pairs={{0,4},{4,8},{8,12},{1,5},{5,9},{9,13},{2,6},{6,10},{10,14},{3,7},{... | collective-permute-start | bytes 2949128 | tf_op jit(solution)/shard_map/ppermute | solution.py:42
  137.2 80.7 %collective-permute-start.9 = (f32[384,640]{1,0:T(8,128)}, f32[384,640]{1,0:T(8,128)}, u32[]{:S(2)}, u32[]{:S(2)}) collective-permute-start(f32[384,640]{1,0:T(8,128)} %collective-permute-done.7), channel_id=1, source_target_pairs={{4,0},{8,4},{12,8},{5,1},{9,5},{13,9},{6,2},{10,6},{14,10},{7,3},{... | collective-permute-start | bytes 2949128 | tf_op jit(solution)/shard_map/ppermute | solution.py:43
  204.1 8.8 %collective-permute-start.3 = (f32[200,384]{1,0:T(8,128)S(1)}, f32[200,384]{1,0:T(8,128)S(1)}, u32[]{:S(2)}, u32[]{:S(2)}) collective-permute-start(f32[200,384]{1,0:T(8,128)S(1)} %concatenate.45), channel_id=1, source_target_pairs={{0,1},{1,0},{2,3},{3,2},{4,5},{5,4},{6,7},{7,6},{8,9},{9,8},{10,11... | collective-permute-start | bytes 921608 | tf_op jit(solution)/shard_map/ppermute | solution.py:127
  207.5 29.2 %collective-permute-start.10 = (f32[384,640]{1,0:T(8,128)}, f32[384,640]{1,0:T(8,128)S(1)}, u32[]{:S(2)}, u32[]{:S(2)}) collective-permute-start(f32[384,640]{1,0:T(8,128)} %collective-permute-done.8), channel_id=1, source_target_pairs={{0,4},{4,8},{8,12},{1,5},{5,9},{9,13},{2,6},{6,10},{10,14},{3,7},{... | collective-permute-start | bytes 2949128 | tf_op jit(solution)/shard_map/ppermute | solution.py:42
  213.6 9.3 %collective-permute-start.4 = (f32[200,384]{1,0:T(8,128)S(1)}, f32[200,384]{1,0:T(8,128)S(1)}, u32[]{:S(2)}, u32[]{:S(2)}) collective-permute-start(f32[200,384]{1,0:T(8,128)S(1)} %pad_add_fusion.3), channel_id=1, source_target_pairs={{0,2},{1,3},{2,0},{3,1},{4,6},{5,7},{6,4},{7,5},{8,10},{9,11},{10,... | collective-permute-start | bytes 921608 | tf_op jit(solution)/shard_map/ppermute | solution.py:130
  217.8 45.4 %collective-permute-start.11 = (f32[384,640]{1,0:T(8,128)}, f32[384,640]{1,0:T(8,128)}, u32[]{:S(2)}, u32[]{:S(2)}) collective-permute-start(f32[384,640]{1,0:T(8,128)} %collective-permute-done.9), channel_id=1, source_target_pairs={{4,0},{8,4},{12,8},{5,1},{9,5},{13,9},{6,2},{10,6},{14,10},{7,3},{... | collective-permute-start | bytes 2949128 | tf_op jit(solution)/shard_map/ppermute | solution.py:43
  223.7 137.2 %all-gather.19.cloned.1.call-start = ((), (), s32[]{:S(2)}) async-start(), calls=%async_computation.3 | async-start | bytes 1474560 | tf_op jit(solution)/shard_map/all_gather | solution.py:33
  274.3 9.0 %collective-permute-start.5 = (f32[4,192,384]{2,1,0:T(8,128)}, f32[4,192,384]{2,1,0:T(8,128)S(1)}, u32[]{:S(2)}, u32[]{:S(2)}) collective-permute-start(f32[4,192,384]{2,1,0:T(8,128)} %bitcast.206), channel_id=1, source_target_pairs={{0,1},{1,0},{2,3},{3,2},{4,5},{5,4},{6,7},{7,6},{8,9},{9,8},{10,11... | collective-permute-start | bytes 3538952 | tf_op jit(solution)/shard_map/ppermute | solution.py:61
  301.3 3.7 collective-permute-start.13
  317.6 9.4 %collective-permute-start.15 = (f32[200,384]{1,0:T(8,128)S(1)}, f32[200,384]{1,0:T(8,128)S(1)}, u32[]{:S(2)}, u32[]{:S(2)}) collective-permute-start(f32[200,384]{1,0:T(8,128)S(1)} %pad_add_fusion.2), channel_id=1, source_target_pairs={{0,2},{1,3},{2,0},{3,1},{4,6},{5,7},{6,4},{7,5},{8,10},{9,11},{10,... | collective-permute-start | bytes 921608 | tf_op jit(solution)/shard_map/ppermute | solution.py:130
  331.3 116.6 %all-gather.21.cloned.1.call-start = ((), (), s32[]{:S(2)}) async-start(), calls=%async_computation.4 | async-start | bytes 1474560 | tf_op jit(solution)/shard_map/all_gather | solution.py:33
  360.9 9.6 %collective-permute-start.16 = (f32[4,192,384]{2,1,0:T(8,128)}, f32[4,192,384]{2,1,0:T(8,128)S(1)}, u32[]{:S(2)}, u32[]{:S(2)}) collective-permute-start(f32[4,192,384]{2,1,0:T(8,128)} %bitcast.210), channel_id=1, source_target_pairs={{0,1},{1,0},{2,3},{3,2},{4,5},{5,4},{6,7},{7,6},{8,9},{9,8},{10,11... | collective-permute-start | bytes 3538952 | tf_op jit(solution)/shard_map/ppermute | solution.py:61
  404.5 9.4 %collective-permute-start.20 = (f32[200,384]{1,0:T(8,128)S(1)}, f32[200,384]{1,0:T(8,128)S(1)}, u32[]{:S(2)}, u32[]{:S(2)}) collective-permute-start(f32[200,384]{1,0:T(8,128)S(1)} %pad_add_fusion.1), channel_id=1, source_target_pairs={{0,2},{1,3},{2,0},{3,1},{4,6},{5,7},{6,4},{7,5},{8,10},{9,11},{10,... | collective-permute-start | bytes 921608 | tf_op jit(solution)/shard_map/ppermute | solution.py:130
  418.3 117.3 %all-gather.23.cloned.1.call-start = ((), (), s32[]{:S(2)}) async-start(), calls=%async_computation.5 | async-start | bytes 1474560 | tf_op jit(solution)/shard_map/all_gather | solution.py:33
  448.0 9.6 %collective-permute-start.21 = (f32[4,192,384]{2,1,0:T(8,128)}, f32[4,192,384]{2,1,0:T(8,128)S(1)}, u32[]{:S(2)}, u32[]{:S(2)}) collective-permute-start(f32[4,192,384]{2,1,0:T(8,128)} %bitcast.214), channel_id=1, source_target_pairs={{0,1},{1,0},{2,3},{3,2},{4,5},{5,4},{6,7},{7,6},{8,9},{9,8},{10,11... | collective-permute-start | bytes 3538952 | tf_op jit(solution)/shard_map/ppermute | solution.py:61
  492.0 9.4 %collective-permute-start.25 = (f32[200,384]{1,0:T(8,128)S(1)}, f32[200,384]{1,0:T(8,128)S(1)}, u32[]{:S(2)}, u32[]{:S(2)}) collective-permute-start(f32[200,384]{1,0:T(8,128)S(1)} %pad_add_fusion), channel_id=1, source_target_pairs={{0,2},{1,3},{2,0},{3,1},{4,6},{5,7},{6,4},{7,5},{8,10},{9,11},{10,... | collective-permute-start | bytes 921608 | tf_op jit(solution)/shard_map/ppermute | solution.py:130
  535.5 13.4 %collective-permute-start.26 = (f32[4,192,384]{2,1,0:T(8,128)}, f32[4,192,384]{2,1,0:T(8,128)S(1)}, u32[]{:S(2)}, u32[]{:S(2)}) collective-permute-start(f32[4,192,384]{2,1,0:T(8,128)} %bitcast.218), channel_id=1, source_target_pairs={{0,1},{1,0},{2,3},{3,2},{4,5},{5,4},{6,7},{7,6},{8,9},{9,8},{10,11... | collective-permute-start | bytes 3538952 | tf_op jit(solution)/shard_map/ppermute | solution.py:61
  (59 other events, 331.9 us)
Sparse Core Ops, SparseCore 0:
  8.9 66.1 all-gather.12
  76.7 106.2 all-gather.14
  223.9 41.2 all-gather.16
  331.5 29.4 all-gather.18
  418.4 29.5 all-gather.20
  505.9 29.5 all-gather.22

commit v8 on v6

--- a/solution.py
+++ b/solution.py
@@ -144,7 +144,7 @@
             exact_dot("stu,suc->stc", every_input, pair_all, exact_first=False) / (count * count)
             + damping * left_all / count
         )
-        return image_of(mixed_all)
+        return image_of(mixed_all), inner_sum(jnp.sum(left_all * mixed_all), inner)
 
     merged = jnp.zeros_like(rhs)
     residual = rhs
@@ -157,8 +157,8 @@
             pair_part = pair_r + beta * pair_part
             direction = residual + beta * direction
             norm_now = norm_next
-        image = apply_operator(pair_part, direction)
-        alpha = norm_now / inner_sum(jnp.sum(direction * image), inner)
+        image, curvature = apply_operator(pair_part, direction)
+        alpha = norm_now / curvature
         merged = merged + alpha * direction
         residual = residual - alpha * image
     norm_next = square_sum(residual)

time: 577 us -> 581 us (level)
  matrix products: 143 us -> 159 us
  other arithmetic: 56.5 us -> 44.9 us
    dot_general x39 -> x36, matrix products: 114 us -> 127 us  [one(): return jnp.einsum(spec, exact, part, preferred_element_type=f32)]
    reduce_sum x3 -> x0, other arithmetic: 11.4 us -> none  [per_device(): jnp.sum(residual * residual)]
where the time goes in v8:
time: 581 us; the launch traced here: 576 us
  waiting for transfers between devices  282 us (49%)
  matrix products  159 us (27%)
  other arithmetic  44.9 us (8%)
  starting transfers between devices  42.3 us (7%)
  between operations  29.3 us (5%)
  local copies, waits for them, and re-layouts  18.8 us (3%)
    all_gather x6, waiting for transfers between devices, site_gather(): lax.all_gather(lax.optimization_barrier(x), 'site')  144 us
    dot_general x36, matrix products, one(): return jnp.einsum(spec, exact, part, preferred_element_type=f32)  127 us
    ppermute x3, waiting for transfers between devices, line_gather(): left = lax.ppermute(left, 'site', [(i + 1, i) for i in range(sites - 1)])  73 us
    dot_general x30, matrix products, one(): return jnp.einsum(spec, part, exact, preferred_element_type=f32)  30.4 us
    ppermute x4, waiting for transfers between devices, pair_sum(): lax.ppermute(part, 'inner', [(i, i ^ bit) for i in range(inner)])  25.8 us
    ppermute x10, waiting for transfers between devices, inner_sum(): x = x + lax.ppermute(x, 'inner', [(i, i ^ bit) for i in range(size)])  23.2 us
    ppermute x10, starting transfers between devices, inner_sum(): x = x + lax.ppermute(x, 'inner', [(i, i ^ bit) for i in range(size)])  16.5 us
    ppermute x3, starting transfers between devices, line_gather(): right = lax.ppermute(right, 'site', [(i, i + 1) for i in range(sites - 1)])  15.9 us
  transfers between devices with their start and end apart: 35, of which 25 were waited for; matrix products, arithmetic and copies ran while one was open for 19% of the time, Pallas kernels for 0%

profile of v8, /device:TPU:0, one launch (start us, length us, event | category | flops | bytes accessed | tf_op | source)
XLA Modules:
  0.0 576.5 jit_solution(18236807251190675359)
XLA Ops:
  17.2 13.6 %collective-permute-done.2 = f32[384,384]{1,0:T(8,128)S(1)} collective-permute-done((f32[384,384]{1,0:T(8,128)S(1)}, f32[384,384]{1,0:T(8,128)S(1)}, u32[]{:S(2)}, u32[]{:S(2)}) %collective-permute-start.2) | collective-permute-done | bytes 589856 | tf_op jit(solution)/shard_map/ppermute | solution.py:55
  33.2 41.9 %all-gather.13.cloned.1.call-done = f32[768,1024]{1,0:T(8,128)} async-done(((f32[192,1024]{1,0:T(8,128)}), f32[768,1024]{1,0:T(8,128)}) %all-gather.13.cloned.1.call-update) | async-done | bytes 3145744 | tf_op jit(solution)/shard_map/all_gather | solution.py:33
  76.5 5.5 collective-permute-start.6
  82.0 52.5 %collective-permute-done.7 = f32[384,640]{1,0:T(8,128)} collective-permute-done((f32[384,640]{1,0:T(8,128)S(1)}, f32[384,640]{1,0:T(8,128)}, u32[]{:S(2)}, u32[]{:S(2)}) %collective-permute-start.7) | collective-permute-done | bytes 983072 | tf_op jit(solution)/shard_map/ppermute | solution.py:43
  135.8 5.7 collective-permute-start.8
  143.9 43.1 %all-gather.15.cloned.1.call-done = f32[1536,640]{1,0:T(8,128)} async-done(((f32[384,640]{1,0:T(8,128)}), f32[1536,640]{1,0:T(8,128)}) %all-gather.15.cloned.1.call-update) | async-done | bytes 3932176 | tf_op jit(solution)/shard_map/all_gather | solution.py:33
  211.2 4.7 collective-permute-start.10
  231.9 10.5 %collective-permute-done.10 = f32[384,640]{1,0:T(8,128)S(1)} collective-permute-done((f32[384,640]{1,0:T(8,128)}, f32[384,640]{1,0:T(8,128)S(1)}, u32[]{:S(2)}, u32[]{:S(2)}) %collective-permute-start.10) | collective-permute-done | bytes 983072 | tf_op jit(solution)/shard_map/ppermute | solution.py:42
  244.7 20.5 %collective-permute-done.11 = f32[384,640]{1,0:T(8,128)S(1)} collective-permute-done((f32[384,640]{1,0:T(8,128)}, f32[384,640]{1,0:T(8,128)S(1)}, u32[]{:S(2)}, u32[]{:S(2)}) %collective-permute-start.11) | collective-permute-done | bytes 983072 | tf_op jit(solution)/shard_map/ppermute | solution.py:43
  276.0 5.8 %fusion.88 = f32[4,384,640]{2,1,0:T(8,128)S(1)} fusion(f32[1024,640]{1,0:T(8,128)} %copy-done.6, bf16[4,192,1024]{2,1,0:T(8,128)(2,1)} %copy-done.32, bf16[4,192,1024]{2,1,0:T(8,128)(2,1)} %copy-done.23), kind=kOutput, calls=%fused_computation.187 | convolution fusion | flops 2022178816 | bytes 9699328 | tf_op jit(solution)/shard_map/std,dc->stc/dot_general | solution.py:26
  306.7 9.5 %multiply_reduce_fusion.6 = (f32[]{:T(128)}, f32[1024,640]{1,0:T(8,128)S(1)}) fusion(f32[1024,640]{1,0:T(8,128)} %copy-done.6, f32[4,384,640]{2,1,0:T(8,128)} %copy-done.20, bf16[4,192,1024]{2,1,0:T(8,128)(2,1)} %copy-done.32, bf16[4,192,1024]{2,1,0:T(8,128)(2,1)} %copy-done.23, f32[1024,640,1]{1,0,2:T(8,128)} %fusion.36, f32[1024,640,1]{1,0,2:T(8,128)} %fusion.35, ...), kind=kOutput, calls=%fused_computation.106 | convolution fusion | flops 2028404736 | bytes 17563656 | tf_op jit(solution)/shard_map/std,stc->dc/dot_general | solution.py:26
  324.3 8.8 %collective-permute-done.15 = f32[200,384]{1,0:T(8,128)S(1)} collective-permute-done((f32[200,384]{1,0:T(8,128)S(1)}, f32[200,384]{1,0:T(8,128)S(1)}, u32[]{:S(2)}, u32[]{:S(2)}) %collective-permute-start.15) | collective-permute-done | bytes 307232 | tf_op jit(solution)/shard_map/ppermute | solution.py:130
  342.1 4.6 fusion.62
  346.7 18.7 %all-gather.19.cloned.1.call-done = f32[768,384]{1,0:T(8,128)} async-done(((f32[192,384]{1,0:T(8,128)}), f32[768,384]{1,0:T(8,128)}) %all-gather.19.cloned.1.call-update) | async-done | bytes 1179664 | tf_op jit(solution)/shard_map/all_gather | solution.py:33
  365.5 5.8 fusion.70
  395.8 9.7 %multiply_reduce_fusion.5 = (f32[]{:T(128)}, f32[1024,640]{1,0:T(8,128)S(1)}) fusion(f32[1024,640]{1,0:T(8,128)} %copy-done.14, f32[4,384,640]{2,1,0:T(8,128)} %copy-done.18, bf16[4,192,1024]{2,1,0:T(8,128)(2,1)} %copy-done.32, bf16[4,192,1024]{2,1,0:T(8,128)(2,1)} %copy-done.23, f32[1024,640,1]{1,0,2:T(8,128)} %fusion.38, f32[1024,640,1]{1,0,2:T(8,128)} %fusion.37, ...), kind=kOutput, calls=%fused_computation.104 | convolution fusion | flops 2028404736 | bytes 17563656 | tf_op jit(solution)/shard_map/std,stc->dc/dot_general | solution.py:26
  414.4 7.8 %collective-permute-done.20 = f32[200,384]{1,0:T(8,128)S(1)} collective-permute-done((f32[200,384]{1,0:T(8,128)S(1)}, f32[200,384]{1,0:T(8,128)S(1)}, u32[]{:S(2)}, u32[]{:S(2)}) %collective-permute-start.20) | collective-permute-done | bytes 307232 | tf_op jit(solution)/shard_map/ppermute | solution.py:130
  435.9 20.4 %all-gather.21.cloned.1.call-done = f32[768,384]{1,0:T(8,128)} async-done(((f32[192,384]{1,0:T(8,128)}), f32[768,384]{1,0:T(8,128)}) %all-gather.21.cloned.1.call-update) | async-done | bytes 1179664 | tf_op jit(solution)/shard_map/all_gather | solution.py:33
  456.4 5.6 fusion.77
  486.7 9.5 %multiply_reduce_fusion.4 = (f32[]{:T(128)}, f32[1024,640]{1,0:T(8,128)S(1)}) fusion(f32[1024,640]{1,0:T(8,128)} %copy-done.13, f32[4,384,640]{2,1,0:T(8,128)} %copy-done.19, bf16[4,192,1024]{2,1,0:T(8,128)(2,1)} %copy-done.32, bf16[4,192,1024]{2,1,0:T(8,128)(2,1)} %copy-done.23, f32[1024,640,1]{1,0,2:T(8,128)} %fusion.40, f32[1024,640,1]{1,0,2:T(8,128)} %fusion.39, ...), kind=kOutput, calls=%fused_computation.102 | convolution fusion | flops 2028404736 | bytes 17563656 | tf_op jit(solution)/shard_map/std,stc->dc/dot_general | solution.py:26
  505.2 7.8 %collective-permute-done.25 = f32[200,384]{1,0:T(8,128)S(1)} collective-permute-done((f32[200,384]{1,0:T(8,128)S(1)}, f32[200,384]{1,0:T(8,128)S(1)}, u32[]{:S(2)}, u32[]{:S(2)}) %collective-permute-start.25) | collective-permute-done | bytes 307232 | tf_op jit(solution)/shard_map/ppermute | solution.py:130
  520.1 4.6 fusion.54
  524.7 20.4 %all-gather.23.cloned.1.call-done = f32[768,384]{1,0:T(8,128)} async-done(((f32[192,384]{1,0:T(8,128)}), f32[768,384]{1,0:T(8,128)}) %all-gather.23.cloned.1.call-update) | async-done | bytes 1179664 | tf_op jit(solution)/shard_map/all_gather | solution.py:33
  545.2 5.6 fusion.84
  (269 shorter events, 204.6 us)
Async XLA Ops:
  6.5 68.6 %all-gather.13.cloned.1.call-start = ((), (), s32[]{:S(2)}) async-start(), calls=%async_computation | async-start | bytes 3932160 | tf_op jit(solution)/shard_map/all_gather | solution.py:33
  8.7 178.3 %all-gather.15.cloned.1.call-start = ((), (), s32[]{:S(2)}) async-start(), calls=%async_computation.1 | async-start | bytes 4915200 | tf_op jit(solution)/shard_map/all_gather | solution.py:33
  14.3 16.6 %collective-permute-start.2 = (f32[384,384]{1,0:T(8,128)S(1)}, f32[384,384]{1,0:T(8,128)S(1)}, u32[]{:S(2)}, u32[]{:S(2)}) collective-permute-start(f32[384,384]{1,0:T(8,128)S(1)} %add.360), channel_id=1, source_target_pairs={{0,2},{1,3},{2,0},{3,1},{4,6},{5,7},{6,4},{7,5},{8,10},{9,11},{10,... | collective-permute-start | bytes 1769480 | tf_op jit(solution)/shard_map/ppermute | solution.py:55
  33.2 242.7 %all-gather.17.cloned.1.call-start = ((), (), s32[]{:S(2)}) async-start(), calls=%async_computation.2 | async-start | bytes 1474560 | tf_op jit(solution)/shard_map/all_gather | solution.py:33
  75.2 115.5 %collective-permute-start = (f32[4,192,1024]{2,1,0:T(8,128)}, f32[4,192,1024]{2,1,0:T(8,128)}, u32[]{:S(2)}, u32[]{:S(2)}) collective-permute-start(f32[4,192,1024]{2,1,0:T(8,128)} %bitcast.206), channel_id=1, source_target_pairs={{0,1},{1,0},{2,3},{3,2},{4,5},{5,4},{6,7},{7,6},{8,9},{9,8},{10,11... | collective-permute-start | bytes 9437192 | tf_op jit(solution)/shard_map/ppermute | solution.py:61
  75.2 59.3 %collective-permute-start.7 = (f32[384,640]{1,0:T(8,128)S(1)}, f32[384,640]{1,0:T(8,128)}, u32[]{:S(2)}, u32[]{:S(2)}) collective-permute-start(f32[384,640]{1,0:T(8,128)S(1)} %convert_multiply_fusion), channel_id=1, source_target_pairs={{4,0},{8,4},{12,8},{5,1},{9,5},{13,9},{6,2},{10,6},{14,10},{7,3},{... | collective-permute-start | bytes 2949128 | tf_op jit(solution)/shard_map/ppermute | solution.py:43
  76.5 59.3 %collective-permute-start.6 = (f32[384,640]{1,0:T(8,128)S(1)}, f32[384,640]{1,0:T(8,128)}, u32[]{:S(2)}, u32[]{:S(2)}) collective-permute-start(f32[384,640]{1,0:T(8,128)S(1)} %convert_multiply_fusion), channel_id=1, source_target_pairs={{0,4},{4,8},{8,12},{1,5},{5,9},{9,13},{2,6},{6,10},{10,14},{3,7},{... | collective-permute-start | bytes 2949128 | tf_op jit(solution)/shard_map/ppermute | solution.py:42
  134.5 86.1 %collective-permute-start.9 = (f32[384,640]{1,0:T(8,128)}, f32[384,640]{1,0:T(8,128)}, u32[]{:S(2)}, u32[]{:S(2)}) collective-permute-start(f32[384,640]{1,0:T(8,128)} %collective-permute-done.7), channel_id=1, source_target_pairs={{4,0},{8,4},{12,8},{5,1},{9,5},{13,9},{6,2},{10,6},{14,10},{7,3},{... | collective-permute-start | bytes 2949128 | tf_op jit(solution)/shard_map/ppermute | solution.py:43
  135.8 75.3 %collective-permute-start.8 = (f32[384,640]{1,0:T(8,128)}, f32[384,640]{1,0:T(8,128)}, u32[]{:S(2)}, u32[]{:S(2)}) collective-permute-start(f32[384,640]{1,0:T(8,128)} %collective-permute-done.6), channel_id=1, source_target_pairs={{0,4},{4,8},{8,12},{1,5},{5,9},{9,13},{2,6},{6,10},{10,14},{3,7},{... | collective-permute-start | bytes 2949128 | tf_op jit(solution)/shard_map/ppermute | solution.py:42
  207.8 8.1 %collective-permute-start.3 = (f32[200,384]{1,0:T(8,128)S(1)}, f32[200,384]{1,0:T(8,128)S(1)}, u32[]{:S(2)}, u32[]{:S(2)}) collective-permute-start(f32[200,384]{1,0:T(8,128)S(1)} %concatenate.45), channel_id=1, source_target_pairs={{0,1},{1,0},{2,3},{3,2},{4,5},{5,4},{6,7},{7,6},{8,9},{9,8},{10,11... | collective-permute-start | bytes 921608 | tf_op jit(solution)/shard_map/ppermute | solution.py:127
  211.2 31.3 %collective-permute-start.10 = (f32[384,640]{1,0:T(8,128)}, f32[384,640]{1,0:T(8,128)S(1)}, u32[]{:S(2)}, u32[]{:S(2)}) collective-permute-start(f32[384,640]{1,0:T(8,128)} %collective-permute-done.8), channel_id=1, source_target_pairs={{0,4},{4,8},{8,12},{1,5},{5,9},{9,13},{2,6},{6,10},{10,14},{3,7},{... | collective-permute-start | bytes 2949128 | tf_op jit(solution)/shard_map/ppermute | solution.py:42
  216.6 9.3 %collective-permute-start.4 = (f32[200,384]{1,0:T(8,128)S(1)}, f32[200,384]{1,0:T(8,128)S(1)}, u32[]{:S(2)}, u32[]{:S(2)}) collective-permute-start(f32[200,384]{1,0:T(8,128)S(1)} %pad_add_fusion.3), channel_id=1, source_target_pairs={{0,2},{1,3},{2,0},{3,1},{4,6},{5,7},{6,4},{7,5},{8,10},{9,11},{10,... | collective-permute-start | bytes 921608 | tf_op jit(solution)/shard_map/ppermute | solution.py:130
  220.7 44.5 %collective-permute-start.11 = (f32[384,640]{1,0:T(8,128)}, f32[384,640]{1,0:T(8,128)S(1)}, u32[]{:S(2)}, u32[]{:S(2)}) collective-permute-start(f32[384,640]{1,0:T(8,128)} %collective-permute-done.9), channel_id=1, source_target_pairs={{4,0},{8,4},{12,8},{5,1},{9,5},{13,9},{6,2},{10,6},{14,10},{7,3},{... | collective-permute-start | bytes 2949128 | tf_op jit(solution)/shard_map/ppermute | solution.py:43
  226.8 138.7 %all-gather.19.cloned.1.call-start = ((), (), s32[]{:S(2)}) async-start(), calls=%async_computation.3 | async-start | bytes 1474560 | tf_op jit(solution)/shard_map/all_gather | solution.py:33
  275.9 9.3 %collective-permute-start.5 = (f32[4,192,384]{2,1,0:T(8,128)}, f32[4,192,384]{2,1,0:T(8,128)S(1)}, u32[]{:S(2)}, u32[]{:S(2)}) collective-permute-start(f32[4,192,384]{2,1,0:T(8,128)} %bitcast.208), channel_id=1, source_target_pairs={{0,1},{1,0},{2,3},{3,2},{4,5},{5,4},{6,7},{7,6},{8,9},{9,8},{10,11... | collective-permute-start | bytes 3538952 | tf_op jit(solution)/shard_map/ppermute | solution.py:61
  301.8 3.7 collective-permute-start.13
  323.7 9.4 %collective-permute-start.15 = (f32[200,384]{1,0:T(8,128)S(1)}, f32[200,384]{1,0:T(8,128)S(1)}, u32[]{:S(2)}, u32[]{:S(2)}) collective-permute-start(f32[200,384]{1,0:T(8,128)S(1)} %pad_add_fusion.2), channel_id=1, source_target_pairs={{0,2},{1,3},{2,0},{3,1},{4,6},{5,7},{6,4},{7,5},{8,10},{9,11},{10,... | collective-permute-start | bytes 921608 | tf_op jit(solution)/shard_map/ppermute | solution.py:130
  337.6 118.7 %all-gather.21.cloned.1.call-start = ((), (), s32[]{:S(2)}) async-start(), calls=%async_computation.4 | async-start | bytes 1474560 | tf_op jit(solution)/shard_map/all_gather | solution.py:33
  365.4 8.7 %collective-permute-start.16 = (f32[4,192,384]{2,1,0:T(8,128)}, f32[4,192,384]{2,1,0:T(8,128)S(1)}, u32[]{:S(2)}, u32[]{:S(2)}) collective-permute-start(f32[4,192,384]{2,1,0:T(8,128)} %bitcast.212), channel_id=1, source_target_pairs={{0,1},{1,0},{2,3},{3,2},{4,5},{5,4},{6,7},{7,6},{8,9},{9,8},{10,11... | collective-permute-start | bytes 3538952 | tf_op jit(solution)/shard_map/ppermute | solution.py:61
  412.9 9.4 %collective-permute-start.20 = (f32[200,384]{1,0:T(8,128)S(1)}, f32[200,384]{1,0:T(8,128)S(1)}, u32[]{:S(2)}, u32[]{:S(2)}) collective-permute-start(f32[200,384]{1,0:T(8,128)S(1)} %pad_add_fusion.1), channel_id=1, source_target_pairs={{0,2},{1,3},{2,0},{3,1},{4,6},{5,7},{6,4},{7,5},{8,10},{9,11},{10,... | collective-permute-start | bytes 921608 | tf_op jit(solution)/shard_map/ppermute | solution.py:130
  426.8 118.3 %all-gather.23.cloned.1.call-start = ((), (), s32[]{:S(2)}) async-start(), calls=%async_computation.5 | async-start | bytes 1474560 | tf_op jit(solution)/shard_map/all_gather | solution.py:33
  456.3 8.5 %collective-permute-start.21 = (f32[4,192,384]{2,1,0:T(8,128)}, f32[4,192,384]{2,1,0:T(8,128)S(1)}, u32[]{:S(2)}, u32[]{:S(2)}) collective-permute-start(f32[4,192,384]{2,1,0:T(8,128)} %bitcast.214), channel_id=1, source_target_pairs={{0,1},{1,0},{2,3},{3,2},{4,5},{5,4},{6,7},{7,6},{8,9},{9,8},{10,11... | collective-permute-start | bytes 3538952 | tf_op jit(solution)/shard_map/ppermute | solution.py:61
  503.6 9.4 %collective-permute-start.25 = (f32[200,384]{1,0:T(8,128)S(1)}, f32[200,384]{1,0:T(8,128)S(1)}, u32[]{:S(2)}, u32[]{:S(2)}) collective-permute-start(f32[200,384]{1,0:T(8,128)S(1)} %pad_add_fusion), channel_id=1, source_target_pairs={{0,2},{1,3},{2,0},{3,1},{4,6},{5,7},{6,4},{7,5},{8,10},{9,11},{10,... | collective-permute-start | bytes 921608 | tf_op jit(solution)/shard_map/ppermute | solution.py:130
  545.1 8.5 %collective-permute-start.26 = (f32[4,192,384]{2,1,0:T(8,128)}, f32[4,192,384]{2,1,0:T(8,128)S(1)}, u32[]{:S(2)}, u32[]{:S(2)}) collective-permute-start(f32[4,192,384]{2,1,0:T(8,128)} %bitcast.210), channel_id=1, source_target_pairs={{0,1},{1,0},{2,3},{3,2},{4,5},{5,4},{6,7},{7,6},{8,9},{9,8},{10,11... | collective-permute-start | bytes 3538952 | tf_op jit(solution)/shard_map/ppermute | solution.py:61
  (62 other events, 353.5 us)
Sparse Core Ops, SparseCore 0:
  8.9 66.1 all-gather.12
  76.7 110.2 all-gather.14
  226.9 38.0 all-gather.16
  337.7 27.6 all-gather.18
  426.9 29.3 all-gather.20
  515.7 29.2 all-gather.22

commit v9 on v6

--- a/solution.py
+++ b/solution.py
@@ -84,12 +84,12 @@
     count = inputs.shape[0]
     rows = grads.shape[1] // sites
 
-    every_input = (line_gather(inputs.astype(f32) * 2.0) * 0.5).astype(bf16)
+    every_input = (site_gather(inputs.astype(f32) * 2.0) * 0.5).astype(bf16)
     core = lax.axis_index("inner") % 2
     split = inner % 2 == 0 and count % 16 == 0
     if split:
         own_rows = lax.dynamic_slice_in_dim(grads, core * (count // 2), count // 2, 0)
-        wide = site_gather(own_rows.astype(f32) * 2.0)
+        wide = line_gather(own_rows.astype(f32) * 2.0)
         every_grad = halves(wide, lambda v: (v * 0.5).astype(bf16))
     else:
         every_grad = (site_gather(grads.astype(f32) * 2.0) * 0.5).astype(bf16)

time: 577 us -> 630 us (1.092)
  waiting for transfers between devices: 282 us -> 254 us
  local copies, waits for them, and re-layouts: 18.5 us -> 46 us
  other arithmetic: 56.5 us -> 80.9 us
  matrix products: 143 us -> 162 us
  starting transfers between devices: 42.8 us -> 50.2 us
    all_gather x6, waiting for transfers between devices: 144 us -> 114 us  [site_gather(): lax.all_gather(lax.optimization_barrier(x), 'site')]
    add x0 -> x4, other arithmetic: none -> 20.5 us  [apply_operator(): exact_dot('stu,suc->stc', every_input, pair_all, exact_first=False)]
    dot_general x39, matrix products: 114 us -> 133 us  [one(): return jnp.einsum(spec, exact, part, preferred_element_type=f32)]
    ppermute x0 -> x7, local copies, waits for them, and re-layouts: none -> 15.6 us  [the longest x3 7.29 us: line_gather(): right = lax.ppermute(right, 'site', [(i, i + 1) for i in range(sites - 1)])]
    ppermute x3, waiting for transfers between devices: 10.7 us -> 0.52 us  [line_gather(): right = lax.ppermute(right, 'site', [(i, i + 1) for i in range(sites - 1)])]
    ppermute x3, waiting for transfers between devices: 73 us -> 79.6 us  [line_gather(): left = lax.ppermute(left, 'site', [(i + 1, i) for i in range(sites - 1)])]
  transfers between devices with their start and end apart: 35 -> 35, of which waited for: 25 -> 28; matrix products, arithmetic and copies ran while one was open for 19% -> 23% of each run, Pallas kernels for 0% -> 0%
where the time goes in v9:
time: 630 us; the launch traced here: 622 us
  waiting for transfers between devices  254 us (40%)
  matrix products  162 us (26%)
  other arithmetic  80.9 us (13%)
  starting transfers between devices  50.2 us (8%)
  local copies, waits for them, and re-layouts  46 us (7%)
  between operations  28.6 us (5%)
    dot_general x39, matrix products, one(): return jnp.einsum(spec, exact, part, preferred_element_type=f32)  133 us
    all_gather x6, waiting for transfers between devices, site_gather(): lax.all_gather(lax.optimization_barrier(x), 'site')  114 us
    ppermute x3, waiting for transfers between devices, line_gather(): left = lax.ppermute(left, 'site', [(i + 1, i) for i in range(sites - 1)])  79.6 us
    ppermute x4, waiting for transfers between devices, pair_sum(): lax.ppermute(part, 'inner', [(i, i ^ bit) for i in range(inner)])  31.4 us
    dot_general x30, matrix products, one(): return jnp.einsum(spec, part, exact, preferred_element_type=f32)  27.6 us
    ppermute x10, waiting for transfers between devices, inner_sum(): x = x + lax.ppermute(x, 'inner', [(i, i ^ bit) for i in range(size)])  21.1 us
    add x4, other arithmetic, apply_operator(): exact_dot('stu,suc->stc', every_input, pair_all, exact_first=False)  20.5 us
    ppermute x3, starting transfers between devices, line_gather(): right = lax.ppermute(right, 'site', [(i, i + 1) for i in range(sites - 1)])  20.5 us
  transfers between devices with their start and end apart: 35, of which 28 were waited for; matrix products, arithmetic and copies ran while one was open for 23% of the time, Pallas kernels for 0%

profile of v9, /device:TPU:0, one launch (start us, length us, event | category | flops | bytes accessed | tf_op | source)
XLA Modules:
  0.0 622.1 jit_solution(2500741606789910917)
XLA Ops:
  18.3 11.6 %collective-permute-done.8 = f32[384,384]{1,0:T(8,128)S(1)} collective-permute-done((f32[384,384]{1,0:T(8,128)S(1)}, f32[384,384]{1,0:T(8,128)S(1)}, u32[]{:S(2)}, u32[]{:S(2)}) %collective-permute-start.8) | collective-permute-done | bytes 589856 | tf_op jit(solution)/shard_map/ppermute | solution.py:55
  38.3 5.4 collective-permute-start
  43.7 44.1 %collective-permute-done.1 = f32[192,1024]{1,0:T(8,128)} collective-permute-done((f32[192,1024]{1,0:T(8,128)}, f32[192,1024]{1,0:T(8,128)}, u32[]{:S(2)}, u32[]{:S(2)}) %collective-permute-start.1) | collective-permute-done | bytes 786464 | tf_op jit(solution)/shard_map/ppermute | solution.py:43
  89.1 9.6 %collective-permute-start.2 = (f32[192,1024]{1,0:T(8,128)}, f32[192,1024]{1,0:T(8,128)}, u32[]{:S(2)}, u32[]{:S(2)}) collective-permute-start(f32[192,1024]{1,0:T(8,128)} %collective-permute-done), channel_id=1, source_target_pairs={{0,4},{4,8},{8,12},{1,5},{5,9},{9,13},{2,6},{6,10},{10,14},{3,7},{... | collective-permute-start | bytes 2359304 | tf_op jit(solution)/shard_map/ppermute | solution.py:42
  105.3 32.9 %collective-permute-done.3 = f32[192,1024]{1,0:T(8,128)S(1)} collective-permute-done((f32[192,1024]{1,0:T(8,128)}, f32[192,1024]{1,0:T(8,128)S(1)}, u32[]{:S(2)}, u32[]{:S(2)}) %collective-permute-start.3) | collective-permute-done | bytes 786464 | tf_op jit(solution)/shard_map/ppermute | solution.py:43
  139.5 5.4 collective-permute-start.4
  212.4 7.8 %collective-permute-done.10 = f32[200,384]{1,0:T(8,128)S(1)} collective-permute-done((f32[200,384]{1,0:T(8,128)S(1)}, f32[200,384]{1,0:T(8,128)S(1)}, u32[]{:S(2)}, u32[]{:S(2)}) %collective-permute-start.10) | collective-permute-done | bytes 307232 | tf_op jit(solution)/shard_map/ppermute | solution.py:130
  221.1 31.7 %all-gather.17.cloned.1.call-done = f32[1536,640]{1,0:T(8,128)} async-done(((f32[384,640]{1,0:T(8,128)}), f32[1536,640]{1,0:T(8,128)}) %all-gather.17.cloned.1.call-update) | async-done | bytes 3932176 | tf_op jit(solution)/shard_map/all_gather | solution.py:33
  261.3 22.1 %all-gather.15.cloned.1.call-done = f32[768,384]{1,0:T(8,128)} async-done(((f32[192,384]{1,0:T(8,128)}), f32[768,384]{1,0:T(8,128)}) %all-gather.15.cloned.1.call-update) | async-done | bytes 1179664 | tf_op jit(solution)/shard_map/all_gather | solution.py:33
  283.4 5.6 fusion.96
  300.4 6.8 %multiply_add_fusion.3 = f32[4,384,640]{2,1,0:T(8,128)} fusion(f32[4,384,640]{2,1,0:T(8,128)} %add_add_fusion.3, f32[4,384,640]{2,1,0:T(8,128)} %fusion.111, f32[4,384,640]{2,1,0:T(8,128)S(1)} %fusion.112, f32[4,384,640]{2,1,0:T(8,128)S(1)} %fusion.109), kind=kLoop, calls=%fused_computation.34 | loop fusion | flops 4915200 | bytes 19660800 | tf_op jit(solution)/shard_map/add | solution.py:144
  340.7 7.8 %collective-permute-done.15 = f32[200,384]{1,0:T(8,128)S(1)} collective-permute-done((f32[200,384]{1,0:T(8,128)S(1)}, f32[200,384]{1,0:T(8,128)S(1)}, u32[]{:S(2)}, u32[]{:S(2)}) %collective-permute-start.15) | collective-permute-done | bytes 307232 | tf_op jit(solution)/shard_map/ppermute | solution.py:130
  362.1 20.2 %all-gather.19.cloned.1.call-done = f32[768,384]{1,0:T(8,128)} async-done(((f32[192,384]{1,0:T(8,128)}), f32[768,384]{1,0:T(8,128)}) %all-gather.19.cloned.1.call-update) | async-done | bytes 1179664 | tf_op jit(solution)/shard_map/all_gather | solution.py:33
  382.3 5.6 fusion.78
  402.0 5.8 fusion.38
  436.3 7.8 %collective-permute-done.20 = f32[200,384]{1,0:T(8,128)S(1)} collective-permute-done((f32[200,384]{1,0:T(8,128)S(1)}, f32[200,384]{1,0:T(8,128)S(1)}, u32[]{:S(2)}, u32[]{:S(2)}) %collective-permute-start.20) | collective-permute-done | bytes 307232 | tf_op jit(solution)/shard_map/ppermute | solution.py:130
  458.0 19.9 %all-gather.21.cloned.1.call-done = f32[768,384]{1,0:T(8,128)} async-done(((f32[192,384]{1,0:T(8,128)}), f32[768,384]{1,0:T(8,128)}) %all-gather.21.cloned.1.call-update) | async-done | bytes 1179664 | tf_op jit(solution)/shard_map/all_gather | solution.py:33
  477.9 5.6 fusion.85
  497.6 5.8 fusion.40
  531.8 7.8 %collective-permute-done.25 = f32[200,384]{1,0:T(8,128)S(1)} collective-permute-done((f32[200,384]{1,0:T(8,128)S(1)}, f32[200,384]{1,0:T(8,128)S(1)}, u32[]{:S(2)}, u32[]{:S(2)}) %collective-permute-start.25) | collective-permute-done | bytes 307232 | tf_op jit(solution)/shard_map/ppermute | solution.py:130
  551.6 20.1 %all-gather.23.cloned.1.call-done = f32[768,384]{1,0:T(8,128)} async-done(((f32[192,384]{1,0:T(8,128)}), f32[768,384]{1,0:T(8,128)}) %all-gather.23.cloned.1.call-update) | async-done | bytes 1179664 | tf_op jit(solution)/shard_map/all_gather | solution.py:33
  571.8 5.6 fusion.92
  589.4 6.2 %fusion.42 = f32[1024,640,1]{1,0,2:T(8,128)S(1)} fusion(bf16[4,384,1024]{1,2,0:T(8,128)(2,1)} %pad_maximum_fusion, f32[4,384,640]{2,1,0:T(8,128)S(1)} %multiply_add_fusion), kind=kOutput, calls=%fused_computation.136 | convolution fusion | flops 2017198080 | bytes 9699328 | tf_op jit(solution)/shard_map/std,stc->dc/dot_general | solution.py:26
  598.4 5.6 fusion.14
  (290 shorter events, 286.4 us)
Async XLA Ops:
  6.5 183.0 %all-gather.13.cloned.1.call-start = ((), (), s32[]{:S(2)}) async-start(), calls=%async_computation | async-start | bytes 4915200 | tf_op jit(solution)/shard_map/all_gather | solution.py:33
  13.4 16.6 %collective-permute-start.8 = (f32[384,384]{1,0:T(8,128)S(1)}, f32[384,384]{1,0:T(8,128)S(1)}, u32[]{:S(2)}, u32[]{:S(2)}) collective-permute-start(f32[384,384]{1,0:T(8,128)S(1)} %add.388), channel_id=1, source_target_pairs={{0,2},{1,3},{2,0},{3,1},{4,6},{5,7},{6,4},{7,5},{8,10},{9,11},{10,... | collective-permute-start | bytes 1769480 | tf_op jit(solution)/shard_map/ppermute | solution.py:55
  32.3 220.5 %all-gather.17.cloned.1.call-start = ((), (), s32[]{:S(2)}) async-start(), calls=%async_computation.2 | async-start | bytes 4915200 | tf_op jit(solution)/shard_map/all_gather | solution.py:33
  37.0 50.8 %collective-permute-start.1 = (f32[192,1024]{1,0:T(8,128)}, f32[192,1024]{1,0:T(8,128)}, u32[]{:S(2)}, u32[]{:S(2)}) collective-permute-start(f32[192,1024]{1,0:T(8,128)} %copy.18), channel_id=1, source_target_pairs={{4,0},{8,4},{12,8},{5,1},{9,5},{13,9},{6,2},{10,6},{14,10},{7,3},{... | collective-permute-start | bytes 2359304 | tf_op jit(solution)/shard_map/ppermute | solution.py:43
  38.3 50.8 %collective-permute-start = (f32[192,1024]{1,0:T(8,128)}, f32[192,1024]{1,0:T(8,128)}, u32[]{:S(2)}, u32[]{:S(2)}) collective-permute-start(f32[192,1024]{1,0:T(8,128)} %copy.18), channel_id=1, source_target_pairs={{0,4},{4,8},{8,12},{1,5},{5,9},{9,13},{2,6},{6,10},{10,14},{3,7},{... | collective-permute-start | bytes 2359304 | tf_op jit(solution)/shard_map/ppermute | solution.py:42
  87.8 50.4 %collective-permute-start.3 = (f32[192,1024]{1,0:T(8,128)}, f32[192,1024]{1,0:T(8,128)S(1)}, u32[]{:S(2)}, u32[]{:S(2)}) collective-permute-start(f32[192,1024]{1,0:T(8,128)} %collective-permute-done.1), channel_id=1, source_target_pairs={{4,0},{8,4},{12,8},{5,1},{9,5},{13,9},{6,2},{10,6},{14,10},{7,3},{... | collective-permute-start | bytes 2359304 | tf_op jit(solution)/shard_map/ppermute | solution.py:43
  89.1 50.4 %collective-permute-start.2 = (f32[192,1024]{1,0:T(8,128)}, f32[192,1024]{1,0:T(8,128)}, u32[]{:S(2)}, u32[]{:S(2)}) collective-permute-start(f32[192,1024]{1,0:T(8,128)} %collective-permute-done), channel_id=1, source_target_pairs={{0,4},{4,8},{8,12},{1,5},{5,9},{9,13},{2,6},{6,10},{10,14},{3,7},{... | collective-permute-start | bytes 2359304 | tf_op jit(solution)/shard_map/ppermute | solution.py:42
  138.2 19.4 %collective-permute-start.5 = (f32[192,1024]{1,0:T(8,128)S(1)}, f32[192,1024]{1,0:T(8,128)}, u32[]{:S(2)}, u32[]{:S(2)}) collective-permute-start(f32[192,1024]{1,0:T(8,128)S(1)} %collective-permute-done.3), channel_id=1, source_target_pairs={{4,0},{8,4},{12,8},{5,1},{9,5},{13,9},{6,2},{10,6},{14,10},{7,3},{... | collective-permute-start | bytes 2359304 | tf_op jit(solution)/shard_map/ppermute | solution.py:43
  139.5 20.1 %collective-permute-start.4 = (f32[192,1024]{1,0:T(8,128)}, f32[192,1024]{1,0:T(8,128)}, u32[]{:S(2)}, u32[]{:S(2)}) collective-permute-start(f32[192,1024]{1,0:T(8,128)} %collective-permute-done.2), channel_id=1, source_target_pairs={{0,4},{4,8},{8,12},{1,5},{5,9},{9,13},{2,6},{6,10},{10,14},{3,7},{... | collective-permute-start | bytes 2359304 | tf_op jit(solution)/shard_map/ppermute | solution.py:42
  172.4 6.0 collective-permute-start.6
  173.4 110.0 %all-gather.15.cloned.1.call-start = ((), (), s32[]{:S(2)}) async-start(), calls=%async_computation.1 | async-start | bytes 1474560 | tf_op jit(solution)/shard_map/all_gather | solution.py:33
  210.9 9.4 %collective-permute-start.10 = (f32[200,384]{1,0:T(8,128)S(1)}, f32[200,384]{1,0:T(8,128)S(1)}, u32[]{:S(2)}, u32[]{:S(2)}) collective-permute-start(f32[200,384]{1,0:T(8,128)S(1)} %pad_add_fusion.3), channel_id=1, source_target_pairs={{0,2},{1,3},{2,0},{3,1},{4,6},{5,7},{6,4},{7,5},{8,10},{9,11},{10,... | collective-permute-start | bytes 921608 | tf_op jit(solution)/shard_map/ppermute | solution.py:130
  221.1 161.2 %all-gather.19.cloned.1.call-start = ((), (), s32[]{:S(2)}) async-start(), calls=%async_computation.3 | async-start | bytes 1474560 | tf_op jit(solution)/shard_map/all_gather | solution.py:33
  283.4 11.0 %collective-permute-start.11 = (f32[4,192,384]{2,1,0:T(8,128)}, f32[4,192,384]{2,1,0:T(8,128)S(1)}, u32[]{:S(2)}, u32[]{:S(2)}) collective-permute-start(f32[4,192,384]{2,1,0:T(8,128)} %bitcast.236), channel_id=1, source_target_pairs={{0,1},{1,0},{2,3},{3,2},{4,5},{5,4},{6,7},{7,6},{8,9},{9,8},{10,11... | collective-permute-start | bytes 3538952 | tf_op jit(solution)/shard_map/ppermute | solution.py:61
  322.9 3.7 collective-permute-start.13
  339.1 9.4 %collective-permute-start.15 = (f32[200,384]{1,0:T(8,128)S(1)}, f32[200,384]{1,0:T(8,128)S(1)}, u32[]{:S(2)}, u32[]{:S(2)}) collective-permute-start(f32[200,384]{1,0:T(8,128)S(1)} %pad_add_fusion.2), channel_id=1, source_target_pairs={{0,2},{1,3},{2,0},{3,1},{4,6},{5,7},{6,4},{7,5},{8,10},{9,11},{10,... | collective-permute-start | bytes 921608 | tf_op jit(solution)/shard_map/ppermute | solution.py:130
  352.8 125.1 %all-gather.21.cloned.1.call-start = ((), (), s32[]{:S(2)}) async-start(), calls=%async_computation.4 | async-start | bytes 1474560 | tf_op jit(solution)/shard_map/all_gather | solution.py:33
  382.3 10.4 %collective-permute-start.16 = (f32[4,192,384]{2,1,0:T(8,128)}, f32[4,192,384]{2,1,0:T(8,128)S(1)}, u32[]{:S(2)}, u32[]{:S(2)}) collective-permute-start(f32[4,192,384]{2,1,0:T(8,128)} %bitcast.238), channel_id=1, source_target_pairs={{0,1},{1,0},{2,3},{3,2},{4,5},{5,4},{6,7},{7,6},{8,9},{9,8},{10,11... | collective-permute-start | bytes 3538952 | tf_op jit(solution)/shard_map/ppermute | solution.py:61
  418.6 3.7 collective-permute-start.18
  434.8 9.4 %collective-permute-start.20 = (f32[200,384]{1,0:T(8,128)S(1)}, f32[200,384]{1,0:T(8,128)S(1)}, u32[]{:S(2)}, u32[]{:S(2)}) collective-permute-start(f32[200,384]{1,0:T(8,128)S(1)} %pad_add_fusion.1), channel_id=1, source_target_pairs={{0,2},{1,3},{2,0},{3,1},{4,6},{5,7},{6,4},{7,5},{8,10},{9,11},{10,... | collective-permute-start | bytes 921608 | tf_op jit(solution)/shard_map/ppermute | solution.py:130
  448.4 123.4 %all-gather.23.cloned.1.call-start = ((), (), s32[]{:S(2)}) async-start(), calls=%async_computation.5 | async-start | bytes 1474560 | tf_op jit(solution)/shard_map/all_gather | solution.py:33
  477.9 10.4 %collective-permute-start.21 = (f32[4,192,384]{2,1,0:T(8,128)}, f32[4,192,384]{2,1,0:T(8,128)S(1)}, u32[]{:S(2)}, u32[]{:S(2)}) collective-permute-start(f32[4,192,384]{2,1,0:T(8,128)} %bitcast.240), channel_id=1, source_target_pairs={{0,1},{1,0},{2,3},{3,2},{4,5},{5,4},{6,7},{7,6},{8,9},{9,8},{10,11... | collective-permute-start | bytes 3538952 | tf_op jit(solution)/shard_map/ppermute | solution.py:61
  530.3 9.4 %collective-permute-start.25 = (f32[200,384]{1,0:T(8,128)S(1)}, f32[200,384]{1,0:T(8,128)S(1)}, u32[]{:S(2)}, u32[]{:S(2)}) collective-permute-start(f32[200,384]{1,0:T(8,128)S(1)} %pad_add_fusion), channel_id=1, source_target_pairs={{0,2},{1,3},{2,0},{3,1},{4,6},{5,7},{6,4},{7,5},{8,10},{9,11},{10,... | collective-permute-start | bytes 921608 | tf_op jit(solution)/shard_map/ppermute | solution.py:130
  571.8 10.4 %collective-permute-start.26 = (f32[4,192,384]{2,1,0:T(8,128)}, f32[4,192,384]{2,1,0:T(8,128)S(1)}, u32[]{:S(2)}, u32[]{:S(2)}) collective-permute-start(f32[4,192,384]{2,1,0:T(8,128)} %bitcast.234), channel_id=1, source_target_pairs={{0,1},{1,0},{2,3},{3,2},{4,5},{5,4},{6,7},{7,6},{8,9},{9,8},{10,11... | collective-permute-start | bytes 3538952 | tf_op jit(solution)/shard_map/ppermute | solution.py:61
  (62 other events, 278.5 us)
Sparse Core Ops, SparseCore 0:
  32.4 107.2 all-gather.12
  173.5 79.2 all-gather.16
  254.4 28.9 all-gather.14
  352.9 29.2 all-gather.18
  448.5 29.2 all-gather.20
  542.4 29.2 all-gather.22

commit v10 on v6

--- a/solution.py
+++ b/solution.py
@@ -84,7 +84,6 @@
     count = inputs.shape[0]
     rows = grads.shape[1] // sites
 
-    every_input = (line_gather(inputs.astype(f32) * 2.0) * 0.5).astype(bf16)
     core = lax.axis_index("inner") % 2
     split = inner % 2 == 0 and count % 16 == 0
     if split:
@@ -111,6 +110,8 @@
         turned = jnp.concatenate([mixed_w_all[:, half:], mixed_w_all[:, :half]], axis=1)
         mixed_w_all = jnp.where(core == 0, mixed_w_all, turned)
     rhs = image_of(mixed_w_all)
+    wide_input, mixed_w_all = lax.optimization_barrier((inputs.astype(f32) * 2.0, mixed_w_all))
+    every_input = (line_gather(wide_input) * 0.5).astype(bf16)
 
     def square_sum(x):
         return inner_sum(jnp.sum(x * x), inner)

time: 577 us -> 578 us (level)
    ppermute x3, waiting for transfers between devices: 73 us -> 20.7 us  [line_gather(): left = lax.ppermute(left, 'site', [(i + 1, i) for i in range(sites - 1)])]
    all_gather x6, waiting for transfers between devices: 144 us -> 177 us  [site_gather(): lax.all_gather(lax.optimization_barrier(x), 'site')]
    ppermute x3, waiting for transfers between devices: 10.7 us -> 32.1 us  [line_gather(): right = lax.ppermute(right, 'site', [(i, i + 1) for i in range(sites - 1)])]
  transfers between devices with their start and end apart: 35 -> 35, of which waited for: 25 -> 26; matrix products, arithmetic and copies ran while one was open for 19% -> 17% of each run, Pallas kernels for 0% -> 0%
where the time goes in v10:
time: 578 us; the launch traced here: 574 us
  waiting for transfers between devices  281 us (49%)
  matrix products  145 us (25%)
  other arithmetic  55.2 us (10%)
  starting transfers between devices  45.5 us (8%)
  between operations  28.5 us (5%)
  local copies, waits for them, and re-layouts  19.2 us (3%)
    all_gather x6, waiting for transfers between devices, site_gather(): lax.all_gather(lax.optimization_barrier(x), 'site')  177 us
    dot_general x39, matrix products, one(): return jnp.einsum(spec, exact, part, preferred_element_type=f32)  116 us
    ppermute x3, waiting for transfers between devices, line_gather(): right = lax.ppermute(right, 'site', [(i, i + 1) for i in range(sites - 1)])  32.1 us
    dot_general x30, matrix products, one(): return jnp.einsum(spec, part, exact, preferred_element_type=f32)  27.4 us
    ppermute x4, waiting for transfers between devices, pair_sum(): lax.ppermute(part, 'inner', [(i, i ^ bit) for i in range(inner)])  23.5 us
    ppermute x10, waiting for transfers between devices, inner_sum(): x = x + lax.ppermute(x, 'inner', [(i, i ^ bit) for i in range(size)])  22.8 us
    ppermute x3, waiting for transfers between devices, line_gather(): left = lax.ppermute(left, 'site', [(i + 1, i) for i in range(sites - 1)])  20.7 us
    ppermute x10, starting transfers between devices, inner_sum(): x = x + lax.ppermute(x, 'inner', [(i, i ^ bit) for i in range(size)])  17.3 us
  transfers between devices with their start and end apart: 35, of which 26 were waited for; matrix products, arithmetic and copies ran while one was open for 17% of the time, Pallas kernels for 0%

profile of v10, /device:TPU:0, one launch (start us, length us, event | category | flops | bytes accessed | tf_op | source)
XLA Modules:
  0.0 574.1 jit_solution(8732753916524851098)
XLA Ops:
  17.2 13.6 %collective-permute-done.2 = f32[384,384]{1,0:T(8,128)S(1)} collective-permute-done((f32[384,384]{1,0:T(8,128)S(1)}, f32[384,384]{1,0:T(8,128)S(1)}, u32[]{:S(2)}, u32[]{:S(2)}) %collective-permute-start.2) | collective-permute-done | bytes 589856 | tf_op jit(solution)/shard_map/ppermute | solution.py:55
  33.3 41.8 %all-gather.13.cloned.1.call-done = f32[768,1024]{1,0:T(8,128)} async-done(((f32[192,1024]{1,0:T(8,128)}), f32[768,1024]{1,0:T(8,128)}) %all-gather.13.cloned.1.call-update) | async-done | bytes 3145744 | tf_op jit(solution)/shard_map/all_gather | solution.py:33
  77.5 74.4 %all-gather.15.cloned.1.call-done = f32[1536,640]{1,0:T(8,128)} async-done(((f32[384,640]{1,0:T(8,128)}), f32[1536,640]{1,0:T(8,128)}) %all-gather.15.cloned.1.call-update) | async-done | bytes 3932176 | tf_op jit(solution)/shard_map/all_gather | solution.py:33
  174.5 5.5 collective-permute-start.6
  190.1 10.3 %collective-permute-done.6 = f32[384,640]{1,0:T(8,128)} collective-permute-done((f32[384,640]{1,0:T(8,128)S(1)}, f32[384,640]{1,0:T(8,128)}, u32[]{:S(2)}, u32[]{:S(2)}) %collective-permute-start.6) | collective-permute-done | bytes 983072 | tf_op jit(solution)/shard_map/ppermute | solution.py:42
  200.4 5.4 collective-permute-start.8
  206.7 5.4 fusion.96
  213.4 4.7 add_add_fusion.3
  218.2 21.3 %collective-permute-done.8 = f32[384,640]{1,0:T(8,128)} collective-permute-done((f32[384,640]{1,0:T(8,128)}, f32[384,640]{1,0:T(8,128)}, u32[]{:S(2)}, u32[]{:S(2)}) %collective-permute-start.8) | collective-permute-done | bytes 983072 | tf_op jit(solution)/shard_map/ppermute | solution.py:42
  239.5 5.7 collective-permute-start.10
  247.8 7.9 %collective-permute-done.9 = f32[384,640]{1,0:T(8,128)S(1)} collective-permute-done((f32[384,640]{1,0:T(8,128)}, f32[384,640]{1,0:T(8,128)S(1)}, u32[]{:S(2)}, u32[]{:S(2)}) %collective-permute-start.9) | collective-permute-done | bytes 983072 | tf_op jit(solution)/shard_map/ppermute | solution.py:43
  268.1 12.8 %collective-permute-done.11 = f32[384,640]{1,0:T(8,128)} collective-permute-done((f32[384,640]{1,0:T(8,128)S(1)}, f32[384,640]{1,0:T(8,128)}, u32[]{:S(2)}, u32[]{:S(2)}) %collective-permute-start.11) | collective-permute-done | bytes 983072 | tf_op jit(solution)/shard_map/ppermute | solution.py:43
  297.0 5.2 multiply_reduce_fusion.5
  322.2 7.8 %collective-permute-done.15 = f32[200,384]{1,0:T(8,128)S(1)} collective-permute-done((f32[200,384]{1,0:T(8,128)S(1)}, f32[200,384]{1,0:T(8,128)S(1)}, u32[]{:S(2)}, u32[]{:S(2)}) %collective-permute-start.15) | collective-permute-done | bytes 307232 | tf_op jit(solution)/shard_map/ppermute | solution.py:131
  343.5 19.7 %all-gather.19.cloned.1.call-done = f32[768,384]{1,0:T(8,128)} async-done(((f32[192,384]{1,0:T(8,128)}), f32[768,384]{1,0:T(8,128)}) %all-gather.19.cloned.1.call-update) | async-done | bytes 1179664 | tf_op jit(solution)/shard_map/all_gather | solution.py:33
  363.3 5.6 fusion.78
  381.8 5.4 multiply_reduce_fusion.3
  408.0 7.8 %collective-permute-done.20 = f32[200,384]{1,0:T(8,128)S(1)} collective-permute-done((f32[200,384]{1,0:T(8,128)S(1)}, f32[200,384]{1,0:T(8,128)S(1)}, u32[]{:S(2)}, u32[]{:S(2)}) %collective-permute-start.20) | collective-permute-done | bytes 307232 | tf_op jit(solution)/shard_map/ppermute | solution.py:131
  429.1 20.4 %all-gather.21.cloned.1.call-done = f32[768,384]{1,0:T(8,128)} async-done(((f32[192,384]{1,0:T(8,128)}), f32[768,384]{1,0:T(8,128)}) %all-gather.21.cloned.1.call-update) | async-done | bytes 1179664 | tf_op jit(solution)/shard_map/all_gather | solution.py:33
  449.7 5.6 fusion.85
  468.2 5.2 multiply_reduce_fusion.1
  494.0 7.8 %collective-permute-done.25 = f32[200,384]{1,0:T(8,128)S(1)} collective-permute-done((f32[200,384]{1,0:T(8,128)S(1)}, f32[200,384]{1,0:T(8,128)S(1)}, u32[]{:S(2)}, u32[]{:S(2)}) %collective-permute-start.25) | collective-permute-done | bytes 307232 | tf_op jit(solution)/shard_map/ppermute | solution.py:131
  513.4 20.5 %all-gather.23.cloned.1.call-done = f32[768,384]{1,0:T(8,128)} async-done(((f32[192,384]{1,0:T(8,128)}), f32[768,384]{1,0:T(8,128)}) %all-gather.23.cloned.1.call-update) | async-done | bytes 1179664 | tf_op jit(solution)/shard_map/all_gather | solution.py:33
  533.8 5.4 fusion.92
  (273 shorter events, 220.4 us)
Async XLA Ops:
  6.5 68.6 %all-gather.13.cloned.1.call-start = ((), (), s32[]{:S(2)}) async-start(), calls=%async_computation | async-start | bytes 3932160 | tf_op jit(solution)/shard_map/all_gather | solution.py:33
  8.7 143.2 %all-gather.15.cloned.1.call-start = ((), (), s32[]{:S(2)}) async-start(), calls=%async_computation.1 | async-start | bytes 4915200 | tf_op jit(solution)/shard_map/all_gather | solution.py:33
  14.3 16.6 %collective-permute-start.2 = (f32[384,384]{1,0:T(8,128)S(1)}, f32[384,384]{1,0:T(8,128)S(1)}, u32[]{:S(2)}, u32[]{:S(2)}) collective-permute-start(f32[384,384]{1,0:T(8,128)S(1)} %add.366), channel_id=1, source_target_pairs={{0,2},{1,3},{2,0},{3,1},{4,6},{5,7},{6,4},{7,5},{8,10},{9,11},{10,... | collective-permute-start | bytes 1769480 | tf_op jit(solution)/shard_map/ppermute | solution.py:55
  33.1 229.9 %all-gather.17.cloned.1.call-start = ((), (), s32[]{:S(2)}) async-start(), calls=%async_computation.2 | async-start | bytes 1474560 | tf_op jit(solution)/shard_map/all_gather | solution.py:33
  75.2 80.4 %collective-permute-start = (f32[4,192,1024]{2,1,0:T(8,128)}, f32[4,192,1024]{2,1,0:T(8,128)}, u32[]{:S(2)}, u32[]{:S(2)}) collective-permute-start(f32[4,192,1024]{2,1,0:T(8,128)} %bitcast.208), channel_id=1, source_target_pairs={{0,1},{1,0},{2,3},{3,2},{4,5},{5,4},{6,7},{7,6},{8,9},{9,8},{10,11... | collective-permute-start | bytes 9437192 | tf_op jit(solution)/shard_map/ppermute | solution.py:61
  172.6 10.6 %collective-permute-start.3 = (f32[200,384]{1,0:T(8,128)S(1)}, f32[200,384]{1,0:T(8,128)S(1)}, u32[]{:S(2)}, u32[]{:S(2)}) collective-permute-start(f32[200,384]{1,0:T(8,128)S(1)} %concatenate.45), channel_id=1, source_target_pairs={{0,1},{1,0},{2,3},{3,2},{4,5},{5,4},{6,7},{7,6},{8,9},{9,8},{10,11... | collective-permute-start | bytes 921608 | tf_op jit(solution)/shard_map/ppermute | solution.py:128
  172.9 39.2 %collective-permute-start.7 = (f32[384,640]{1,0:T(8,128)S(1)}, f32[384,640]{1,0:T(8,128)}, u32[]{:S(2)}, u32[]{:S(2)}) collective-permute-start(f32[384,640]{1,0:T(8,128)S(1)} %convert_multiply_fusion), channel_id=1, source_target_pairs={{4,0},{8,4},{12,8},{5,1},{9,5},{13,9},{6,2},{10,6},{14,10},{7,3},{... | collective-permute-start | bytes 2949128 | tf_op jit(solution)/shard_map/ppermute | solution.py:43
  174.5 25.9 %collective-permute-start.6 = (f32[384,640]{1,0:T(8,128)S(1)}, f32[384,640]{1,0:T(8,128)}, u32[]{:S(2)}, u32[]{:S(2)}) collective-permute-start(f32[384,640]{1,0:T(8,128)S(1)} %convert_multiply_fusion), channel_id=1, source_target_pairs={{0,4},{4,8},{8,12},{1,5},{5,9},{9,13},{2,6},{6,10},{10,14},{3,7},{... | collective-permute-start | bytes 2949128 | tf_op jit(solution)/shard_map/ppermute | solution.py:42
  183.9 21.9 %collective-permute-start.4 = (f32[200,384]{1,0:T(8,128)S(1)}, f32[200,384]{1,0:T(8,128)S(1)}, u32[]{:S(2)}, u32[]{:S(2)}) collective-permute-start(f32[200,384]{1,0:T(8,128)S(1)} %pad_add_fusion.3), channel_id=1, source_target_pairs={{0,2},{1,3},{2,0},{3,1},{4,6},{5,7},{6,4},{7,5},{8,10},{9,11},{10,... | collective-permute-start | bytes 921608 | tf_op jit(solution)/shard_map/ppermute | solution.py:131
  200.4 39.1 %collective-permute-start.8 = (f32[384,640]{1,0:T(8,128)}, f32[384,640]{1,0:T(8,128)}, u32[]{:S(2)}, u32[]{:S(2)}) collective-permute-start(f32[384,640]{1,0:T(8,128)} %collective-permute-done.6), channel_id=1, source_target_pairs={{0,4},{4,8},{8,12},{1,5},{5,9},{9,13},{2,6},{6,10},{10,14},{3,7},{... | collective-permute-start | bytes 2949128 | tf_op jit(solution)/shard_map/ppermute | solution.py:42
  206.6 156.5 %all-gather.19.cloned.1.call-start = ((), (), s32[]{:S(2)}) async-start(), calls=%async_computation.3 | async-start | bytes 1474560 | tf_op jit(solution)/shard_map/all_gather | solution.py:33
  212.1 43.5 %collective-permute-start.9 = (f32[384,640]{1,0:T(8,128)}, f32[384,640]{1,0:T(8,128)S(1)}, u32[]{:S(2)}, u32[]{:S(2)}) collective-permute-start(f32[384,640]{1,0:T(8,128)} %collective-permute-done.7), channel_id=1, source_target_pairs={{4,0},{8,4},{12,8},{5,1},{9,5},{13,9},{6,2},{10,6},{14,10},{7,3},{... | collective-permute-start | bytes 2949128 | tf_op jit(solution)/shard_map/ppermute | solution.py:43
  239.5 26.3 %collective-permute-start.10 = (f32[384,640]{1,0:T(8,128)}, f32[384,640]{1,0:T(8,128)S(1)}, u32[]{:S(2)}, u32[]{:S(2)}) collective-permute-start(f32[384,640]{1,0:T(8,128)} %collective-permute-done.8), channel_id=1, source_target_pairs={{0,4},{4,8},{8,12},{1,5},{5,9},{9,13},{2,6},{6,10},{10,14},{3,7},{... | collective-permute-start | bytes 2949128 | tf_op jit(solution)/shard_map/ppermute | solution.py:42
  255.6 25.2 %collective-permute-start.11 = (f32[384,640]{1,0:T(8,128)S(1)}, f32[384,640]{1,0:T(8,128)}, u32[]{:S(2)}, u32[]{:S(2)}) collective-permute-start(f32[384,640]{1,0:T(8,128)S(1)} %collective-permute-done.9), channel_id=1, source_target_pairs={{4,0},{8,4},{12,8},{5,1},{9,5},{13,9},{6,2},{10,6},{14,10},{7,3},{... | collective-permute-start | bytes 2949128 | tf_op jit(solution)/shard_map/ppermute | solution.py:43
  263.0 23.0 %collective-permute-start.5 = (f32[4,192,384]{2,1,0:T(8,128)}, f32[4,192,384]{2,1,0:T(8,128)S(1)}, u32[]{:S(2)}, u32[]{:S(2)}) collective-permute-start(f32[4,192,384]{2,1,0:T(8,128)} %bitcast.210), channel_id=1, source_target_pairs={{0,1},{1,0},{2,3},{3,2},{4,5},{5,4},{6,7},{7,6},{8,9},{9,8},{10,11... | collective-permute-start | bytes 3538952 | tf_op jit(solution)/shard_map/ppermute | solution.py:61
  320.7 9.4 %collective-permute-start.15 = (f32[200,384]{1,0:T(8,128)S(1)}, f32[200,384]{1,0:T(8,128)S(1)}, u32[]{:S(2)}, u32[]{:S(2)}) collective-permute-start(f32[200,384]{1,0:T(8,128)S(1)} %pad_add_fusion.2), channel_id=1, source_target_pairs={{0,2},{1,3},{2,0},{3,1},{4,6},{5,7},{6,4},{7,5},{8,10},{9,11},{10,... | collective-permute-start | bytes 921608 | tf_op jit(solution)/shard_map/ppermute | solution.py:131
  334.3 115.3 %all-gather.21.cloned.1.call-start = ((), (), s32[]{:S(2)}) async-start(), calls=%async_computation.4 | async-start | bytes 1474560 | tf_op jit(solution)/shard_map/all_gather | solution.py:33
  363.2 8.6 %collective-permute-start.16 = (f32[4,192,384]{2,1,0:T(8,128)}, f32[4,192,384]{2,1,0:T(8,128)S(1)}, u32[]{:S(2)}, u32[]{:S(2)}) collective-permute-start(f32[4,192,384]{2,1,0:T(8,128)} %bitcast.214), channel_id=1, source_target_pairs={{0,1},{1,0},{2,3},{3,2},{4,5},{5,4},{6,7},{7,6},{8,9},{9,8},{10,11... | collective-permute-start | bytes 3538952 | tf_op jit(solution)/shard_map/ppermute | solution.py:61
  390.3 3.7 collective-permute-start.18
  406.4 9.4 %collective-permute-start.20 = (f32[200,384]{1,0:T(8,128)S(1)}, f32[200,384]{1,0:T(8,128)S(1)}, u32[]{:S(2)}, u32[]{:S(2)}) collective-permute-start(f32[200,384]{1,0:T(8,128)S(1)} %pad_add_fusion.1), channel_id=1, source_target_pairs={{0,2},{1,3},{2,0},{3,1},{4,6},{5,7},{6,4},{7,5},{8,10},{9,11},{10,... | collective-permute-start | bytes 921608 | tf_op jit(solution)/shard_map/ppermute | solution.py:131
  420.1 113.7 %all-gather.23.cloned.1.call-start = ((), (), s32[]{:S(2)}) async-start(), calls=%async_computation.5 | async-start | bytes 1474560 | tf_op jit(solution)/shard_map/all_gather | solution.py:33
  449.6 8.5 %collective-permute-start.21 = (f32[4,192,384]{2,1,0:T(8,128)}, f32[4,192,384]{2,1,0:T(8,128)S(1)}, u32[]{:S(2)}, u32[]{:S(2)}) collective-permute-start(f32[4,192,384]{2,1,0:T(8,128)} %bitcast.216), channel_id=1, source_target_pairs={{0,1},{1,0},{2,3},{3,2},{4,5},{5,4},{6,7},{7,6},{8,9},{9,8},{10,11... | collective-permute-start | bytes 3538952 | tf_op jit(solution)/shard_map/ppermute | solution.py:61
  492.5 9.4 %collective-permute-start.25 = (f32[200,384]{1,0:T(8,128)S(1)}, f32[200,384]{1,0:T(8,128)S(1)}, u32[]{:S(2)}, u32[]{:S(2)}) collective-permute-start(f32[200,384]{1,0:T(8,128)S(1)} %pad_add_fusion), channel_id=1, source_target_pairs={{0,2},{1,3},{2,0},{3,1},{4,6},{5,7},{6,4},{7,5},{8,10},{9,11},{10,... | collective-permute-start | bytes 921608 | tf_op jit(solution)/shard_map/ppermute | solution.py:131
  533.8 8.3 %collective-permute-start.26 = (f32[4,192,384]{2,1,0:T(8,128)}, f32[4,192,384]{2,1,0:T(8,128)S(1)}, u32[]{:S(2)}, u32[]{:S(2)}) collective-permute-start(f32[4,192,384]{2,1,0:T(8,128)} %bitcast.212), channel_id=1, source_target_pairs={{0,1},{1,0},{2,3},{3,2},{4,5},{5,4},{6,7},{7,6},{8,9},{9,8},{10,11... | collective-permute-start | bytes 3538952 | tf_op jit(solution)/shard_map/ppermute | solution.py:61
  (61 other events, 367.4 us)
Sparse Core Ops, SparseCore 0:
  8.9 66.1 all-gather.12
  76.7 75.0 all-gather.14
  206.8 40.1 all-gather.16
  334.5 28.6 all-gather.18
  420.2 29.3 all-gather.20
  504.5 29.3 all-gather.22

commit v11 on v10

--- a/solution.py
+++ b/solution.py
@@ -38,7 +38,13 @@
     me = lax.axis_index("site")
     out = lax.dynamic_update_slice_in_dim(jnp.zeros((sites,) + x.shape, x.dtype), x[None], me, 0)
     right = left = x
-    for step in range(1, sites):
+    steps = sites
+    if sites == 4:
+        far = lax.ppermute(x, "site", [(0, 3), (3, 0)])
+        now = lax.dynamic_index_in_dim(out, 3 - me, 0)
+        out = lax.dynamic_update_slice_in_dim(out, now + far[None], 3 - me, 0)
+        steps = 3
+    for step in range(1, steps):
         right = lax.ppermute(right, "site", [(i, i + 1) for i in range(sites - 1)])
         left = lax.ppermute(left, "site", [(i + 1, i) for i in range(sites - 1)])
         for block, at in ((right, (me - step) % sites), (left, (me + step) % sites)):

time: 578 us -> 565 us (0.978)
  starting transfers between devices: 45.5 us -> 39.5 us
    ppermute x0 -> x1, waiting for transfers between devices: none -> 23.5 us  [line_gather(): far = lax.ppermute(x, 'site', [(0, 3), (3, 0)])]
    ppermute x3 -> x2, waiting for transfers between devices: 32.1 us -> 10.4 us  [line_gather(): right = lax.ppermute(right, 'site', [(i, i + 1) for i in range(sites - 1)])]
    ppermute x3 -> x2, waiting for transfers between devices: 20.7 us -> 0.01 us  [line_gather(): left = lax.ppermute(left, 'site', [(i + 1, i) for i in range(sites - 1)])]
    all_gather x6, waiting for transfers between devices: 177 us -> 188 us  [site_gather(): lax.all_gather(lax.optimization_barrier(x), 'site')]
    ppermute x3 -> x2, starting transfers between devices: 16.7 us -> 9.87 us  [line_gather(): right = lax.ppermute(right, 'site', [(i, i + 1) for i in range(sites - 1)])]
    dynamic_update_slice x6 -> x4, other arithmetic: 14.9 us -> 9.97 us  [line_gather(): out = lax.dynamic_update_slice_in_dim(out, now + block[None], at, 0)]
  transfers between devices with their start and end apart: 35 -> 34, of which waited for: 26 -> 25; matrix products, arithmetic and copies ran while one was open for 17% -> 17% of each run, Pallas kernels for 0% -> 0%
where the time goes in v11:
time: 565 us; the launch traced here: 561 us
  waiting for transfers between devices  276 us (49%)
  matrix products  145 us (26%)
  other arithmetic  52.9 us (9%)
  starting transfers between devices  39.5 us (7%)
  between operations  28.3 us (5%)
  local copies, waits for them, and re-layouts  19.2 us (3%)
    all_gather x6, waiting for transfers between devices, site_gather(): lax.all_gather(lax.optimization_barrier(x), 'site')  188 us
    dot_general x39, matrix products, one(): return jnp.einsum(spec, exact, part, preferred_element_type=f32)  116 us
    dot_general x30, matrix products, one(): return jnp.einsum(spec, part, exact, preferred_element_type=f32)  27.4 us
    ppermute x4, waiting for transfers between devices, pair_sum(): lax.ppermute(part, 'inner', [(i, i ^ bit) for i in range(inner)])  26.5 us
    ppermute x1, waiting for transfers between devices, line_gather(): far = lax.ppermute(x, 'site', [(0, 3), (3, 0)])  23.5 us
    ppermute x10, waiting for transfers between devices, inner_sum(): x = x + lax.ppermute(x, 'inner', [(i, i ^ bit) for i in range(size)])  23.4 us
    ppermute x10, starting transfers between devices, inner_sum(): x = x + lax.ppermute(x, 'inner', [(i, i ^ bit) for i in range(size)])  17.4 us
    reduce_sum x3, other arithmetic, per_device(): jnp.sum(residual * residual)  11.4 us
  transfers between devices with their start and end apart: 34, of which 25 were waited for; matrix products, arithmetic and copies ran while one was open for 17% of the time, Pallas kernels for 0%

profile of v11, /device:TPU:0, one launch (start us, length us, event | category | flops | bytes accessed | tf_op | source)
XLA Modules:
  0.0 561.3 jit_solution(14532872456709356016)
XLA Ops:
  17.2 13.6 %collective-permute-done.2 = f32[384,384]{1,0:T(8,128)S(1)} collective-permute-done((f32[384,384]{1,0:T(8,128)S(1)}, f32[384,384]{1,0:T(8,128)S(1)}, u32[]{:S(2)}, u32[]{:S(2)}) %collective-permute-start.2) | collective-permute-done | bytes 589856 | tf_op jit(solution)/shard_map/ppermute | solution.py:61
  33.4 41.8 %all-gather.13.cloned.1.call-done = f32[768,1024]{1,0:T(8,128)} async-done(((f32[192,1024]{1,0:T(8,128)}), f32[768,1024]{1,0:T(8,128)}) %all-gather.13.cloned.1.call-update) | async-done | bytes 3145744 | tf_op jit(solution)/shard_map/all_gather | solution.py:33
  77.5 74.4 %all-gather.15.cloned.1.call-done = f32[1536,640]{1,0:T(8,128)} async-done(((f32[384,640]{1,0:T(8,128)}), f32[1536,640]{1,0:T(8,128)}) %all-gather.15.cloned.1.call-update) | async-done | bytes 3932176 | tf_op jit(solution)/shard_map/all_gather | solution.py:33
  174.4 5.5 collective-permute-start.7
  187.4 4.6 fusion.94
  195.9 5.4 fusion.96
  205.7 4.7 add_add_fusion.3
  212.1 23.5 %collective-permute-done.6 = f32[384,640]{1,0:T(8,128)} collective-permute-done((f32[384,640]{1,0:T(8,128)S(1)}, f32[384,640]{1,0:T(8,128)}, u32[]{:S(2)}, u32[]{:S(2)}) %collective-permute-start.6) | collective-permute-done | bytes 983072 | tf_op jit(solution)/shard_map/ppermute | solution.py:43
  240.7 7.2 %all-gather.17.cloned.1.call-done = f32[768,384]{1,0:T(8,128)} async-done(((f32[192,384]{1,0:T(8,128)}), f32[768,384]{1,0:T(8,128)}) %all-gather.17.cloned.1.call-update) | async-done | bytes 1179664 | tf_op jit(solution)/shard_map/all_gather | solution.py:33
  251.2 10.4 %collective-permute-done.9 = f32[384,640]{1,0:T(8,128)S(1)} collective-permute-done((f32[384,640]{1,0:T(8,128)}, f32[384,640]{1,0:T(8,128)S(1)}, u32[]{:S(2)}, u32[]{:S(2)}) %collective-permute-start.9) | collective-permute-done | bytes 983072 | tf_op jit(solution)/shard_map/ppermute | solution.py:48
  279.9 5.2 multiply_reduce_fusion.5
  305.5 7.8 %collective-permute-done.14 = f32[200,384]{1,0:T(8,128)S(1)} collective-permute-done((f32[200,384]{1,0:T(8,128)S(1)}, f32[200,384]{1,0:T(8,128)S(1)}, u32[]{:S(2)}, u32[]{:S(2)}) %collective-permute-start.14) | collective-permute-done | bytes 307232 | tf_op jit(solution)/shard_map/ppermute | solution.py:137
  326.7 23.4 %all-gather.19.cloned.1.call-done = f32[768,384]{1,0:T(8,128)} async-done(((f32[192,384]{1,0:T(8,128)}), f32[768,384]{1,0:T(8,128)}) %all-gather.19.cloned.1.call-update) | async-done | bytes 1179664 | tf_op jit(solution)/shard_map/all_gather | solution.py:33
  350.2 5.6 %fusion.78 = f32[4,384,640]{2,1,0:T(8,128)S(1)} fusion(f32[1024,640]{1,0:T(8,128)} %copy-done.12, bf16[4,192,1024]{2,1,0:T(8,128)(2,1)} %copy-done.30, bf16[4,192,1024]{2,1,0:T(8,128)(2,1)} %copy-done.21), kind=kOutput, calls=%fused_computation.183 | convolution fusion | flops 2022178816 | bytes 9699328 | tf_op jit(solution)/shard_map/std,dc->stc/dot_general | solution.py:26
  368.8 5.4 multiply_reduce_fusion.3
  394.9 7.9 %collective-permute-done.19 = f32[200,384]{1,0:T(8,128)S(1)} collective-permute-done((f32[200,384]{1,0:T(8,128)S(1)}, f32[200,384]{1,0:T(8,128)S(1)}, u32[]{:S(2)}, u32[]{:S(2)}) %collective-permute-start.19) | collective-permute-done | bytes 307232 | tf_op jit(solution)/shard_map/ppermute | solution.py:137
  411.4 4.6 fusion.66
  416.0 20.4 %all-gather.21.cloned.1.call-done = f32[768,384]{1,0:T(8,128)} async-done(((f32[192,384]{1,0:T(8,128)}), f32[768,384]{1,0:T(8,128)}) %all-gather.21.cloned.1.call-update) | async-done | bytes 1179664 | tf_op jit(solution)/shard_map/all_gather | solution.py:33
  436.5 5.6 fusion.85
  455.0 5.1 multiply_reduce_fusion.1
  481.1 7.8 %collective-permute-done.24 = f32[200,384]{1,0:T(8,128)S(1)} collective-permute-done((f32[200,384]{1,0:T(8,128)S(1)}, f32[200,384]{1,0:T(8,128)S(1)}, u32[]{:S(2)}, u32[]{:S(2)}) %collective-permute-start.24) | collective-permute-done | bytes 307232 | tf_op jit(solution)/shard_map/ppermute | solution.py:137
  496.0 4.6 fusion.62
  500.5 20.4 %all-gather.23.cloned.1.call-done = f32[768,384]{1,0:T(8,128)} async-done(((f32[192,384]{1,0:T(8,128)}), f32[768,384]{1,0:T(8,128)}) %all-gather.23.cloned.1.call-update) | async-done | bytes 1179664 | tf_op jit(solution)/shard_map/all_gather | solution.py:33
  521.0 5.4 fusion.92
  (270 shorter events, 212.5 us)
Async XLA Ops:
  6.5 68.6 %all-gather.13.cloned.1.call-start = ((), (), s32[]{:S(2)}) async-start(), calls=%async_computation | async-start | bytes 3932160 | tf_op jit(solution)/shard_map/all_gather | solution.py:33
  8.7 143.2 %all-gather.15.cloned.1.call-start = ((), (), s32[]{:S(2)}) async-start(), calls=%async_computation.1 | async-start | bytes 4915200 | tf_op jit(solution)/shard_map/all_gather | solution.py:33
  14.3 16.6 %collective-permute-start.2 = (f32[384,384]{1,0:T(8,128)S(1)}, f32[384,384]{1,0:T(8,128)S(1)}, u32[]{:S(2)}, u32[]{:S(2)}) collective-permute-start(f32[384,384]{1,0:T(8,128)S(1)} %add.350), channel_id=1, source_target_pairs={{0,2},{1,3},{2,0},{3,1},{4,6},{5,7},{6,4},{7,5},{8,10},{9,11},{10,... | collective-permute-start | bytes 1769480 | tf_op jit(solution)/shard_map/ppermute | solution.py:61
  33.1 214.8 %all-gather.17.cloned.1.call-start = ((), (), s32[]{:S(2)}) async-start(), calls=%async_computation.2 | async-start | bytes 1474560 | tf_op jit(solution)/shard_map/all_gather | solution.py:33
  75.2 80.4 %collective-permute-start = (f32[4,192,1024]{2,1,0:T(8,128)}, f32[4,192,1024]{2,1,0:T(8,128)}, u32[]{:S(2)}, u32[]{:S(2)}) collective-permute-start(f32[4,192,1024]{2,1,0:T(8,128)} %bitcast.204), channel_id=1, source_target_pairs={{0,1},{1,0},{2,3},{3,2},{4,5},{5,4},{6,7},{7,6},{8,9},{9,8},{10,11... | collective-permute-start | bytes 9437192 | tf_op jit(solution)/shard_map/ppermute | solution.py:67
  172.6 12.5 %collective-permute-start.3 = (f32[200,384]{1,0:T(8,128)S(1)}, f32[200,384]{1,0:T(8,128)S(1)}, u32[]{:S(2)}, u32[]{:S(2)}) collective-permute-start(f32[200,384]{1,0:T(8,128)S(1)} %concatenate.45), channel_id=1, source_target_pairs={{0,1},{1,0},{2,3},{3,2},{4,5},{5,4},{6,7},{7,6},{8,9},{9,8},{10,11... | collective-permute-start | bytes 921608 | tf_op jit(solution)/shard_map/ppermute | solution.py:134
  172.9 37.5 %collective-permute-start.8 = (f32[384,640]{1,0:T(8,128)S(1)}, f32[384,640]{1,0:T(8,128)}, u32[]{:S(2)}, u32[]{:S(2)}) collective-permute-start(f32[384,640]{1,0:T(8,128)S(1)} %convert_multiply_fusion), channel_id=1, source_target_pairs={{4,0},{8,4},{12,8},{5,1},{9,5},{13,9},{6,2},{10,6},{14,10},{7,3},{... | collective-permute-start | bytes 2949128 | tf_op jit(solution)/shard_map/ppermute | solution.py:49
  174.4 26.8 %collective-permute-start.7 = (f32[384,640]{1,0:T(8,128)S(1)}, f32[384,640]{1,0:T(8,128)}, u32[]{:S(2)}, u32[]{:S(2)}) collective-permute-start(f32[384,640]{1,0:T(8,128)S(1)} %convert_multiply_fusion), channel_id=1, source_target_pairs={{0,4},{4,8},{8,12},{1,5},{5,9},{9,13},{2,6},{6,10},{10,14},{3,7},{... | collective-permute-start | bytes 2949128 | tf_op jit(solution)/shard_map/ppermute | solution.py:48
  180.0 55.6 %collective-permute-start.6 = (f32[384,640]{1,0:T(8,128)S(1)}, f32[384,640]{1,0:T(8,128)}, u32[]{:S(2)}, u32[]{:S(2)}) collective-permute-start(f32[384,640]{1,0:T(8,128)S(1)} %convert_multiply_fusion), channel_id=1, source_target_pairs={{0,12},{12,0},{1,13},{13,1},{2,14},{14,2},{3,15},{15,3},{16,28},{2... | collective-permute-start | bytes 2949128 | tf_op jit(solution)/shard_map/ppermute | solution.py:43
  185.8 9.2 %collective-permute-start.4 = (f32[200,384]{1,0:T(8,128)S(1)}, f32[200,384]{1,0:T(8,128)S(1)}, u32[]{:S(2)}, u32[]{:S(2)}) collective-permute-start(f32[200,384]{1,0:T(8,128)S(1)} %pad_add_fusion.3), channel_id=1, source_target_pairs={{0,2},{1,3},{2,0},{3,1},{4,6},{5,7},{6,4},{7,5},{8,10},{9,11},{10,... | collective-permute-start | bytes 921608 | tf_op jit(solution)/shard_map/ppermute | solution.py:137
  195.8 154.3 %all-gather.19.cloned.1.call-start = ((), (), s32[]{:S(2)}) async-start(), calls=%async_computation.3 | async-start | bytes 1474560 | tf_op jit(solution)/shard_map/all_gather | solution.py:33
  201.3 60.3 %collective-permute-start.9 = (f32[384,640]{1,0:T(8,128)}, f32[384,640]{1,0:T(8,128)S(1)}, u32[]{:S(2)}, u32[]{:S(2)}) collective-permute-start(f32[384,640]{1,0:T(8,128)} %collective-permute-done.7), channel_id=1, source_target_pairs={{0,4},{4,8},{8,12},{1,5},{5,9},{9,13},{2,6},{6,10},{10,14},{3,7},{... | collective-permute-start | bytes 2949128 | tf_op jit(solution)/shard_map/ppermute | solution.py:48
  210.4 53.5 %collective-permute-start.10 = (f32[384,640]{1,0:T(8,128)}, f32[384,640]{1,0:T(8,128)}, u32[]{:S(2)}, u32[]{:S(2)}) collective-permute-start(f32[384,640]{1,0:T(8,128)} %collective-permute-done.8), channel_id=1, source_target_pairs={{4,0},{8,4},{12,8},{5,1},{9,5},{13,9},{6,2},{10,6},{14,10},{7,3},{... | collective-permute-start | bytes 2949128 | tf_op jit(solution)/shard_map/ppermute | solution.py:49
  248.0 21.0 %collective-permute-start.5 = (f32[4,192,384]{2,1,0:T(8,128)}, f32[4,192,384]{2,1,0:T(8,128)S(1)}, u32[]{:S(2)}, u32[]{:S(2)}) collective-permute-start(f32[4,192,384]{2,1,0:T(8,128)} %bitcast.206), channel_id=1, source_target_pairs={{0,1},{1,0},{2,3},{3,2},{4,5},{5,4},{6,7},{7,6},{8,9},{9,8},{10,11... | collective-permute-start | bytes 3538952 | tf_op jit(solution)/shard_map/ppermute | solution.py:67
  287.8 3.7 collective-permute-start.12
  303.9 9.4 %collective-permute-start.14 = (f32[200,384]{1,0:T(8,128)S(1)}, f32[200,384]{1,0:T(8,128)S(1)}, u32[]{:S(2)}, u32[]{:S(2)}) collective-permute-start(f32[200,384]{1,0:T(8,128)S(1)} %pad_add_fusion.2), channel_id=1, source_target_pairs={{0,2},{1,3},{2,0},{3,1},{4,6},{5,7},{6,4},{7,5},{8,10},{9,11},{10,... | collective-permute-start | bytes 921608 | tf_op jit(solution)/shard_map/ppermute | solution.py:137
  317.6 118.8 %all-gather.21.cloned.1.call-start = ((), (), s32[]{:S(2)}) async-start(), calls=%async_computation.4 | async-start | bytes 1474560 | tf_op jit(solution)/shard_map/all_gather | solution.py:33
  350.1 8.6 %collective-permute-start.15 = (f32[4,192,384]{2,1,0:T(8,128)}, f32[4,192,384]{2,1,0:T(8,128)S(1)}, u32[]{:S(2)}, u32[]{:S(2)}) collective-permute-start(f32[4,192,384]{2,1,0:T(8,128)} %bitcast.210), channel_id=1, source_target_pairs={{0,1},{1,0},{2,3},{3,2},{4,5},{5,4},{6,7},{7,6},{8,9},{9,8},{10,11... | collective-permute-start | bytes 3538952 | tf_op jit(solution)/shard_map/ppermute | solution.py:67
  377.3 3.7 collective-permute-start.17
  393.4 9.4 %collective-permute-start.19 = (f32[200,384]{1,0:T(8,128)S(1)}, f32[200,384]{1,0:T(8,128)S(1)}, u32[]{:S(2)}, u32[]{:S(2)}) collective-permute-start(f32[200,384]{1,0:T(8,128)S(1)} %pad_add_fusion.1), channel_id=1, source_target_pairs={{0,2},{1,3},{2,0},{3,1},{4,6},{5,7},{6,4},{7,5},{8,10},{9,11},{10,... | collective-permute-start | bytes 921608 | tf_op jit(solution)/shard_map/ppermute | solution.py:137
  407.0 114.0 %all-gather.23.cloned.1.call-start = ((), (), s32[]{:S(2)}) async-start(), calls=%async_computation.5 | async-start | bytes 1474560 | tf_op jit(solution)/shard_map/all_gather | solution.py:33
  436.4 8.5 %collective-permute-start.20 = (f32[4,192,384]{2,1,0:T(8,128)}, f32[4,192,384]{2,1,0:T(8,128)S(1)}, u32[]{:S(2)}, u32[]{:S(2)}) collective-permute-start(f32[4,192,384]{2,1,0:T(8,128)} %bitcast.212), channel_id=1, source_target_pairs={{0,1},{1,0},{2,3},{3,2},{4,5},{5,4},{6,7},{7,6},{8,9},{9,8},{10,11... | collective-permute-start | bytes 3538952 | tf_op jit(solution)/shard_map/ppermute | solution.py:67
  479.5 9.4 %collective-permute-start.24 = (f32[200,384]{1,0:T(8,128)S(1)}, f32[200,384]{1,0:T(8,128)S(1)}, u32[]{:S(2)}, u32[]{:S(2)}) collective-permute-start(f32[200,384]{1,0:T(8,128)S(1)} %pad_add_fusion), channel_id=1, source_target_pairs={{0,2},{1,3},{2,0},{3,1},{4,6},{5,7},{6,4},{7,5},{8,10},{9,11},{10,... | collective-permute-start | bytes 921608 | tf_op jit(solution)/shard_map/ppermute | solution.py:137
  521.0 8.3 %collective-permute-start.25 = (f32[4,192,384]{2,1,0:T(8,128)}, f32[4,192,384]{2,1,0:T(8,128)S(1)}, u32[]{:S(2)}, u32[]{:S(2)}) collective-permute-start(f32[4,192,384]{2,1,0:T(8,128)} %bitcast.208), channel_id=1, source_target_pairs={{0,1},{1,0},{2,3},{3,2},{4,5},{5,4},{6,7},{7,6},{8,9},{9,8},{10,11... | collective-permute-start | bytes 3538952 | tf_op jit(solution)/shard_map/ppermute | solution.py:67
  (60 other events, 382.3 us)
Sparse Core Ops, SparseCore 0:
  8.9 66.1 all-gather.12
  76.7 75.0 all-gather.14
  195.9 51.9 all-gather.16
  317.7 32.3 all-gather.18
  407.1 29.2 all-gather.20
  491.6 29.2 all-gather.22

commit v12 on v11

--- a/solution.py
+++ b/solution.py
@@ -141,6 +141,8 @@
     def pair_spread(pair_part):
         if not split:
             return site_gather(pair_part)
+        if sites <= 4:
+            return halves(line_gather(pair_part))
         return halves(site_gather(pair_part))
 
     def apply_operator(pair_part, direction):

time: 565 us -> 548 us (0.970)
  starting transfers between devices: 39.5 us -> 86.9 us
  waiting for transfers between devices: 276 us -> 254 us
  matrix products: 145 us -> 125 us
  other arithmetic: 52.9 us -> 37.4 us
  local copies, waits for them, and re-layouts: 19.2 us -> 9.98 us
    all_gather x6 -> x2, waiting for transfers between devices: 188 us -> 115 us  [site_gather(): lax.all_gather(lax.optimization_barrier(x), 'site')]
    ppermute x2 -> x10, waiting for transfers between devices: 10.4 us -> 67.3 us  [line_gather(): right = lax.ppermute(right, 'site', [(i, i + 1) for i in range(sites - 1)])]
    ppermute x1 -> x5, waiting for transfers between devices: 23.5 us -> 0.01 us  [line_gather(): far = lax.ppermute(x, 'site', [(0, 3), (3, 0)])]
    dot_general x39, matrix products: 116 us -> 95.3 us  [one(): return jnp.einsum(spec, exact, part, preferred_element_type=f32)]
    ppermute x2 -> x10, waiting for transfers between devices: 0.01 us -> 19.8 us  [line_gather(): left = lax.ppermute(left, 'site', [(i + 1, i) for i in range(sites - 1)])]
    ppermute x2 -> x10, starting transfers between devices: 9.87 us -> 28.6 us  [line_gather(): right = lax.ppermute(right, 'site', [(i, i + 1) for i in range(sites - 1)])]
    ppermute x1 -> x5, starting transfers between devices: 1.91 us -> 19.9 us  [line_gather(): far = lax.ppermute(x, 'site', [(0, 3), (3, 0)])]
    ppermute x2 -> x10, starting transfers between devices: 3.24 us -> 14.3 us  [line_gather(): left = lax.ppermute(left, 'site', [(i + 1, i) for i in range(sites - 1)])]
  transfers between devices with their start and end apart: 34 -> 50, of which waited for: 25 -> 32; matrix products, arithmetic and copies ran while one was open for 17% -> 12% of each run, Pallas kernels for 0% -> 0%
where the time goes in v12:
time: 548 us; the launch traced here: 542 us
  waiting for transfers between devices  254 us (46%)
  matrix products  125 us (23%)
  starting transfers between devices  86.9 us (16%)
  other arithmetic  37.4 us (7%)
  between operations  29.6 us (5%)
  local copies, waits for them, and re-layouts  9.98 us (2%)
    all_gather x2, waiting for transfers between devices, site_gather(): lax.all_gather(lax.optimization_barrier(x), 'site')  115 us
    dot_general x39, matrix products, one(): return jnp.einsum(spec, exact, part, preferred_element_type=f32)  95.3 us
    ppermute x10, waiting for transfers between devices, line_gather(): right = lax.ppermute(right, 'site', [(i, i + 1) for i in range(sites - 1)])  67.3 us
    ppermute x10, starting transfers between devices, line_gather(): right = lax.ppermute(right, 'site', [(i, i + 1) for i in range(sites - 1)])  28.6 us
    dot_general x30, matrix products, one(): return jnp.einsum(spec, part, exact, preferred_element_type=f32)  27.4 us
    ppermute x4, waiting for transfers between devices, pair_sum(): lax.ppermute(part, 'inner', [(i, i ^ bit) for i in range(inner)])  23.3 us
    ppermute x10, waiting for transfers between devices, inner_sum(): x = x + lax.ppermute(x, 'inner', [(i, i ^ bit) for i in range(size)])  22.1 us
    ppermute x5, starting transfers between devices, line_gather(): far = lax.ppermute(x, 'site', [(0, 3), (3, 0)])  19.9 us
  transfers between devices with their start and end apart: 50, of which 32 were waited for; matrix products, arithmetic and copies ran while one was open for 12% of the time, Pallas kernels for 0%

profile of v12, /device:TPU:0, one launch (start us, length us, event | category | flops | bytes accessed | tf_op | source)
XLA Modules:
  0.0 542.3 jit_solution(16236885198975182575)
XLA Ops:
  17.2 13.6 %collective-permute-done.2 = f32[384,384]{1,0:T(8,128)S(1)} collective-permute-done((f32[384,384]{1,0:T(8,128)S(1)}, f32[384,384]{1,0:T(8,128)S(1)}, u32[]{:S(2)}, u32[]{:S(2)}) %collective-permute-start.2) | collective-permute-done | bytes 589856 | tf_op jit(solution)/shard_map/ppermute | solution.py:61
  33.2 42.0 %all-gather.5.cloned.1.call-done = f32[768,1024]{1,0:T(8,128)} async-done(((f32[192,1024]{1,0:T(8,128)}), f32[768,1024]{1,0:T(8,128)}) %all-gather.5.cloned.1.call-update) | async-done | bytes 3145744 | tf_op jit(solution)/shard_map/all_gather | solution.py:33
  78.7 73.2 %all-gather.7.cloned.1.call-done = f32[1536,640]{1,0:T(8,128)} async-done(((f32[384,640]{1,0:T(8,128)}), f32[1536,640]{1,0:T(8,128)}) %all-gather.7.cloned.1.call-update) | async-done | bytes 3932176 | tf_op jit(solution)/shard_map/all_gather | solution.py:33
  189.5 11.0 %collective-permute-done.12 = f32[384,640]{1,0:T(8,128)S(1)} collective-permute-done((f32[384,640]{1,0:T(8,128)S(1)}, f32[384,640]{1,0:T(8,128)S(1)}, u32[]{:S(2)}, u32[]{:S(2)}) %collective-permute-start.12) | collective-permute-done | bytes 983072 | tf_op jit(solution)/shard_map/ppermute | solution.py:48
  200.5 4.4 collective-permute-start.14
  206.5 6.4 %collective-permute-start.5 = (f32[192,384]{1,0:T(8,128)S(1)}, f32[192,384]{1,0:T(8,128)S(1)}, u32[]{:S(2)}, u32[]{:S(2)}) collective-permute-start(f32[192,384]{1,0:T(8,128)S(1)} %slice.43), channel_id=1, source_target_pairs={{0,12},{12,0},{1,13},{13,1},{2,14},{14,2},{3,15},{15,3},{16,28},{2... | collective-permute-start | bytes 884744 | tf_op jit(solution)/shard_map/ppermute | solution.py:43
  215.8 22.2 %collective-permute-done.6 = f32[192,384]{1,0:T(8,128)S(1)} collective-permute-done((f32[192,384]{1,0:T(8,128)S(1)}, f32[192,384]{1,0:T(8,128)S(1)}, u32[]{:S(2)}, u32[]{:S(2)}) %collective-permute-start.6) | collective-permute-done | bytes 294944 | tf_op jit(solution)/shard_map/ppermute | solution.py:48
  237.9 4.4 collective-permute-start.8
  247.5 5.0 collective-permute-done.9
  265.5 5.2 multiply_reduce_fusion.5
  290.9 8.0 %collective-permute-done.19 = f32[200,384]{1,0:T(8,128)S(1)} collective-permute-done((f32[200,384]{1,0:T(8,128)S(1)}, f32[200,384]{1,0:T(8,128)S(1)}, u32[]{:S(2)}, u32[]{:S(2)}) %collective-permute-start.19) | collective-permute-done | bytes 307232 | tf_op jit(solution)/shard_map/ppermute | solution.py:137
  313.8 6.7 %collective-permute-done.21 = f32[192,384]{1,0:T(8,128)S(1)} collective-permute-done((f32[192,384]{1,0:T(8,128)S(1)}, f32[192,384]{1,0:T(8,128)S(1)}, u32[]{:S(2)}, u32[]{:S(2)}) %collective-permute-start.21) | collective-permute-done | bytes 294944 | tf_op jit(solution)/shard_map/ppermute | solution.py:48
  320.6 4.4 collective-permute-start.23
  330.3 5.0 collective-permute-done.24
  351.1 5.1 multiply_reduce_fusion.3
  377.0 7.6 %collective-permute-done.29 = f32[200,384]{1,0:T(8,128)S(1)} collective-permute-done((f32[200,384]{1,0:T(8,128)S(1)}, f32[200,384]{1,0:T(8,128)S(1)}, u32[]{:S(2)}, u32[]{:S(2)}) %collective-permute-start.29) | collective-permute-done | bytes 307232 | tf_op jit(solution)/shard_map/ppermute | solution.py:137
  398.6 6.7 %collective-permute-done.31 = f32[192,384]{1,0:T(8,128)S(1)} collective-permute-done((f32[192,384]{1,0:T(8,128)S(1)}, f32[192,384]{1,0:T(8,128)S(1)}, u32[]{:S(2)}, u32[]{:S(2)}) %collective-permute-start.31) | collective-permute-done | bytes 294944 | tf_op jit(solution)/shard_map/ppermute | solution.py:48
  405.4 4.4 collective-permute-start.33
  415.1 5.0 collective-permute-done.34
  435.9 5.1 multiply_reduce_fusion.1
  461.7 7.7 %collective-permute-done.39 = f32[200,384]{1,0:T(8,128)S(1)} collective-permute-done((f32[200,384]{1,0:T(8,128)S(1)}, f32[200,384]{1,0:T(8,128)S(1)}, u32[]{:S(2)}, u32[]{:S(2)}) %collective-permute-start.39) | collective-permute-done | bytes 307232 | tf_op jit(solution)/shard_map/ppermute | solution.py:137
  483.4 6.7 %collective-permute-done.41 = f32[192,384]{1,0:T(8,128)S(1)} collective-permute-done((f32[192,384]{1,0:T(8,128)S(1)}, f32[192,384]{1,0:T(8,128)S(1)}, u32[]{:S(2)}, u32[]{:S(2)}) %collective-permute-start.41) | collective-permute-done | bytes 294944 | tf_op jit(solution)/shard_map/ppermute | solution.py:48
  490.2 4.4 collective-permute-start.43
  499.9 5.0 collective-permute-done.44
  (275 shorter events, 243.7 us)
Async XLA Ops:
  6.5 68.6 %all-gather.5.cloned.1.call-start = ((), (), s32[]{:S(2)}) async-start(), calls=%async_computation | async-start | bytes 3932160 | tf_op jit(solution)/shard_map/all_gather | solution.py:33
  8.7 143.1 %all-gather.7.cloned.1.call-start = ((), (), s32[]{:S(2)}) async-start(), calls=%async_computation.1 | async-start | bytes 4915200 | tf_op jit(solution)/shard_map/all_gather | solution.py:33
  14.3 16.6 %collective-permute-start.2 = (f32[384,384]{1,0:T(8,128)S(1)}, f32[384,384]{1,0:T(8,128)S(1)}, u32[]{:S(2)}, u32[]{:S(2)}) collective-permute-start(f32[384,384]{1,0:T(8,128)S(1)} %add.479), channel_id=1, source_target_pairs={{0,2},{1,3},{2,0},{3,1},{4,6},{5,7},{6,4},{7,5},{8,10},{9,11},{10,... | collective-permute-start | bytes 1769480 | tf_op jit(solution)/shard_map/ppermute | solution.py:61
  75.2 86.2 %collective-permute-start = (f32[4,192,1024]{2,1,0:T(8,128)}, f32[4,192,1024]{2,1,0:T(8,128)}, u32[]{:S(2)}, u32[]{:S(2)}) collective-permute-start(f32[4,192,1024]{2,1,0:T(8,128)} %bitcast.288), channel_id=1, source_target_pairs={{0,1},{1,0},{2,3},{3,2},{4,5},{5,4},{6,7},{7,6},{8,9},{9,8},{10,11... | collective-permute-start | bytes 9437192 | tf_op jit(solution)/shard_map/ppermute | solution.py:67
  155.6 50.7 %collective-permute-start.11 = (f32[384,640]{1,0:T(8,128)S(1)}, f32[384,640]{1,0:T(8,128)S(1)}, u32[]{:S(2)}, u32[]{:S(2)}) collective-permute-start(f32[384,640]{1,0:T(8,128)S(1)} %convert_multiply_fusion), channel_id=1, source_target_pairs={{0,12},{12,0},{1,13},{13,1},{2,14},{14,2},{3,15},{15,3},{16,28},{2... | collective-permute-start | bytes 2949128 | tf_op jit(solution)/shard_map/ppermute | solution.py:43
  158.1 42.4 %collective-permute-start.12 = (f32[384,640]{1,0:T(8,128)S(1)}, f32[384,640]{1,0:T(8,128)S(1)}, u32[]{:S(2)}, u32[]{:S(2)}) collective-permute-start(f32[384,640]{1,0:T(8,128)S(1)} %convert_multiply_fusion), channel_id=1, source_target_pairs={{0,4},{4,8},{8,12},{1,5},{5,9},{9,13},{2,6},{6,10},{10,14},{3,7},{... | collective-permute-start | bytes 2949128 | tf_op jit(solution)/shard_map/ppermute | solution.py:48
  159.5 45.5 %collective-permute-start.13 = (f32[384,640]{1,0:T(8,128)S(1)}, f32[384,640]{1,0:T(8,128)S(1)}, u32[]{:S(2)}, u32[]{:S(2)}) collective-permute-start(f32[384,640]{1,0:T(8,128)S(1)} %convert_multiply_fusion), channel_id=1, source_target_pairs={{4,0},{8,4},{12,8},{5,1},{9,5},{13,9},{6,2},{10,6},{14,10},{7,3},{... | collective-permute-start | bytes 2949128 | tf_op jit(solution)/shard_map/ppermute | solution.py:49
  184.9 21.5 %collective-permute-start.4 = (f32[200,384]{1,0:T(8,128)S(1)}, f32[200,384]{1,0:T(8,128)S(1)}, u32[]{:S(2)}, u32[]{:S(2)}) collective-permute-start(f32[200,384]{1,0:T(8,128)S(1)} %pad_add_fusion.3), channel_id=1, source_target_pairs={{0,2},{1,3},{2,0},{3,1},{4,6},{5,7},{6,4},{7,5},{8,10},{9,11},{10,... | collective-permute-start | bytes 921608 | tf_op jit(solution)/shard_map/ppermute | solution.py:137
  200.5 52.8 %collective-permute-start.14 = (f32[384,640]{1,0:T(8,128)S(1)}, f32[384,640]{1,0:T(8,128)S(1)}, u32[]{:S(2)}, u32[]{:S(2)}) collective-permute-start(f32[384,640]{1,0:T(8,128)S(1)} %collective-permute-done.12), channel_id=1, source_target_pairs={{0,4},{4,8},{8,12},{1,5},{5,9},{9,13},{2,6},{6,10},{10,14},{3,7},{... | collective-permute-start | bytes 2949128 | tf_op jit(solution)/shard_map/ppermute | solution.py:48
  204.9 48.5 %collective-permute-start.15 = (f32[384,640]{1,0:T(8,128)S(1)}, f32[384,640]{1,0:T(8,128)S(1)}, u32[]{:S(2)}, u32[]{:S(2)}) collective-permute-start(f32[384,640]{1,0:T(8,128)S(1)} %collective-permute-done.13), channel_id=1, source_target_pairs={{4,0},{8,4},{12,8},{5,1},{9,5},{13,9},{6,2},{10,6},{14,10},{7,3},{... | collective-permute-start | bytes 2949128 | tf_op jit(solution)/shard_map/ppermute | solution.py:49
  206.5 35.8 %collective-permute-start.5 = (f32[192,384]{1,0:T(8,128)S(1)}, f32[192,384]{1,0:T(8,128)S(1)}, u32[]{:S(2)}, u32[]{:S(2)}) collective-permute-start(f32[192,384]{1,0:T(8,128)S(1)} %slice.43), channel_id=1, source_target_pairs={{0,12},{12,0},{1,13},{13,1},{2,14},{14,2},{3,15},{15,3},{16,28},{2... | collective-permute-start | bytes 884744 | tf_op jit(solution)/shard_map/ppermute | solution.py:43
  212.9 25.1 %collective-permute-start.6 = (f32[192,384]{1,0:T(8,128)S(1)}, f32[192,384]{1,0:T(8,128)S(1)}, u32[]{:S(2)}, u32[]{:S(2)}) collective-permute-start(f32[192,384]{1,0:T(8,128)S(1)} %slice.43), channel_id=1, source_target_pairs={{0,4},{4,8},{8,12},{1,5},{5,9},{9,13},{2,6},{6,10},{10,14},{3,7},{... | collective-permute-start | bytes 884744 | tf_op jit(solution)/shard_map/ppermute | solution.py:48
  214.3 28.1 %collective-permute-start.7 = (f32[192,384]{1,0:T(8,128)S(1)}, f32[192,384]{1,0:T(8,128)S(1)}, u32[]{:S(2)}, u32[]{:S(2)}) collective-permute-start(f32[192,384]{1,0:T(8,128)S(1)} %slice.43), channel_id=1, source_target_pairs={{4,0},{8,4},{12,8},{5,1},{9,5},{13,9},{6,2},{10,6},{14,10},{7,3},{... | collective-permute-start | bytes 884744 | tf_op jit(solution)/shard_map/ppermute | solution.py:49
  304.7 20.3 %collective-permute-start.20 = (f32[192,384]{1,0:T(8,128)S(1)}, f32[192,384]{1,0:T(8,128)S(1)}, u32[]{:S(2)}, u32[]{:S(2)}) collective-permute-start(f32[192,384]{1,0:T(8,128)S(1)} %get-tuple-element.32), channel_id=1, source_target_pairs={{0,12},{12,0},{1,13},{13,1},{2,14},{14,2},{3,15},{15,3},{16,28},{2... | collective-permute-start | bytes 884744 | tf_op jit(solution)/shard_map/ppermute | solution.py:43
  308.4 12.1 %collective-permute-start.21 = (f32[192,384]{1,0:T(8,128)S(1)}, f32[192,384]{1,0:T(8,128)S(1)}, u32[]{:S(2)}, u32[]{:S(2)}) collective-permute-start(f32[192,384]{1,0:T(8,128)S(1)} %get-tuple-element.32), channel_id=1, source_target_pairs={{0,4},{4,8},{8,12},{1,5},{5,9},{9,13},{2,6},{6,10},{10,14},{3,7},{... | collective-permute-start | bytes 884744 | tf_op jit(solution)/shard_map/ppermute | solution.py:48
  309.7 15.3 %collective-permute-start.22 = (f32[192,384]{1,0:T(8,128)S(1)}, f32[192,384]{1,0:T(8,128)S(1)}, u32[]{:S(2)}, u32[]{:S(2)}) collective-permute-start(f32[192,384]{1,0:T(8,128)S(1)} %get-tuple-element.32), channel_id=1, source_target_pairs={{4,0},{8,4},{12,8},{5,1},{9,5},{13,9},{6,2},{10,6},{14,10},{7,3},{... | collective-permute-start | bytes 884744 | tf_op jit(solution)/shard_map/ppermute | solution.py:49
  389.6 20.2 %collective-permute-start.30 = (f32[192,384]{1,0:T(8,128)S(1)}, f32[192,384]{1,0:T(8,128)S(1)}, u32[]{:S(2)}, u32[]{:S(2)}) collective-permute-start(f32[192,384]{1,0:T(8,128)S(1)} %get-tuple-element.28), channel_id=1, source_target_pairs={{0,12},{12,0},{1,13},{13,1},{2,14},{14,2},{3,15},{15,3},{16,28},{2... | collective-permute-start | bytes 884744 | tf_op jit(solution)/shard_map/ppermute | solution.py:43
  393.3 12.1 %collective-permute-start.31 = (f32[192,384]{1,0:T(8,128)S(1)}, f32[192,384]{1,0:T(8,128)S(1)}, u32[]{:S(2)}, u32[]{:S(2)}) collective-permute-start(f32[192,384]{1,0:T(8,128)S(1)} %get-tuple-element.28), channel_id=1, source_target_pairs={{0,4},{4,8},{8,12},{1,5},{5,9},{9,13},{2,6},{6,10},{10,14},{3,7},{... | collective-permute-start | bytes 884744 | tf_op jit(solution)/shard_map/ppermute | solution.py:48
  394.6 15.3 %collective-permute-start.32 = (f32[192,384]{1,0:T(8,128)S(1)}, f32[192,384]{1,0:T(8,128)S(1)}, u32[]{:S(2)}, u32[]{:S(2)}) collective-permute-start(f32[192,384]{1,0:T(8,128)S(1)} %get-tuple-element.28), channel_id=1, source_target_pairs={{4,0},{8,4},{12,8},{5,1},{9,5},{13,9},{6,2},{10,6},{14,10},{7,3},{... | collective-permute-start | bytes 884744 | tf_op jit(solution)/shard_map/ppermute | solution.py:49
  409.9 10.2 %collective-permute-start.34 = (f32[192,384]{1,0:T(8,128)S(1)}, f32[192,384]{1,0:T(8,128)S(1)}, u32[]{:S(2)}, u32[]{:S(2)}) collective-permute-start(f32[192,384]{1,0:T(8,128)S(1)} %collective-permute-done.32), channel_id=1, source_target_pairs={{4,0},{8,4},{12,8},{5,1},{9,5},{13,9},{6,2},{10,6},{14,10},{7,3},{... | collective-permute-start | bytes 884744 | tf_op jit(solution)/shard_map/ppermute | solution.py:49
  474.4 20.1 %collective-permute-start.40 = (f32[192,384]{1,0:T(8,128)S(1)}, f32[192,384]{1,0:T(8,128)S(1)}, u32[]{:S(2)}, u32[]{:S(2)}) collective-permute-start(f32[192,384]{1,0:T(8,128)S(1)} %get-tuple-element.24), channel_id=1, source_target_pairs={{0,12},{12,0},{1,13},{13,1},{2,14},{14,2},{3,15},{15,3},{16,28},{2... | collective-permute-start | bytes 884744 | tf_op jit(solution)/shard_map/ppermute | solution.py:43
  478.0 12.1 %collective-permute-start.41 = (f32[192,384]{1,0:T(8,128)S(1)}, f32[192,384]{1,0:T(8,128)S(1)}, u32[]{:S(2)}, u32[]{:S(2)}) collective-permute-start(f32[192,384]{1,0:T(8,128)S(1)} %get-tuple-element.24), channel_id=1, source_target_pairs={{0,4},{4,8},{8,12},{1,5},{5,9},{9,13},{2,6},{6,10},{10,14},{3,7},{... | collective-permute-start | bytes 884744 | tf_op jit(solution)/shard_map/ppermute | solution.py:48
  479.4 15.3 %collective-permute-start.42 = (f32[192,384]{1,0:T(8,128)S(1)}, f32[192,384]{1,0:T(8,128)S(1)}, u32[]{:S(2)}, u32[]{:S(2)}) collective-permute-start(f32[192,384]{1,0:T(8,128)S(1)} %get-tuple-element.24), channel_id=1, source_target_pairs={{4,0},{8,4},{12,8},{5,1},{9,5},{13,9},{6,2},{10,6},{14,10},{7,3},{... | collective-permute-start | bytes 884744 | tf_op jit(solution)/shard_map/ppermute | solution.py:49
  494.7 10.2 %collective-permute-start.44 = (f32[192,384]{1,0:T(8,128)S(1)}, f32[192,384]{1,0:T(8,128)S(1)}, u32[]{:S(2)}, u32[]{:S(2)}) collective-permute-start(f32[192,384]{1,0:T(8,128)S(1)} %collective-permute-done.42), channel_id=1, source_target_pairs={{4,0},{8,4},{12,8},{5,1},{9,5},{13,9},{6,2},{10,6},{14,10},{7,3},{... | collective-permute-start | bytes 884744 | tf_op jit(solution)/shard_map/ppermute | solution.py:49
  (52 other events, 594.8 us)
Sparse Core Ops, SparseCore 0:
  8.9 66.1 all-gather.4
  76.7 75.0 all-gather.6

commit v13 on v12

--- a/solution.py
+++ b/solution.py
@@ -110,7 +110,7 @@
 
     left_w = jnp.dot(grads, site_weights[0], preferred_element_type=f32)
     mixed_w = mixed_of(left_w, token_pair(left_w))
-    mixed_w_all = site_gather(mixed_w)
+    mixed_w_all = line_gather(mixed_w) if sites <= 4 else site_gather(mixed_w)
     if split:
         half = count // 2
         turned = jnp.concatenate([mixed_w_all[:, half:], mixed_w_all[:, :half]], axis=1)

time: 548 us -> 568 us (1.036)
  waiting for transfers between devices: 254 us -> 213 us
  starting transfers between devices: 86.9 us -> 123 us
  other arithmetic: 37.4 us -> 52.3 us
  matrix products: 125 us -> 137 us
    all_gather x2 -> x1, waiting for transfers between devices: 115 us -> 0.01 us  [site_gather(): lax.all_gather(lax.optimization_barrier(x), 'site')]
    ppermute x10 -> x12, waiting for transfers between devices: 67.3 us -> 100 us  [line_gather(): right = lax.ppermute(right, 'site', [(i, i + 1) for i in range(sites - 1)])]
    ppermute x5 -> x6, waiting for transfers between devices: 0.01 us -> 32 us  [line_gather(): far = lax.ppermute(x, 'site', [(0, 3), (3, 0)])]
    ppermute x10 -> x12, starting transfers between devices: 28.6 us -> 57.5 us  [line_gather(): right = lax.ppermute(right, 'site', [(i, i + 1) for i in range(sites - 1)])]
    dot_general x39, matrix products: 95.3 us -> 108 us  [one(): return jnp.einsum(spec, exact, part, preferred_element_type=f32)]
    dynamic_update_slice x20 -> x24, other arithmetic: 1.39 us -> 12.2 us  [line_gather(): out = lax.dynamic_update_slice_in_dim(out, now + block[None], at, 0)]
    ppermute x4, waiting for transfers between devices: 23.3 us -> 30.5 us  [pair_sum(): lax.ppermute(part, 'inner', [(i, i ^ bit) for i in range(inner)])]
    ppermute x5 -> x6, starting transfers between devices: 19.9 us -> 24.9 us  [line_gather(): far = lax.ppermute(x, 'site', [(0, 3), (3, 0)])]
  transfers between devices with their start and end apart: 50 -> 54, of which waited for: 32 -> 37; matrix products, arithmetic and copies ran while one was open for 12% -> 17% of each run, Pallas kernels for 0% -> 0%
where the time goes in v13:
time: 568 us; the launch traced here: 567 us
  waiting for transfers between devices  213 us (38%)
  matrix products  137 us (24%)
  starting transfers between devices  123 us (22%)
  other arithmetic  52.3 us (9%)
  between operations  29.6 us (5%)
  local copies, waits for them, and re-layouts  12.2 us (2%)
    dot_general x39, matrix products, one(): return jnp.einsum(spec, exact, part, preferred_element_type=f32)  108 us
    ppermute x12, waiting for transfers between devices, line_gather(): right = lax.ppermute(right, 'site', [(i, i + 1) for i in range(sites - 1)])  100 us
    ppermute x12, starting transfers between devices, line_gather(): right = lax.ppermute(right, 'site', [(i, i + 1) for i in range(sites - 1)])  57.5 us
    ppermute x6, waiting for transfers between devices, line_gather(): far = lax.ppermute(x, 'site', [(0, 3), (3, 0)])  32 us
    ppermute x4, waiting for transfers between devices, pair_sum(): lax.ppermute(part, 'inner', [(i, i ^ bit) for i in range(inner)])  30.5 us
    dot_general x30, matrix products, one(): return jnp.einsum(spec, part, exact, preferred_element_type=f32)  27.8 us
    ppermute x6, starting transfers between devices, line_gather(): far = lax.ppermute(x, 'site', [(0, 3), (3, 0)])  24.9 us
    ppermute x12, waiting for transfers between devices, line_gather(): left = lax.ppermute(left, 'site', [(i + 1, i) for i in range(sites - 1)])  22 us
  transfers between devices with their start and end apart: 54, of which 37 were waited for; matrix products, arithmetic and copies ran while one was open for 17% of the time, Pallas kernels for 0%

profile of v13, /device:TPU:0, one launch (start us, length us, event | category | flops | bytes accessed | tf_op | source)
XLA Modules:
  0.0 567.5 jit_solution(17372224883388489943)
XLA Ops:
  17.2 13.6 %collective-permute-done.2 = f32[384,384]{1,0:T(8,128)S(1)} collective-permute-done((f32[384,384]{1,0:T(8,128)S(1)}, f32[384,384]{1,0:T(8,128)S(1)}, u32[]{:S(2)}, u32[]{:S(2)}) %collective-permute-start.2) | collective-permute-done | bytes 589856 | tf_op jit(solution)/shard_map/ppermute | solution.py:61
  40.7 6.6 %collective-permute-start.3 = (f32[384,640]{1,0:T(8,128)}, f32[384,640]{1,0:T(8,128)}, u32[]{:S(2)}, u32[]{:S(2)}) collective-permute-start(f32[384,640]{1,0:T(8,128)} %get-tuple-element.46), channel_id=1, source_target_pairs={{0,12},{12,0},{1,13},{13,1},{2,14},{14,2},{3,15},{15,3},{16,28},{2... | collective-permute-start | bytes 2949128 | tf_op jit(solution)/shard_map/ppermute | solution.py:43
  47.4 35.4 %collective-permute-done.4 = f32[384,640]{1,0:T(8,128)S(1)} collective-permute-done((f32[384,640]{1,0:T(8,128)}, f32[384,640]{1,0:T(8,128)S(1)}, u32[]{:S(2)}, u32[]{:S(2)}) %collective-permute-start.4) | collective-permute-done | bytes 983072 | tf_op jit(solution)/shard_map/ppermute | solution.py:48
  82.8 22.9 %collective-permute-start.6 = (f32[384,640]{1,0:T(8,128)S(1)}, f32[384,640]{1,0:T(8,128)S(1)}, u32[]{:S(2)}, u32[]{:S(2)}) collective-permute-start(f32[384,640]{1,0:T(8,128)S(1)} %collective-permute-done.4), channel_id=1, source_target_pairs={{0,4},{4,8},{8,12},{1,5},{5,9},{9,13},{2,6},{6,10},{10,14},{3,7},{... | collective-permute-start | bytes 2949128 | tf_op jit(solution)/shard_map/ppermute | solution.py:48
  107.1 10.7 %collective-permute-done.3 = f32[384,640]{1,0:T(8,128)} collective-permute-done((f32[384,640]{1,0:T(8,128)}, f32[384,640]{1,0:T(8,128)}, u32[]{:S(2)}, u32[]{:S(2)}) %collective-permute-start.3) | collective-permute-done | bytes 983072 | tf_op jit(solution)/shard_map/ppermute | solution.py:43
  124.9 9.2 %collective-permute-done.6 = f32[384,640]{1,0:T(8,128)S(1)} collective-permute-done((f32[384,640]{1,0:T(8,128)S(1)}, f32[384,640]{1,0:T(8,128)S(1)}, u32[]{:S(2)}, u32[]{:S(2)}) %collective-permute-start.6) | collective-permute-done | bytes 983072 | tf_op jit(solution)/shard_map/ppermute | solution.py:48
  152.5 5.6 collective-permute-start.16
  158.4 14.0 %collective-permute-done.17 = f32[384,640]{1,0:T(8,128)} collective-permute-done((f32[384,640]{1,0:T(8,128)S(1)}, f32[384,640]{1,0:T(8,128)}, u32[]{:S(2)}, u32[]{:S(2)}) %collective-permute-start.17) | collective-permute-done | bytes 983072 | tf_op jit(solution)/shard_map/ppermute | solution.py:48
  178.6 21.3 %collective-permute-done.16 = f32[384,640]{1,0:T(8,128)S(1)} collective-permute-done((f32[384,640]{1,0:T(8,128)S(1)}, f32[384,640]{1,0:T(8,128)S(1)}, u32[]{:S(2)}, u32[]{:S(2)}) %collective-permute-start.16) | collective-permute-done | bytes 983072 | tf_op jit(solution)/shard_map/ppermute | solution.py:43
  217.4 13.4 %fusion.58 = f32[384,640]{0,1:T(8,128)S(1)} fusion(f32[640,384]{1,0:T(8,128)S(1)} %fusion.142, f32[640,384]{1,0:T(8,128)S(1)} %fusion.140, bf16[1,384,1024]{2,1,0:T(8,128)(2,1)S(1)} %copy-done.7, f32[1024,640]{1,0:T(8,128)S(1)} %get-tuple-element.48), kind=kOutput, calls=%fused_computation.168 | convolution fusion | flops 507084800 | bytes 6356992 | tf_op jit(solution)/shard_map/td,dc->tc/dot_general | solution.py:26
  237.5 7.3 %collective-permute-done.9 = f32[200,384]{1,0:T(8,128)S(1)} collective-permute-done((f32[200,384]{1,0:T(8,128)S(1)}, f32[200,384]{1,0:T(8,128)S(1)}, u32[]{:S(2)}, u32[]{:S(2)}) %collective-permute-start.9) | collective-permute-done | bytes 307232 | tf_op jit(solution)/shard_map/ppermute | solution.py:137
  252.4 6.9 %collective-permute-done.11 = f32[192,384]{1,0:T(8,128)S(1)} collective-permute-done((f32[192,384]{1,0:T(8,128)S(1)}, f32[192,384]{1,0:T(8,128)S(1)}, u32[]{:S(2)}, u32[]{:S(2)}) %collective-permute-start.11) | collective-permute-done | bytes 294944 | tf_op jit(solution)/shard_map/ppermute | solution.py:48
  268.8 5.2 collective-permute-done.14
  290.6 5.0 multiply_reduce_fusion.5
  316.2 7.7 %collective-permute-done.24 = f32[200,384]{1,0:T(8,128)S(1)} collective-permute-done((f32[200,384]{1,0:T(8,128)S(1)}, f32[200,384]{1,0:T(8,128)S(1)}, u32[]{:S(2)}, u32[]{:S(2)}) %collective-permute-start.24) | collective-permute-done | bytes 307232 | tf_op jit(solution)/shard_map/ppermute | solution.py:137
  338.7 6.7 %collective-permute-done.26 = f32[192,384]{1,0:T(8,128)S(1)} collective-permute-done((f32[192,384]{1,0:T(8,128)S(1)}, f32[192,384]{1,0:T(8,128)S(1)}, u32[]{:S(2)}, u32[]{:S(2)}) %collective-permute-start.26) | collective-permute-done | bytes 294944 | tf_op jit(solution)/shard_map/ppermute | solution.py:48
  355.2 5.0 collective-permute-done.29
  376.3 5.1 multiply_reduce_fusion.3
  402.1 7.7 %collective-permute-done.34 = f32[200,384]{1,0:T(8,128)S(1)} collective-permute-done((f32[200,384]{1,0:T(8,128)S(1)}, f32[200,384]{1,0:T(8,128)S(1)}, u32[]{:S(2)}, u32[]{:S(2)}) %collective-permute-start.34) | collective-permute-done | bytes 307232 | tf_op jit(solution)/shard_map/ppermute | solution.py:137
  424.0 6.7 %collective-permute-done.36 = f32[192,384]{1,0:T(8,128)S(1)} collective-permute-done((f32[192,384]{1,0:T(8,128)S(1)}, f32[192,384]{1,0:T(8,128)S(1)}, u32[]{:S(2)}, u32[]{:S(2)}) %collective-permute-start.36) | collective-permute-done | bytes 294944 | tf_op jit(solution)/shard_map/ppermute | solution.py:48
  440.5 5.0 collective-permute-done.39
  461.5 5.0 multiply_reduce_fusion.1
  486.9 7.7 %collective-permute-done.44 = f32[200,384]{1,0:T(8,128)S(1)} collective-permute-done((f32[200,384]{1,0:T(8,128)S(1)}, f32[200,384]{1,0:T(8,128)S(1)}, u32[]{:S(2)}, u32[]{:S(2)}) %collective-permute-start.44) | collective-permute-done | bytes 307232 | tf_op jit(solution)/shard_map/ppermute | solution.py:137
  508.7 6.8 %collective-permute-done.46 = f32[192,384]{1,0:T(8,128)S(1)} collective-permute-done((f32[192,384]{1,0:T(8,128)S(1)}, f32[192,384]{1,0:T(8,128)S(1)}, u32[]{:S(2)}, u32[]{:S(2)}) %collective-permute-start.46) | collective-permute-done | bytes 294944 | tf_op jit(solution)/shard_map/ppermute | solution.py:48
  (290 shorter events, 297.4 us)
Async XLA Ops:
  6.5 129.8 %all-gather.3.cloned.1.call-start = ((), (), s32[]{:S(2)}) async-start(), calls=%async_computation | async-start | bytes 3932160 | tf_op jit(solution)/shard_map/all_gather | solution.py:33
  14.3 16.6 %collective-permute-start.2 = (f32[384,384]{1,0:T(8,128)S(1)}, f32[384,384]{1,0:T(8,128)S(1)}, u32[]{:S(2)}, u32[]{:S(2)}) collective-permute-start(f32[384,384]{1,0:T(8,128)S(1)} %add.511), channel_id=1, source_target_pairs={{0,2},{1,3},{2,0},{3,1},{4,6},{5,7},{6,4},{7,5},{8,10},{9,11},{10,... | collective-permute-start | bytes 1769480 | tf_op jit(solution)/shard_map/ppermute | solution.py:61
  35.7 47.2 %collective-permute-start.4 = (f32[384,640]{1,0:T(8,128)}, f32[384,640]{1,0:T(8,128)S(1)}, u32[]{:S(2)}, u32[]{:S(2)}) collective-permute-start(f32[384,640]{1,0:T(8,128)} %get-tuple-element.46), channel_id=1, source_target_pairs={{0,4},{4,8},{8,12},{1,5},{5,9},{9,13},{2,6},{6,10},{10,14},{3,7},{... | collective-permute-start | bytes 2949128 | tf_op jit(solution)/shard_map/ppermute | solution.py:48
  39.4 66.4 %collective-permute-start.5 = (f32[384,640]{1,0:T(8,128)}, f32[384,640]{1,0:T(8,128)S(1)}, u32[]{:S(2)}, u32[]{:S(2)}) collective-permute-start(f32[384,640]{1,0:T(8,128)} %get-tuple-element.46), channel_id=1, source_target_pairs={{4,0},{8,4},{12,8},{5,1},{9,5},{13,9},{6,2},{10,6},{14,10},{7,3},{... | collective-permute-start | bytes 2949128 | tf_op jit(solution)/shard_map/ppermute | solution.py:49
  40.7 77.1 %collective-permute-start.3 = (f32[384,640]{1,0:T(8,128)}, f32[384,640]{1,0:T(8,128)}, u32[]{:S(2)}, u32[]{:S(2)}) collective-permute-start(f32[384,640]{1,0:T(8,128)} %get-tuple-element.46), channel_id=1, source_target_pairs={{0,12},{12,0},{1,13},{13,1},{2,14},{14,2},{3,15},{15,3},{16,28},{2... | collective-permute-start | bytes 2949128 | tf_op jit(solution)/shard_map/ppermute | solution.py:43
  82.8 51.3 %collective-permute-start.6 = (f32[384,640]{1,0:T(8,128)S(1)}, f32[384,640]{1,0:T(8,128)S(1)}, u32[]{:S(2)}, u32[]{:S(2)}) collective-permute-start(f32[384,640]{1,0:T(8,128)S(1)} %collective-permute-done.4), channel_id=1, source_target_pairs={{0,4},{4,8},{8,12},{1,5},{5,9},{9,13},{2,6},{6,10},{10,14},{3,7},{... | collective-permute-start | bytes 2949128 | tf_op jit(solution)/shard_map/ppermute | solution.py:48
  105.8 32.5 %collective-permute-start.7 = (f32[384,640]{1,0:T(8,128)S(1)}, f32[384,640]{1,0:T(8,128)}, u32[]{:S(2)}, u32[]{:S(2)}) collective-permute-start(f32[384,640]{1,0:T(8,128)S(1)} %collective-permute-done.5), channel_id=1, source_target_pairs={{4,0},{8,4},{12,8},{5,1},{9,5},{13,9},{6,2},{10,6},{14,10},{7,3},{... | collective-permute-start | bytes 2949128 | tf_op jit(solution)/shard_map/ppermute | solution.py:49
  136.4 66.3 %collective-permute-start = (f32[4,192,1024]{2,1,0:T(8,128)}, f32[4,192,1024]{2,1,0:T(8,128)}, u32[]{:S(2)}, u32[]{:S(2)}) collective-permute-start(f32[4,192,1024]{2,1,0:T(8,128)} %bitcast.309), channel_id=1, source_target_pairs={{0,1},{1,0},{2,3},{3,2},{4,5},{5,4},{6,7},{7,6},{8,9},{9,8},{10,11... | collective-permute-start | bytes 9437192 | tf_op jit(solution)/shard_map/ppermute | solution.py:67
  147.7 24.6 %collective-permute-start.17 = (f32[384,640]{1,0:T(8,128)S(1)}, f32[384,640]{1,0:T(8,128)}, u32[]{:S(2)}, u32[]{:S(2)}) collective-permute-start(f32[384,640]{1,0:T(8,128)S(1)} %convert_multiply_fusion), channel_id=1, source_target_pairs={{0,4},{4,8},{8,12},{1,5},{5,9},{9,13},{2,6},{6,10},{10,14},{3,7},{... | collective-permute-start | bytes 2949128 | tf_op jit(solution)/shard_map/ppermute | solution.py:48
  151.2 25.8 %collective-permute-start.18 = (f32[384,640]{1,0:T(8,128)S(1)}, f32[384,640]{1,0:T(8,128)S(1)}, u32[]{:S(2)}, u32[]{:S(2)}) collective-permute-start(f32[384,640]{1,0:T(8,128)S(1)} %convert_multiply_fusion), channel_id=1, source_target_pairs={{4,0},{8,4},{12,8},{5,1},{9,5},{13,9},{6,2},{10,6},{14,10},{7,3},{... | collective-permute-start | bytes 2949128 | tf_op jit(solution)/shard_map/ppermute | solution.py:49
  152.5 47.4 %collective-permute-start.16 = (f32[384,640]{1,0:T(8,128)S(1)}, f32[384,640]{1,0:T(8,128)S(1)}, u32[]{:S(2)}, u32[]{:S(2)}) collective-permute-start(f32[384,640]{1,0:T(8,128)S(1)} %convert_multiply_fusion), channel_id=1, source_target_pairs={{0,12},{12,0},{1,13},{13,1},{2,14},{14,2},{3,15},{15,3},{16,28},{2... | collective-permute-start | bytes 2949128 | tf_op jit(solution)/shard_map/ppermute | solution.py:43
  172.4 60.8 %collective-permute-start.19 = (f32[384,640]{1,0:T(8,128)}, f32[384,640]{1,0:T(8,128)S(1)}, u32[]{:S(2)}, u32[]{:S(2)}) collective-permute-start(f32[384,640]{1,0:T(8,128)} %collective-permute-done.17), channel_id=1, source_target_pairs={{0,4},{4,8},{8,12},{1,5},{5,9},{9,13},{2,6},{6,10},{10,14},{3,7},{... | collective-permute-start | bytes 2949128 | tf_op jit(solution)/shard_map/ppermute | solution.py:48
  177.0 56.4 %collective-permute-start.20 = (f32[384,640]{1,0:T(8,128)S(1)}, f32[384,640]{1,0:T(8,128)S(1)}, u32[]{:S(2)}, u32[]{:S(2)}) collective-permute-start(f32[384,640]{1,0:T(8,128)S(1)} %collective-permute-done.18), channel_id=1, source_target_pairs={{4,0},{8,4},{12,8},{5,1},{9,5},{13,9},{6,2},{10,6},{14,10},{7,3},{... | collective-permute-start | bytes 2949128 | tf_op jit(solution)/shard_map/ppermute | solution.py:49
  245.0 18.7 %collective-permute-start.10 = (f32[192,384]{1,0:T(8,128)S(1)}, f32[192,384]{1,0:T(8,128)S(1)}, u32[]{:S(2)}, u32[]{:S(2)}) collective-permute-start(f32[192,384]{1,0:T(8,128)S(1)} %slice.43), channel_id=1, source_target_pairs={{0,12},{12,0},{1,13},{13,1},{2,14},{14,2},{3,15},{15,3},{16,28},{2... | collective-permute-start | bytes 884744 | tf_op jit(solution)/shard_map/ppermute | solution.py:43
  246.9 12.4 %collective-permute-start.11 = (f32[192,384]{1,0:T(8,128)S(1)}, f32[192,384]{1,0:T(8,128)S(1)}, u32[]{:S(2)}, u32[]{:S(2)}) collective-permute-start(f32[192,384]{1,0:T(8,128)S(1)} %slice.43), channel_id=1, source_target_pairs={{0,4},{4,8},{8,12},{1,5},{5,9},{9,13},{2,6},{6,10},{10,14},{3,7},{... | collective-permute-start | bytes 884744 | tf_op jit(solution)/shard_map/ppermute | solution.py:48
  250.9 12.8 %collective-permute-start.12 = (f32[192,384]{1,0:T(8,128)S(1)}, f32[192,384]{1,0:T(8,128)S(1)}, u32[]{:S(2)}, u32[]{:S(2)}) collective-permute-start(f32[192,384]{1,0:T(8,128)S(1)} %slice.43), channel_id=1, source_target_pairs={{4,0},{8,4},{12,8},{5,1},{9,5},{13,9},{6,2},{10,6},{14,10},{7,3},{... | collective-permute-start | bytes 884744 | tf_op jit(solution)/shard_map/ppermute | solution.py:49
  329.7 20.2 %collective-permute-start.25 = (f32[192,384]{1,0:T(8,128)S(1)}, f32[192,384]{1,0:T(8,128)S(1)}, u32[]{:S(2)}, u32[]{:S(2)}) collective-permute-start(f32[192,384]{1,0:T(8,128)S(1)} %get-tuple-element.32), channel_id=1, source_target_pairs={{0,12},{12,0},{1,13},{13,1},{2,14},{14,2},{3,15},{15,3},{16,28},{2... | collective-permute-start | bytes 884744 | tf_op jit(solution)/shard_map/ppermute | solution.py:43
  333.3 12.1 %collective-permute-start.26 = (f32[192,384]{1,0:T(8,128)S(1)}, f32[192,384]{1,0:T(8,128)S(1)}, u32[]{:S(2)}, u32[]{:S(2)}) collective-permute-start(f32[192,384]{1,0:T(8,128)S(1)} %get-tuple-element.32), channel_id=1, source_target_pairs={{0,4},{4,8},{8,12},{1,5},{5,9},{9,13},{2,6},{6,10},{10,14},{3,7},{... | collective-permute-start | bytes 884744 | tf_op jit(solution)/shard_map/ppermute | solution.py:48
  334.7 15.3 %collective-permute-start.27 = (f32[192,384]{1,0:T(8,128)S(1)}, f32[192,384]{1,0:T(8,128)S(1)}, u32[]{:S(2)}, u32[]{:S(2)}) collective-permute-start(f32[192,384]{1,0:T(8,128)S(1)} %get-tuple-element.32), channel_id=1, source_target_pairs={{4,0},{8,4},{12,8},{5,1},{9,5},{13,9},{6,2},{10,6},{14,10},{7,3},{... | collective-permute-start | bytes 884744 | tf_op jit(solution)/shard_map/ppermute | solution.py:49
  415.0 20.1 %collective-permute-start.35 = (f32[192,384]{1,0:T(8,128)S(1)}, f32[192,384]{1,0:T(8,128)S(1)}, u32[]{:S(2)}, u32[]{:S(2)}) collective-permute-start(f32[192,384]{1,0:T(8,128)S(1)} %get-tuple-element.28), channel_id=1, source_target_pairs={{0,12},{12,0},{1,13},{13,1},{2,14},{14,2},{3,15},{15,3},{16,28},{2... | collective-permute-start | bytes 884744 | tf_op jit(solution)/shard_map/ppermute | solution.py:43
  418.6 12.1 %collective-permute-start.36 = (f32[192,384]{1,0:T(8,128)S(1)}, f32[192,384]{1,0:T(8,128)S(1)}, u32[]{:S(2)}, u32[]{:S(2)}) collective-permute-start(f32[192,384]{1,0:T(8,128)S(1)} %get-tuple-element.28), channel_id=1, source_target_pairs={{0,4},{4,8},{8,12},{1,5},{5,9},{9,13},{2,6},{6,10},{10,14},{3,7},{... | collective-permute-start | bytes 884744 | tf_op jit(solution)/shard_map/ppermute | solution.py:48
  419.9 15.3 %collective-permute-start.37 = (f32[192,384]{1,0:T(8,128)S(1)}, f32[192,384]{1,0:T(8,128)S(1)}, u32[]{:S(2)}, u32[]{:S(2)}) collective-permute-start(f32[192,384]{1,0:T(8,128)S(1)} %get-tuple-element.28), channel_id=1, source_target_pairs={{4,0},{8,4},{12,8},{5,1},{9,5},{13,9},{6,2},{10,6},{14,10},{7,3},{... | collective-permute-start | bytes 884744 | tf_op jit(solution)/shard_map/ppermute | solution.py:49
  499.7 20.1 %collective-permute-start.45 = (f32[192,384]{1,0:T(8,128)S(1)}, f32[192,384]{1,0:T(8,128)S(1)}, u32[]{:S(2)}, u32[]{:S(2)}) collective-permute-start(f32[192,384]{1,0:T(8,128)S(1)} %get-tuple-element.24), channel_id=1, source_target_pairs={{0,12},{12,0},{1,13},{13,1},{2,14},{14,2},{3,15},{15,3},{16,28},{2... | collective-permute-start | bytes 884744 | tf_op jit(solution)/shard_map/ppermute | solution.py:43
  504.6 15.3 %collective-permute-start.47 = (f32[192,384]{1,0:T(8,128)S(1)}, f32[192,384]{1,0:T(8,128)S(1)}, u32[]{:S(2)}, u32[]{:S(2)}) collective-permute-start(f32[192,384]{1,0:T(8,128)S(1)} %get-tuple-element.24), channel_id=1, source_target_pairs={{4,0},{8,4},{12,8},{5,1},{9,5},{13,9},{6,2},{10,6},{14,10},{7,3},{... | collective-permute-start | bytes 884744 | tf_op jit(solution)/shard_map/ppermute | solution.py:49
  (57 other events, 692.2 us)
Sparse Core Ops, SparseCore 0:
  8.9 93.5 all-gather.2
